TPU v7x, 256 devices: a whole 4x4x8 slice. The times are simulated.
256 devices in a mesh: date: 64 (over x, y, z_lo, core), rng: 4 (over z_hi).
Axes of the slice: x: 4, y: 4, z: 8 (z_hi: 4, z_lo: 2; z = z_hi * 2 + z_lo), core: 2. Of those that a mesh axis runs over, the one named last changes fastest.
Arguments:
- slc_re: bfloat16 [64, 2048, 512], P('date', None, 'rng'), may hold values from -170 to 170
- slc_im: bfloat16 [64, 2048, 512], P('date', None, 'rng'), may hold values from -170 to 170
- ref_date: int32 [1], replicated, may hold values from 0 to 63
- gain: float32 [2048], replicated, may hold values from 0.25 to 2
- bperp: int32 [64], replicated, may hold values from -200 to 199
- tdays: int32 [64], replicated, may hold values from 0 to 1899
- mask: int32 [2048, 512], P(None, 'rng'), may hold values from 0 to 1, as said below
Outputs:
- periodogram: float32 [2048, 512, 256], P('date', 'rng')
Inputs may be any that keep to these rules, and one draw needn't show every extreme that they name: `mask`: each aligned block of 32 lines by 128 range columns holds exactly 1024 candidates.
All inputs are finite; a program needn't handle non-finite values.
Results may differ from a plain program's by a relative error of at most 0.0067.
Values may be sent and summed in bfloat16 or wider, within the bound.
No kernel may reach another device: no remote copies, remote signals or barrier semaphores. Data moves between devices by JAX's collectives and lax.ppermute only.
A program may use at most 64 MiB of HBM per device.

v0:
```python
import math

import jax
import jax.numpy as jnp
from jax import lax
from jax.sharding import PartitionSpec as P

HGRID = 16
VGRID = 16
PHASE_Q = 1024


def broadcast(shard, axis, root):
    mine = lax.axis_index(axis) == root
    return lax.psum(jnp.where(mine, shard, jnp.zeros_like(shard)), axis)


def dft_tables(length):
    positions = jnp.arange(length, dtype=jnp.int32)
    products = positions[:, None] * positions[None, :] % length
    angles = products.astype(jnp.float32) * (2.0 * math.pi / length)
    return (jnp.cos(angles).astype(jnp.bfloat16), jnp.sin(angles).astype(jnp.bfloat16))


def phase_tables(bperp, tdays):
    grid_points = jnp.arange(HGRID * VGRID, dtype=jnp.int32)
    height_step = grid_points // VGRID
    speed_step = grid_points % VGRID
    quanta = (
        bperp[:, None] * height_step[None, :] + tdays[:, None] * speed_step[None, :]
    ) % PHASE_Q
    angles = quanta.astype(jnp.float32) * (2.0 * math.pi / PHASE_Q)
    phase_re = jnp.cos(angles).astype(jnp.bfloat16)
    phase_im = jnp.sin(angles).astype(jnp.bfloat16)
    upper = jnp.concatenate([phase_re, -phase_im], axis=1)
    lower = jnp.concatenate([phase_im, phase_re], axis=1)
    return jnp.concatenate([upper, lower], axis=0)


def coherence_map(piece_re, piece_im, phase_table):
    date_count = piece_re.shape[0]
    grid_size = phase_table.shape[1] // 2
    stacked = jnp.concatenate([piece_re, piece_im], axis=0)
    spectra = lax.dot_general(
        stacked, phase_table, (((0,), (0,)), ((), ())), preferred_element_type=jnp.float32
    )
    peri_re = spectra[:, :grid_size]
    peri_im = spectra[:, grid_size:]
    wide_re = piece_re.astype(jnp.float32)
    wide_im = piece_im.astype(jnp.float32)
    pixel_power = jnp.sum(wide_re * wide_re + wide_im * wide_im, axis=0) / date_count
    return (peri_re * peri_re + peri_im * peri_im) / (date_count * jnp.maximum(pixel_power, 1.0))[
        :, None
    ]


def shards(slc_re, slc_im, ref_date, gain, bperp, tdays, mask):
    date_dev, lines, rg_dev = slc_re.shape
    date_axis = lax.axis_size("date")
    pixel_total = lines * rg_dev * lax.axis_size("rng")
    ref_index = ref_date[0]
    owner_index = ref_index // date_dev
    owner_slot = ref_index % date_dev
    own_re = lax.dynamic_index_in_dim(slc_re, owner_slot, 0, keepdims=False)
    own_im = lax.dynamic_index_in_dim(slc_im, owner_slot, 0, keepdims=False)
    ref_re, ref_im = (
        broadcast(own_re, "date", owner_index),
        broadcast(own_im, "date", owner_index),
    )
    wide_re = slc_re.astype(jnp.float32)
    wide_im = slc_im.astype(jnp.float32)
    ref_wide_re = ref_re.astype(jnp.float32)
    ref_wide_im = ref_im.astype(jnp.float32)
    local_sums = jnp.sum(wide_re * wide_re + wide_im * wide_im, axis=(1, 2))
    ref_local = jnp.sum(ref_wide_re * ref_wide_re + ref_wide_im * ref_wide_im)
    date_sums, ref_sum = lax.psum((local_sums, ref_local), "rng")
    scales = lax.rsqrt(date_sums / pixel_total + 1e-06)
    ref_scale = lax.rsqrt(ref_sum / pixel_total + 1e-06)
    own_part_re = wide_re * scales[:, None, None]
    own_part_im = wide_im * scales[:, None, None]
    ref_part_re = (ref_wide_re * ref_scale)[None]
    ref_part_im = (ref_wide_im * ref_scale)[None]
    ifg_re = (own_part_re * ref_part_re + own_part_im * ref_part_im).astype(jnp.bfloat16)
    ifg_im = (own_part_im * ref_part_re - own_part_re * ref_part_im).astype(jnp.bfloat16)
    cos_table, sin_table = dft_tables(lines)
    pair = jnp.stack([ifg_re, ifg_im])
    cos_part = jnp.einsum("fl,kdlc->kdfc", cos_table, pair, preferred_element_type=jnp.float32)
    sin_part = jnp.einsum("fl,kdlc->kdfc", sin_table, pair, preferred_element_type=jnp.float32)
    spec_re = cos_part[0] + sin_part[1]
    spec_im = cos_part[1] - sin_part[0]
    weights = gain[:, None]
    held = jnp.stack(
        [(spec_re * weights).astype(jnp.bfloat16), (spec_im * weights).astype(jnp.bfloat16)]
    )
    back_cos = jnp.einsum("fl,kdfc->kdlc", cos_table, held, preferred_element_type=jnp.float32)
    back_sin = jnp.einsum("fl,kdfc->kdlc", sin_table, held, preferred_element_type=jnp.float32)
    filt_re = ((back_cos[0] - back_sin[1]) * (1.0 / lines)).astype(jnp.bfloat16)
    filt_im = ((back_sin[0] + back_cos[1]) * (1.0 / lines)).astype(jnp.bfloat16)
    phase_table = phase_tables(bperp, tdays)
    grid_size = HGRID * VGRID
    lines_dev = lines // date_axis
    my_index = lax.axis_index("date")
    piece_re = lax.all_to_all(filt_re, "date", split_axis=1, concat_axis=0, tiled=True)
    piece_im = lax.all_to_all(filt_im, "date", split_axis=1, concat_axis=0, tiled=True)
    row_count = piece_re.shape[1]
    col_count = piece_re.shape[2]
    flat_re = piece_re.reshape(piece_re.shape[0], row_count * col_count)
    flat_im = piece_im.reshape(piece_im.shape[0], row_count * col_count)
    result = coherence_map(flat_re, flat_im, phase_table)
    mapped = result.reshape(row_count, col_count, grid_size)
    mask_rows = lax.dynamic_slice_in_dim(mask, my_index * lines_dev, lines_dev, 0)
    return mapped * mask_rows.astype(jnp.float32)[:, :, None]


def solution(mesh):
    in_specs = (P("date", None, "rng"), P("date", None, "rng"), P(), P(), P(), P(), P(None, "rng"))
    out_specs = P("date", "rng", None)
    return jax.shard_map(shards, mesh=mesh, in_specs=in_specs, out_specs=out_specs, check_vma=False)
```

profile of v0, /device:TPU:1, one launch (start us, length us, event | category | flops | bytes accessed | tf_op | source)
XLA Modules:
  0.0 924.3 jit_solution(13972574443800671142)
XLA Ops:
  6.5 1.2 copy.20
  7.8 1.2 copy.21
  9.7 1.1 select_bitcast_fusion
  10.8 0.9 fusion.39
  11.7 561.3 %all-reduce.4.cloned.1.call-done = (bf16[2048,128]{0,1:T(8,128)(2,1)}, bf16[2048,128]{0,1:T(8,128)(2,1)}) async-done(((bf16[2048,128]{0,1:T(8,128)(2,1)}, bf16[2048,128]{0,1:T(8,128)(2,1)}), (bf16[2048,128]{0,1:T(8,128)(2,1)}, bf16[2048,128]{0,1:T(8,128)(2,1)})) %all-reduce.4.cloned.1.call-update) | async-done | bytes 1048592 | tf_op jit(solution)/shard_map/psum | solution.py:15
  572.9 2.1 fusion.41
  575.0 10.5 %all-reduce = (f32[]{:T(128)}, f32[1]{0:T(128)}) all-reduce(f32[]{:T(128)} %fusion.41, f32[1]{0:T(128)} %bitcast), channel_id=1, replica_groups=mesh['date'=64,'rng'=4] {'rng'}, use_global_device_ids=true, to_apply=%region_5.6 | all-reduce | flops 2 | bytes 16 | tf_op jit(solution)/shard_map/psum | solution.py:76
  587.0 1.7 fusion.59
  588.9 63.5 %fusion.18 = f32[2,1,2048,128]{2,3,0,1:T(8,128)S(1)} fusion(bf16[2,2048,128]{1,2,0:T(8,128)(2,1)S(1)} %maximum_bitcast_fusion.18), kind=kOutput, calls=%fused_computation.21 | convolution fusion | flops 2210398208 | bytes 3145728 | tf_op jit(solution)/shard_map/fl,kdlc->kdfc/dot_general | solution.py:87
  652.4 64.0 %fusion.24 = f32[2,1,2048,128]{2,3,0,1:T(8,128)S(1)} fusion(bf16[2,2048,128]{1,2,0:T(8,128)(2,1)S(1)} %maximum_bitcast_fusion.20), kind=kOutput, calls=%fused_computation.23 | convolution fusion | flops 2210398208 | bytes 3145728 | tf_op jit(solution)/shard_map/fl,kdlc->kdfc/dot_general | solution.py:88
  716.4 0.4 fusion.51
  717.0 63.2 %fusion.21 = f32[2,1,2048,128]{2,3,0,1:T(8,128)S(1)} fusion(bf16[2,2048,128]{1,2,0:T(8,128)(2,1)S(1)} %maximum_bitcast_fusion.19), kind=kOutput, calls=%fused_computation.22 | convolution fusion | flops 2210398208 | bytes 3145728 | tf_op jit(solution)/shard_map/fl,kdfc->kdlc/dot_general | solution.py:95
  780.3 63.5 %fusion.27 = f32[2,1,2048,128]{2,3,0,1:T(8,128)S(1)} fusion(bf16[2,2048,128]{1,2,0:T(8,128)(2,1)S(1)} %maximum_bitcast_fusion.21), kind=kOutput, calls=%fused_computation.24 | convolution fusion | flops 2210398208 | bytes 3145728 | tf_op jit(solution)/shard_map/fl,kdfc->kdlc/dot_general | solution.py:96
  843.8 0.4 fusion.56
  844.2 0.8 copy.25
  845.0 0.5 broadcast.173
  845.5 11.7 %reduce.6 = bf16[2048,128]{1,0:T(8,128)(2,1)S(1)} reduce(bf16[2048,1,128]{2,1,0:T(2,128)(2,1)S(1)} %bitcast.126, bf16[]{:T(256)} %broadcast.173), dimensions={1}, to_apply=%bitcast.80.reduce_sub_computation | reduce | bytes 1048578
  857.2 0.9 reshape.172
  858.2 9.5 %all-to-all-start = ((bf16[64,2,2048]{2,1,0:T(2,128)(2,1)}), bf16[64,2,2048]{2,1,0:T(2,128)(2,1)S(1)}, u32[]{:S(2)}, u32[]{:S(2)}) async-start(bf16[64,2,2048]{2,1,0:T(2,128)(2,1)} %reshape.172), calls=%async_computation | async-start | bytes 1048576 | tf_op jit(solution)/shard_map/all_to_all | solution.py:103
  867.7 0.8 copy.26
  868.4 11.5 %reduce.5 = bf16[2048,128]{1,0:T(8,128)(2,1)S(1)} reduce(bf16[2048,1,128]{2,1,0:T(2,128)(2,1)S(1)} %bitcast.127, bf16[]{:T(256)} %broadcast.173), dimensions={1}, to_apply=%bitcast.78.reduce_sub_computation | reduce | bytes 1048578
  880.0 0.9 reshape.170
  880.9 9.2 all-to-all-start.1
  890.1 0.7 dynamic-slice_convert_fusion
  891.5 0.5 reshape.173
  892.1 8.8 bitcast_reduce_fusion
  901.1 1.7 all-to-all-done.1
  902.7 0.5 reshape.171
  903.3 8.8 bitcast_reduce_fusion.1
  912.5 1.3 fusion.52
  913.8 0.8 fusion.17
  914.6 2.4 broadcast_multiply_fusion
  (20 shorter events, 1.8 us)
Async XLA Ops:
  6.5 566.4 %all-reduce.4.cloned.1.call-start = ((), (), s32[]{:S(2)}) async-start(), calls=%async_computation.2 | async-start | bytes 2097152 | tf_op jit(solution)/shard_map/psum | solution.py:15
  652.4 64.1 %copy-start = (f32[2048]{0:T(1024)S(1)}, f32[2048]{0:T(1024)}, u32[]{:S(2)}) copy-start(f32[2048]{0:T(1024)} %param.10) | copy-start | bytes 24580
  843.8 47.0 %copy-start.1 = (s32[64]{0:T(128)S(1)}, s32[64]{0:T(128)}, u32[]{:S(2)}) copy-start(s32[64]{0:T(128)} %param.12) | copy-start | bytes 772
  843.8 47.0 %copy-start.2 = (s32[64]{0:T(128)S(1)}, s32[64]{0:T(128)}, u32[]{:S(2)}) copy-start(s32[64]{0:T(128)} %param.11) | copy-start | bytes 772
  858.2 22.7 %all-to-all-start = ((bf16[64,2,2048]{2,1,0:T(2,128)(2,1)}), bf16[64,2,2048]{2,1,0:T(2,128)(2,1)S(1)}, u32[]{:S(2)}, u32[]{:S(2)}) async-start(bf16[64,2,2048]{2,1,0:T(2,128)(2,1)} %reshape.172), calls=%async_computation | async-start | bytes 1048576 | tf_op jit(solution)/shard_map/all_to_all | solution.py:103
  880.9 21.8 %all-to-all-start.1 = ((bf16[64,2,2048]{2,1,0:T(2,128)(2,1)}), bf16[64,2,2048]{2,1,0:T(2,128)(2,1)S(1)}, u32[]{:S(2)}, u32[]{:S(2)}) async-start(bf16[64,2,2048]{2,1,0:T(2,128)(2,1)} %reshape.170), calls=%async_computation.1 | async-start | bytes 1048576 | tf_op jit(solution)/shard_map/all_to_all | solution.py:104
Sparse Core Ops, SparseCore 0:
  10.9 561.9 all-reduce.3
where the time goes:
time: 932 us; the launch traced here: 924 us
  waiting for transfers between devices  563 us (60%)
  matrix products  256 us (27%)
  other arithmetic  35 us (4%)
  local copies, waits for them, and re-layouts  25.4 us (3%)
  starting transfers between devices  18.7 us (2%)
  between operations  16.2 us (2%)
  blocking collectives  10.5 us (1%)
    psum x1, waiting for transfers between devices, broadcast(): return lax.psum(jnp.where(mine, shard, jnp.zeros_like(shard)), axis)  561 us
    dot_general x1, matrix products, shards(): jnp.einsum('fl,kdlc->kdfc', sin_table, pair, preferred_element_type=jnp.f...  64 us
    dot_general x1, matrix products, shards(): jnp.einsum('fl,kdfc->kdlc', sin_table, held, preferred_element_type=jnp.f...  63.5 us
    dot_general x1, matrix products, shards(): jnp.einsum('fl,kdlc->kdfc', cos_table, pair, preferred_element_type=jnp.f...  63.5 us
    dot_general x1, matrix products, shards(): jnp.einsum('fl,kdfc->kdlc', cos_table, held, preferred_element_type=jnp.f...  63.2 us
    unnamed x2, other arithmetic  23.3 us
  transfers between devices with their start and end apart: 3, of which 2 were waited for; matrix products, arithmetic and copies ran while one was open for 3% of the time, Pallas kernels for 0%

commit v1 on v0

v1 whole, which is shorter than its diff:
```python
import math

import jax
import jax.numpy as jnp
import numpy as np
from jax import lax
from jax.sharding import PartitionSpec as P

HGRID = 16
VGRID = 16
PHASE_Q = 1024


def dft_table(length):
    split = 64
    hi_count = length // split
    freq = jnp.arange(length, dtype=jnp.int32)[:, None]
    step = 2.0 * math.pi / length
    hi_ang = ((freq * (split * jnp.arange(hi_count, dtype=jnp.int32)[None, :])) % length).astype(
        jnp.float32
    ) * step
    lo_ang = ((freq * jnp.arange(split, dtype=jnp.int32)[None, :]) % length).astype(
        jnp.float32
    ) * step
    hi_c, hi_s = jnp.cos(hi_ang)[:, :, None], jnp.sin(hi_ang)[:, :, None]
    lo_c, lo_s = jnp.cos(lo_ang)[:, None, :], jnp.sin(lo_ang)[:, None, :]
    cos_t = (hi_c * lo_c - hi_s * lo_s).reshape(length, length)
    sin_t = (hi_c * lo_s + hi_s * lo_c).reshape(length, length)
    table = jnp.concatenate([cos_t, sin_t], axis=1).astype(jnp.bfloat16)
    return lax.optimization_barrier(table)


def phase_tables(bperp, tdays):
    grid_points = jnp.arange(HGRID * VGRID, dtype=jnp.int32)
    height_step = grid_points // VGRID
    speed_step = grid_points % VGRID
    quanta = (
        bperp[:, None] * height_step[None, :] + tdays[:, None] * speed_step[None, :]
    ) % PHASE_Q
    angles = quanta.astype(jnp.float32) * (2.0 * math.pi / PHASE_Q)
    phase_re = jnp.cos(angles).astype(jnp.bfloat16)
    phase_im = jnp.sin(angles).astype(jnp.bfloat16)
    upper = jnp.concatenate([phase_re, -phase_im], axis=1)
    lower = jnp.concatenate([phase_im, phase_re], axis=1)
    return jnp.concatenate([upper, lower], axis=0)


def shards(slc_re, slc_im, ref_date, gain, bperp, tdays, mask):
    date_dev, lines, rg_dev = slc_re.shape
    assert date_dev == 1
    n_date = lax.axis_size("date")
    n_rng = lax.axis_size("rng")
    cols = rg_dev // n_date
    lines_dev = lines // n_date
    pixel_total = lines * rg_dev * n_rng
    me = lax.axis_index("date")
    f32 = jnp.float32

    own_re = slc_re[0]
    own_im = slc_im[0]
    wide_re = own_re.astype(f32)
    wide_im = own_im.astype(f32)
    local = jnp.sum(wide_re * wide_re + wide_im * wide_im)
    onehot = jnp.where(jnp.arange(n_date) == me, local, 0.0)
    date_sums = lax.psum(onehot, ("date", "rng"))
    scales = lax.rsqrt(date_sums / pixel_total + 1e-06)

    def to_date_rows(x):
        xt = x.T.reshape(cols, n_date, lines).transpose(1, 0, 2).reshape(n_date * cols, lines)
        return lax.all_to_all(xt, "date", split_axis=0, concat_axis=0, tiled=True)

    x_re = to_date_rows(own_re)
    x_im = to_date_rows(own_im)

    ref_index = ref_date[0]
    ref_scale = scales[ref_index]
    ref_re = lax.dynamic_slice_in_dim(x_re, ref_index * cols, cols, 0).astype(f32) * ref_scale
    ref_im = lax.dynamic_slice_in_dim(x_im, ref_index * cols, cols, 0).astype(f32) * ref_scale
    ref_re = jnp.tile(ref_re, (n_date, 1))
    ref_im = jnp.tile(ref_im, (n_date, 1))
    row_scale = jnp.repeat(scales, cols)[:, None]
    a_re = x_re.astype(f32) * row_scale
    a_im = x_im.astype(f32) * row_scale
    ifg_re = (a_re * ref_re + a_im * ref_im).astype(jnp.bfloat16)
    ifg_im = (a_im * ref_re - a_re * ref_im).astype(jnp.bfloat16)

    table = dft_table(lines)
    rows = n_date * cols
    stacked = jnp.concatenate([ifg_re, ifg_im], axis=0)
    fwd = jnp.dot(stacked, table, preferred_element_type=f32)
    spec_re = fwd[:rows, :lines] + fwd[rows:, lines:]
    spec_im = fwd[rows:, :lines] - fwd[:rows, lines:]
    weights = gain[None, :]
    held = jnp.concatenate(
        [(spec_re * weights).astype(jnp.bfloat16), (spec_im * weights).astype(jnp.bfloat16)],
        axis=0,
    )
    back = jnp.dot(held, table, preferred_element_type=f32)
    filt_re = ((back[:rows, :lines] - back[rows:, lines:]) * (1.0 / lines)).astype(jnp.bfloat16)
    filt_im = ((back[:rows, lines:] + back[rows:, :lines]) * (1.0 / lines)).astype(jnp.bfloat16)

    def to_pixel_rows(x):
        got = lax.all_to_all(x.T, "date", split_axis=0, concat_axis=0, tiled=True)
        return got.reshape(n_date, lines_dev, rows).transpose(1, 0, 2).reshape(-1, rows)

    y_re = to_pixel_rows(filt_re)
    y_im = to_pixel_rows(filt_im)

    grid_size = HGRID * VGRID
    phase = phase_tables(bperp, tdays).reshape(2, n_date, 2, grid_size)
    eye = jnp.eye(cols, dtype=jnp.bfloat16)
    big = (phase[:, :, None, None, :, :] * eye[None, None, :, :, None, None]).reshape(
        2 * rows, cols * 2 * grid_size
    )
    ys = jnp.concatenate([y_re, y_im], axis=1)
    spectra = jnp.dot(ys, big, preferred_element_type=f32).reshape(-1, cols, 2, grid_size)
    peri_re = spectra[:, :, 0, :]
    peri_im = spectra[:, :, 1, :]
    wr = y_re.astype(f32)
    wi = y_im.astype(f32)
    sel = jnp.asarray(np.tile(np.eye(cols, dtype=np.float32), (n_date, 1)))
    pixel_power = (
        jnp.dot(wr * wr + wi * wi, sel, precision=lax.Precision.HIGHEST) / n_date
    )
    result = (peri_re * peri_re + peri_im * peri_im) / (
        n_date * jnp.maximum(pixel_power, 1.0)
    )[:, :, None]
    result = result.reshape(lines_dev, n_date, cols, grid_size).transpose(0, 2, 1, 3)
    result = result.reshape(lines_dev, cols * n_date, grid_size)
    mask_rows = lax.dynamic_slice_in_dim(mask, me * lines_dev, lines_dev, 0)
    return result * mask_rows.astype(f32)[:, :, None]


def solution(mesh):
    in_specs = (P("date", None, "rng"), P("date", None, "rng"), P(), P(), P(), P(), P(None, "rng"))
    out_specs = P("date", "rng", None)
    return jax.shard_map(shards, mesh=mesh, in_specs=in_specs, out_specs=out_specs, check_vma=False)
```

time: 932 us -> 212 us (0.23)
  waiting for transfers between devices: 563 us -> 22 us
  matrix products: 256 us -> 22.8 us
  blocking collectives: 10.5 us -> 80.4 us
  between operations: 16.2 us -> 0.96 us
  local copies, waits for them, and re-layouts: 25.4 us -> 12.6 us
  starting transfers between devices: 18.7 us -> 28.7 us
    psum x1 -> x0, waiting for transfers between devices: 561 us -> none  [broadcast(): return lax.psum(jnp.where(mine, shard, jnp.zeros_like(shard)), axis)]
    dot_general x5 -> x4, matrix products: 256 us -> 22.8 us  [the longest x1 10.2 us: shards(): fwd = jnp.dot(stacked, table, preferred_element_type=f32)]
    psum x1, blocking collectives: 10.5 us -> 80.4 us  [shards(): date_sums = lax.psum(onehot, ('date', 'rng'))]
    unnamed x2 -> x0, other arithmetic: 23.3 us -> none
    all_to_all x2 -> x4, waiting for transfers between devices: 1.67 us -> 22 us  [the longest x2 22 us: to_pixel_rows(): got = lax.all_to_all(x.T, 'date', split_axis=0, concat_axis=0, tiled=True)]
    all_to_all x2, local copies, waits for them, and re-layouts: 17.5 us -> 0.4 us  [to_date_rows(): return lax.all_to_all(xt, 'date', split_axis=0, concat_axis=0, tiled=True)]
    concatenate x0 -> x2, other arithmetic: none -> 13.8 us  [the longest x1 13.8 us: dft_table(): table = jnp.concatenate([cos_t, sin_t], axis=1).astype(jnp.bfloat16)]
    all_to_all x2 -> x4, starting transfers between devices: 18.7 us -> 28.7 us  [the longest x2 19.2 us: to_date_rows(): return lax.all_to_all(xt, 'date', split_axis=0, concat_axis=0, tiled=True)]
  transfers between devices with their start and end apart: 3 -> 4, of which waited for: 2 -> 2; matrix products, arithmetic and copies ran while one was open for 3% -> 16% of each run, Pallas kernels for 0% -> 0%
where the time goes in v1:
time: 212 us; the launch traced here: 211 us
  blocking collectives  80.4 us (38%)
  other arithmetic  43.8 us (21%)
  starting transfers between devices  28.7 us (14%)
  matrix products  22.8 us (11%)
  waiting for transfers between devices  22 us (10%)
  local copies, waits for them, and re-layouts  12.6 us (6%)
    psum x1, blocking collectives, shards(): date_sums = lax.psum(onehot, ('date', 'rng'))  80.4 us
    all_to_all x2, waiting for transfers between devices, to_pixel_rows(): got = lax.all_to_all(x.T, 'date', split_axis=0, concat_axis=0, tiled=True)  22 us
    all_to_all x2, starting transfers between devices, to_date_rows(): return lax.all_to_all(xt, 'date', split_axis=0, concat_axis=0, tiled=True)  19.2 us
    concatenate x1, other arithmetic, dft_table(): table = jnp.concatenate([cos_t, sin_t], axis=1).astype(jnp.bfloat16)  13.8 us
    dot_general x1, matrix products, shards(): fwd = jnp.dot(stacked, table, preferred_element_type=f32)  10.2 us
    dot_general x1, matrix products, shards(): back = jnp.dot(held, table, preferred_element_type=f32)  10.2 us
    all_to_all x2, starting transfers between devices, to_pixel_rows(): got = lax.all_to_all(x.T, 'date', split_axis=0, concat_axis=0, tiled=True)  9.56 us
    another operation x1, other arithmetic  8.21 us
  transfers between devices with their start and end apart: 4, of which 2 were waited for; matrix products, arithmetic and copies ran while one was open for 16% of the time, Pallas kernels for 0%

profile of v1, /device:TPU:1, one launch (start us, length us, event | category | flops | bytes accessed | tf_op | source)
XLA Modules:
  0.0 211.2 jit_solution(16790087384997871464)
XLA Ops:
  0.0 1.2 copy.24
  1.3 1.3 copy.25
  2.6 10.3 %all-to-all-start.1 = ((bf16[64,2,2048]{2,1,0:T(2,128)(2,1)}), bf16[64,2,2048]{2,1,0:T(2,128)(2,1)S(1)}, u32[]{:S(2)}, u32[]{:S(2)}) async-start(bf16[64,2,2048]{2,1,0:T(2,128)(2,1)} %copy.25), calls=%async_computation.1 | async-start | bytes 1048576 | tf_op jit(solution)/shard_map/all_to_all | solution.py:70
  12.9 1.1 fusion.44
  14.0 2.0 fusion.38
  16.1 1.2 copy.22
  17.3 1.3 copy.23
  18.7 8.2 %subtract_convert_fusion = (bf16[2048,32,64]{0,2,1:T(8,128)(2,1)}, bf16[2048,32,64]{0,2,1:T(8,128)(2,1)}) fusion(f32[2048,64]{0,1:T(8,128)S(1)} %get-tuple-element.19, f32[2048,32]{0,1:T(8,128)S(1)} %get-tuple-element.16, f32[2048,64]{0,1:T(8,128)S(1)} %get-tuple-element.20, f32[2048,32]{0,1:T(8,128)S(1)} %get-tuple-element.15), kind=kLoop, calls=%fused_computation.2 | loop fusion | flops 33554432 | bytes 18350080 | tf_op jit(solution)/shard_map/convert.3
  26.9 8.8 %all-to-all-start = ((bf16[64,2,2048]{2,1,0:T(2,128)(2,1)}), bf16[64,2,2048]{2,1,0:T(2,128)(2,1)S(1)}, u32[]{:S(2)}, u32[]{:S(2)}) async-start(bf16[64,2,2048]{2,1,0:T(2,128)(2,1)} %copy.23), calls=%async_computation | async-start | bytes 1048576 | tf_op jit(solution)/shard_map/all_to_all | solution.py:70
  35.7 13.8 %pad_maximum_fusion = bf16[2048,4096]{0,1:T(8,128)(2,1)} fusion(bf16[2048,2048]{0,1:T(8,128)(2,1)} %bitcast.53, bf16[2048,2048]{0,1:T(8,128)(2,1)} %bitcast.52), kind=kLoop, calls=%fused_computation | loop fusion | flops 33554432 | bytes 33554432 | tf_op jit(solution)/shard_map/concatenate | solution.py:29
  50.2 0.9 add_reduce_fusion
  51.7 80.4 %psum.7 = f32[64]{0:T(128)S(1)} all-reduce(f32[64]{0:T(128)S(1)} %compare_select_fusion), channel_id=1, replica_groups=mesh['date'=64,'rng'=4] {'date','rng'}, use_global_device_ids=true, to_apply=%region_1.2 | all-reduce | flops 64 | bytes 512 | tf_op jit(solution)/shard_map/psum | solution.py:65
  133.4 0.7 convert_multiply_fusion.2
  134.7 0.7 tile.21
  135.9 0.7 tile.9
  136.6 1.7 add_convert_fusion.1
  138.3 10.2 %fusion.11 = f32[256,4096]{1,0:T(8,128)} fusion(bf16[2048,4096]{0,1:T(8,128)(2,1)} %pad_maximum_fusion, bf16[128,2048]{1,0:T(8,128)(2,1)S(1)} %get-tuple-element.10, bf16[128,2048]{1,0:T(8,128)(2,1)S(1)} %get-tuple-element.9), kind=kOutput, calls=%fused_computation.23 | convolution fusion | flops 4297064448 | bytes 22020096 | tf_op jit(solution)/shard_map/dot_general | solution.py:90
  148.5 2.5 %fusion.10 = (bf16[128,2048]{1,0:T(8,128)(2,1)S(1)}, bf16[128,2048]{1,0:T(8,128)(2,1)S(1)}) fusion(f32[256,4096]{1,0:T(8,128)} %fusion.11, f32[2048]{0:T(1024)S(1)} %copy-done.2), kind=kLoop, calls=%fused_computation.22 | loop fusion | flops 1572864 | bytes 5251072 | tf_op jit(solution)/shard_map/convert_element_type | solution.py:95
  151.0 10.2 %fusion.15 = f32[256,4096]{1,0:T(8,128)} fusion(bf16[2048,4096]{0,1:T(8,128)(2,1)} %pad_maximum_fusion, bf16[128,2048]{1,0:T(8,128)(2,1)S(1)} %get-tuple-element.6, bf16[128,2048]{1,0:T(8,128)(2,1)S(1)} %get-tuple-element.5), kind=kOutput, calls=%fused_computation.27 | convolution fusion | flops 4297064448 | bytes 22020096 | tf_op jit(solution)/shard_map/dot_general | solution.py:98
  161.2 2.6 %fusion.30 = (bf16[2048,128]{0,1:T(8,128)(2,1)S(1)}, bf16[2048,128]{0,1:T(8,128)(2,1)S(1)}) fusion(f32[256,4096]{1,0:T(8,128)} %fusion.15), kind=kLoop, calls=%fused_computation.51 | loop fusion | flops 1572864 | bytes 5242880 | tf_op jit(solution)/shard_map/transpose | solution.py:103
  163.8 1.0 copy.28
  164.8 5.0 %all-to-all-start.3 = ((bf16[64,32,128]{2,1,0:T(8,128)(2,1)}), bf16[64,32,128]{2,1,0:T(8,128)(2,1)S(1)}, u32[]{:S(2)}, u32[]{:S(2)}) async-start(bf16[64,32,128]{2,1,0:T(8,128)(2,1)} %bitcast.17), calls=%async_computation.3 | async-start | bytes 1048576 | tf_op jit(solution)/shard_map/all_to_all | solution.py:103
  169.8 1.0 copy.26
  170.8 11.9 %all-to-all-done.3 = bf16[64,32,128]{2,1,0:T(8,128)(2,1)S(1)} async-done(((bf16[64,32,128]{2,1,0:T(8,128)(2,1)}), bf16[64,32,128]{2,1,0:T(8,128)(2,1)S(1)}, u32[]{:S(2)}, u32[]{:S(2)}) %all-to-all-start.3) | async-done | bytes 524320 | tf_op jit(solution)/shard_map/all_to_all | solution.py:103
  182.7 4.5 %all-to-all-start.2 = ((bf16[64,32,128]{2,1,0:T(8,128)(2,1)}), bf16[64,32,128]{2,1,0:T(8,128)(2,1)S(1)}, u32[]{:S(2)}, u32[]{:S(2)}) async-start(bf16[64,32,128]{2,1,0:T(8,128)(2,1)} %bitcast.13), calls=%async_computation.2 | async-start | bytes 1048576 | tf_op jit(solution)/shard_map/all_to_all | solution.py:103
  189.1 0.7 dynamic-slice_convert_fusion
  190.0 10.1 %all-to-all-done.2 = bf16[64,32,128]{2,1,0:T(8,128)(2,1)S(1)} async-done(((bf16[64,32,128]{2,1,0:T(8,128)(2,1)}), bf16[64,32,128]{2,1,0:T(8,128)(2,1)S(1)}, u32[]{:S(2)}, u32[]{:S(2)}) %all-to-all-start.2) | async-done | bytes 524320 | tf_op jit(solution)/shard_map/all_to_all | solution.py:103
  200.3 1.3 fusion.19
  201.6 2.6 %fusion = f32[2048,2,1,256]{3,0,2,1:T(8,128)} fusion(f32[2048,2,2,256]{3,0,2,1:T(8,128)S(1)} %fusion.19), kind=kLoop, calls=%fused_computation.4 | loop fusion | flops 3145728 | bytes 12582912 | tf_op jit(solution)/shard_map/add | solution.py:125
  204.2 1.1 fusion.2
  205.4 2.6 %divide_bitcast_fusion = f32[32,2,64,256]{3,2,0,1:T(8,128)S(1)} fusion(f32[32,64,2,256]{3,1,0,2:T(8,128)} %bitcast.54, f32[32,64,2]{1,0,2:T(8,128)S(1)} %div.33), kind=kLoop, calls=%fused_computation.7 | loop fusion | flops 1048576 | bytes 8404992 | tf_op jit(solution)/shard_map/transpose | solution.py:128
  208.5 2.6 %bitcast_multiply_fusion = f32[32,128,256]{2,1,0:T(8,128)} fusion(f32[32,2,64,256]{3,2,1,0:T(8,128)S(1)} %copy.31, f32[32,128]{1,0:T(8,128)S(1)} %dynamic-slice_convert_fusion), kind=kLoop, calls=%fused_computation.6 | loop fusion | flops 1048576 | bytes 8404992 | tf_op jit(solution)/shard_map/mul | solution.py:131
  (37 shorter events, 5.8 us)
Async XLA Ops:
  2.6 24.3 %all-to-all-start.1 = ((bf16[64,2,2048]{2,1,0:T(2,128)(2,1)}), bf16[64,2,2048]{2,1,0:T(2,128)(2,1)S(1)}, u32[]{:S(2)}, u32[]{:S(2)}) async-start(bf16[64,2,2048]{2,1,0:T(2,128)(2,1)} %copy.25), calls=%async_computation.1 | async-start | bytes 1048576 | tf_op jit(solution)/shard_map/all_to_all | solution.py:70
  26.9 106.3 %all-to-all-start = ((bf16[64,2,2048]{2,1,0:T(2,128)(2,1)}), bf16[64,2,2048]{2,1,0:T(2,128)(2,1)S(1)}, u32[]{:S(2)}, u32[]{:S(2)}) async-start(bf16[64,2,2048]{2,1,0:T(2,128)(2,1)} %copy.23), calls=%async_computation | async-start | bytes 1048576 | tf_op jit(solution)/shard_map/all_to_all | solution.py:70
  133.1 0.9 copy-start
  133.4 0.8 copy-start.1
  138.3 10.2 %copy-start.2 = (f32[2048]{0:T(1024)S(1)}, f32[2048]{0:T(1024)}, u32[]{:S(2)}) copy-start(f32[2048]{0:T(1024)} %param.11) | copy-start | bytes 24580
  161.2 26.1 %copy-start.3 = (s32[64]{0:T(128)S(1)}, s32[64]{0:T(128)}, u32[]{:S(2)}) copy-start(s32[64]{0:T(128)} %param.13) | copy-start | bytes 772
  161.2 26.1 %copy-start.4 = (s32[64]{0:T(128)S(1)}, s32[64]{0:T(128)}, u32[]{:S(2)}) copy-start(s32[64]{0:T(128)} %param.12) | copy-start | bytes 772
  164.8 17.9 %all-to-all-start.3 = ((bf16[64,32,128]{2,1,0:T(8,128)(2,1)}), bf16[64,32,128]{2,1,0:T(8,128)(2,1)S(1)}, u32[]{:S(2)}, u32[]{:S(2)}) async-start(bf16[64,32,128]{2,1,0:T(8,128)(2,1)} %bitcast.17), calls=%async_computation.3 | async-start | bytes 1048576 | tf_op jit(solution)/shard_map/all_to_all | solution.py:103
  182.7 17.4 %all-to-all-start.2 = ((bf16[64,32,128]{2,1,0:T(8,128)(2,1)}), bf16[64,32,128]{2,1,0:T(8,128)(2,1)S(1)}, u32[]{:S(2)}, u32[]{:S(2)}) async-start(bf16[64,32,128]{2,1,0:T(8,128)(2,1)} %bitcast.13), calls=%async_computation.2 | async-start | bytes 1048576 | tf_op jit(solution)/shard_map/all_to_all | solution.py:103
  201.6 2.6 %copy-start.5 = (f32[128,2]{1,0:T(8,128)S(1)}, f32[128,2]{1,0:T(8,128)}, u32[]{:S(2)}) copy-start(f32[128,2]{1,0:T(8,128)} %constant.105.clone) | copy-start | bytes 3076

commit v2 on v1

--- a/solution.py
+++ b/solution.py
@@ -24,10 +24,9 @@
     ) * step
     hi_c, hi_s = jnp.cos(hi_ang)[:, :, None], jnp.sin(hi_ang)[:, :, None]
     lo_c, lo_s = jnp.cos(lo_ang)[:, None, :], jnp.sin(lo_ang)[:, None, :]
-    cos_t = (hi_c * lo_c - hi_s * lo_s).reshape(length, length)
-    sin_t = (hi_c * lo_s + hi_s * lo_c).reshape(length, length)
-    table = jnp.concatenate([cos_t, sin_t], axis=1).astype(jnp.bfloat16)
-    return lax.optimization_barrier(table)
+    cos_t = (hi_c * lo_c - hi_s * lo_s).reshape(length, length).astype(jnp.bfloat16)
+    sin_t = (hi_c * lo_s + hi_s * lo_c).reshape(length, length).astype(jnp.bfloat16)
+    return lax.optimization_barrier((cos_t, sin_t))
 
 
 def phase_tables(bperp, tdays):
@@ -61,16 +60,17 @@
     wide_re = own_re.astype(f32)
     wide_im = own_im.astype(f32)
     local = jnp.sum(wide_re * wide_re + wide_im * wide_im)
-    onehot = jnp.where(jnp.arange(n_date) == me, local, 0.0)
-    date_sums = lax.psum(onehot, ("date", "rng"))
+    spread = jnp.broadcast_to(local, (n_date * n_rng, 1))
+    gathered = lax.all_to_all(spread, ("date", "rng"), split_axis=0, concat_axis=0, tiled=True)
+    date_sums = jnp.sum(gathered.reshape(n_date, n_rng), axis=1)
     scales = lax.rsqrt(date_sums / pixel_total + 1e-06)
 
-    def to_date_rows(x):
-        xt = x.T.reshape(cols, n_date, lines).transpose(1, 0, 2).reshape(n_date * cols, lines)
-        return lax.all_to_all(xt, "date", split_axis=0, concat_axis=0, tiled=True)
-
-    x_re = to_date_rows(own_re)
-    x_im = to_date_rows(own_im)
+    both = jnp.stack([own_re.T, own_im.T]).reshape(2, cols, n_date, lines)
+    both = both.transpose(2, 0, 1, 3).reshape(n_date * 2 * cols, lines)
+    got = lax.all_to_all(both, "date", split_axis=0, concat_axis=0, tiled=True)
+    got = got.reshape(n_date, 2, cols, lines)
+    x_re = got[:, 0].reshape(n_date * cols, lines)
+    x_im = got[:, 1].reshape(n_date * cols, lines)
 
     ref_index = ref_date[0]
     ref_scale = scales[ref_index]
@@ -84,27 +84,28 @@
     ifg_re = (a_re * ref_re + a_im * ref_im).astype(jnp.bfloat16)
     ifg_im = (a_im * ref_re - a_re * ref_im).astype(jnp.bfloat16)
 
-    table = dft_table(lines)
+    cos_t, sin_t = dft_table(lines)
     rows = n_date * cols
     stacked = jnp.concatenate([ifg_re, ifg_im], axis=0)
-    fwd = jnp.dot(stacked, table, preferred_element_type=f32)
-    spec_re = fwd[:rows, :lines] + fwd[rows:, lines:]
-    spec_im = fwd[rows:, :lines] - fwd[:rows, lines:]
+    fc = jnp.dot(stacked, cos_t, preferred_element_type=f32)
+    fs = jnp.dot(stacked, sin_t, preferred_element_type=f32)
+    spec_re = fc[:rows] + fs[rows:]
+    spec_im = fc[rows:] - fs[:rows]
     weights = gain[None, :]
     held = jnp.concatenate(
         [(spec_re * weights).astype(jnp.bfloat16), (spec_im * weights).astype(jnp.bfloat16)],
         axis=0,
     )
-    back = jnp.dot(held, table, preferred_element_type=f32)
-    filt_re = ((back[:rows, :lines] - back[rows:, lines:]) * (1.0 / lines)).astype(jnp.bfloat16)
-    filt_im = ((back[:rows, lines:] + back[rows:, :lines]) * (1.0 / lines)).astype(jnp.bfloat16)
+    bc = jnp.dot(held, cos_t, preferred_element_type=f32)
+    bs = jnp.dot(held, sin_t, preferred_element_type=f32)
+    filt_re = ((bc[:rows] - bs[rows:]) * (1.0 / lines)).astype(jnp.bfloat16)
+    filt_im = ((bs[:rows] + bc[rows:]) * (1.0 / lines)).astype(jnp.bfloat16)
 
-    def to_pixel_rows(x):
-        got = lax.all_to_all(x.T, "date", split_axis=0, concat_axis=0, tiled=True)
-        return got.reshape(n_date, lines_dev, rows).transpose(1, 0, 2).reshape(-1, rows)
-
-    y_re = to_pixel_rows(filt_re)
-    y_im = to_pixel_rows(filt_im)
+    pair = jnp.concatenate([filt_re, filt_im], axis=0).T
+    got = lax.all_to_all(pair, "date", split_axis=0, concat_axis=0, tiled=True)
+    ys = got.reshape(n_date, lines_dev, 2 * rows).transpose(1, 0, 2).reshape(-1, 2 * rows)
+    y_re = ys[:, :rows]
+    y_im = ys[:, rows:]
 
     grid_size = HGRID * VGRID
     phase = phase_tables(bperp, tdays).reshape(2, n_date, 2, grid_size)
@@ -112,7 +113,6 @@
     big = (phase[:, :, None, None, :, :] * eye[None, None, :, :, None, None]).reshape(
         2 * rows, cols * 2 * grid_size
     )
-    ys = jnp.concatenate([y_re, y_im], axis=1)
     spectra = jnp.dot(ys, big, preferred_element_type=f32).reshape(-1, cols, 2, grid_size)
     peri_re = spectra[:, :, 0, :]
     peri_im = spectra[:, :, 1, :]

time: 212 us -> 114 us (0.54)
  blocking collectives: 80.4 us -> 0 us
  other arithmetic: 43.8 us -> 26.6 us
  waiting for transfers between devices: 22 us -> 30.8 us
  matrix products: 22.8 us -> 15.6 us
  starting transfers between devices: 28.7 us -> 25.6 us
    psum x1 -> x0, blocking collectives: 80.4 us -> none  [shards(): date_sums = lax.psum(onehot, ('date', 'rng'))]
    concatenate x1 -> x0, other arithmetic: 13.8 us -> none  [dft_table(): table = jnp.concatenate([cos_t, sin_t], axis=1).astype(jnp.bfloat16)]
    all_to_all x4 -> x3, waiting for transfers between devices: 22 us -> 30.8 us  [the longest x1 15.8 us: shards(): got = lax.all_to_all(pair, 'date', split_axis=0, concat_axis=0, tiled=True)]
    convert_element_type x0 -> x2, other arithmetic: none -> 8.67 us  [the longest x1 8.27 us: dft_table(): (hi_c * lo_s + hi_s * lo_c).reshape(length, length).astype(jnp.bfloat16)]
    another operation x1, other arithmetic: 8.21 us -> 0.1 us  [shards(): both = jnp.stack([own_re.T, own_im.T]).reshape(2, cols, n_date, lines)]
    dot_general x2 -> x4, matrix products: 20.3 us -> 13.2 us  [the longest x1 5.89 us: shards(): fc = jnp.dot(stacked, cos_t, preferred_element_type=f32)]
    transpose x6 -> x2, local copies, waits for them, and re-layouts: 5.07 us -> 1.89 us  [the longest x1 1.31 us: shards(): pair = jnp.concatenate([filt_re, filt_im], axis=0).T]
    all_to_all x4 -> x3, starting transfers between devices: 28.7 us -> 25.6 us  [the longest x1 15.6 us: shards(): lax.all_to_all(spread, ('date', 'rng'), split_axis=0, concat_axis=0, tile...]
  transfers between devices with their start and end apart: 4 -> 3, of which waited for: 2 -> 3; matrix products, arithmetic and copies ran while one was open for 16% -> 16% of each run, Pallas kernels for 0% -> 0%
where the time goes in v2:
time: 114 us
  waiting for transfers between devices  30.8 us (27%)
  other arithmetic  26.6 us (23%)
  starting transfers between devices  25.6 us (22%)
  matrix products  15.6 us (14%)
  local copies, waits for them, and re-layouts  14.1 us (12%)
    all_to_all x1, waiting for transfers between devices, shards(): got = lax.all_to_all(pair, 'date', split_axis=0, concat_axis=0, tiled=True)  15.8 us
    all_to_all x1, starting transfers between devices, shards(): lax.all_to_all(spread, ('date', 'rng'), split_axis=0, concat_axis=0, tile...  15.6 us
    all_to_all x1, waiting for transfers between devices, shards(): lax.all_to_all(spread, ('date', 'rng'), split_axis=0, concat_axis=0, tile...  11 us
    convert_element_type x1, other arithmetic, dft_table(): (hi_c * lo_s + hi_s * lo_c).reshape(length, length).astype(jnp.bfloat16)  8.27 us
    dot_general x1, matrix products, shards(): fc = jnp.dot(stacked, cos_t, preferred_element_type=f32)  5.89 us
    all_to_all x1, starting transfers between devices, shards(): got = lax.all_to_all(both, 'date', split_axis=0, concat_axis=0, tiled=True)  5.13 us
    all_to_all x1, starting transfers between devices, shards(): got = lax.all_to_all(pair, 'date', split_axis=0, concat_axis=0, tiled=True)  4.78 us
    all_to_all x1, waiting for transfers between devices, shards(): got = lax.all_to_all(both, 'date', split_axis=0, concat_axis=0, tiled=True)  4.07 us
  transfers between devices with their start and end apart: 3, of which 3 were waited for; matrix products, arithmetic and copies ran while one was open for 16% of the time, Pallas kernels for 0%

profile of v2, /device:TPU:1, one launch (start us, length us, event | category | flops | bytes accessed | tf_op | source)
XLA Modules:
  0.0 113.8 jit_solution(7835930602624382222)
XLA Ops:
  0.0 1.2 %copy.25 = bf16[1,2048,128]{1,2,0:T(8,128)(2,1)S(1)} copy(bf16[1,2048,128]{2,1,0:T(8,128)(2,1)} %param.8) | data formatting | bytes 1048576 | tf_op args[0]
  1.3 1.2 %copy.26 = bf16[1,2048,128]{1,2,0:T(8,128)(2,1)S(1)} copy(bf16[1,2048,128]{2,1,0:T(8,128)(2,1)} %param.9) | data formatting | bytes 1048576 | tf_op args[1]
  2.5 0.9 add_reduce_fusion
  3.4 1.4 %broadcast_in_dim.4 = f32[256,1,1]{2,1,0:T(1,128)} broadcast(f32[]{:T(128)} %add_reduce_fusion), dimensions={} | broadcast | bytes 1028 | tf_op jit(solution)/shard_map/broadcast_in_dim | solution.py:63
  4.7 15.6 %all-to-all-start.1 = ((f32[256,1,1]{2,1,0:T(1,128)}), f32[256,1,1]{2,1,0:T(1,128)S(1)}, u32[]{:S(2)}, u32[]{:S(2)}) async-start(f32[256,1,1]{2,1,0:T(1,128)} %broadcast_in_dim.4), calls=%async_computation.1 | async-start | bytes 262144 | tf_op jit(solution)/shard_map/all_to_all | solution.py:64
  20.5 1.8 %copy.27 = bf16[64,4,2048]{2,1,0:T(4,128)(2,1)} copy(bf16[64,4,2048]{2,0,1:T(8,128)(2,1)S(1)} %bitcast.70) | data formatting | bytes 2097152 | tf_op jit(solution)/shard_map/all_to_all | solution.py:70
  22.3 11.0 %all-to-all-done.1 = f32[256,1,1]{2,1,0:T(1,128)S(1)} async-done(((f32[256,1,1]{2,1,0:T(1,128)}), f32[256,1,1]{2,1,0:T(1,128)S(1)}, u32[]{:S(2)}, u32[]{:S(2)}) %all-to-all-start.1) | async-done | bytes 1056 | tf_op jit(solution)/shard_map/all_to_all | solution.py:64
  33.3 5.1 %all-to-all-start = ((bf16[64,4,2048]{2,1,0:T(4,128)(2,1)}), bf16[64,4,2048]{2,1,0:T(4,128)(2,1)S(1)}, u32[]{:S(2)}, u32[]{:S(2)}) async-start(bf16[64,4,2048]{2,1,0:T(4,128)(2,1)} %copy.27), calls=%async_computation | async-start | bytes 2097152 | tf_op jit(solution)/shard_map/all_to_all | solution.py:70
  39.1 2.0 %fusion.31 = (f32[2048,64]{0,1:T(8,128)S(1)}, f32[2048,64]{0,1:T(8,128)S(1)}) fusion(), kind=kLoop, calls=%fused_computation.60 | loop fusion | flops 1835008 | bytes 1048576 | tf_op jit(solution)/shard_map/sin | solution.py:26
  41.1 1.1 fusion.37
  42.2 8.3 %add_convert_fusion = (bf16[2048,32,64]{0,2,1:T(8,128)(2,1)}, bf16[2048,32,64]{0,2,1:T(8,128)(2,1)}) fusion(f32[2048,64]{0,1:T(8,128)S(1)} %get-tuple-element.23, f32[2048,32]{0,1:T(8,128)S(1)} %get-tuple-element.22, f32[2048,64]{0,1:T(8,128)S(1)} %get-tuple-element.24, f32[2048,32]{0,1:T(8,128)S(1)} %get-tuple-element.21), kind=kLoop, calls=%fused_computation | loop fusion | flops 33554432 | bytes 18350080 | tf_op jit(solution)/shard_map/convert_element_type | solution.py:28
  50.5 1.0 reduce
  52.7 4.1 %all-to-all-done = bf16[64,4,2048]{2,1,0:T(4,128)(2,1)S(1)} async-done(((bf16[64,4,2048]{2,1,0:T(4,128)(2,1)}), bf16[64,4,2048]{2,1,0:T(4,128)(2,1)S(1)}, u32[]{:S(2)}, u32[]{:S(2)}) %all-to-all-start) | async-done | bytes 1048608 | tf_op jit(solution)/shard_map/all_to_all | solution.py:70
  56.7 0.7 reshape.196
  57.5 0.7 slice_bitcast_fusion.1
  58.6 0.7 convert_multiply_fusion.2
  59.9 0.7 tile.21
  61.1 0.7 tile.9
  61.9 1.8 %add_convert_fusion.1 = (bf16[128,2048]{1,0:T(8,128)(2,1)S(1)}, bf16[128,2048]{1,0:T(8,128)(2,1)S(1)}) fusion(f32[128,2048]{1,0:T(8,128)S(1)} %tile.21, bf16[128,2048]{1,0:T(8,128)(2,1)} %copy-done.1, f32[128,2048]{1,0:T(8,128)S(1)} %tile.9, bf16[128,2048]{1,0:T(8,128)(2,1)} %copy-done, f32[128]{0:T(128)S(1)} %mul.306), kind=kLoop, calls=%fused_computation.32 | loop fusion | flops 3145728 | bytes 4194816 | tf_op jit(solution)/shard_map/convert_element_type | solution.py:84
  63.7 5.9 %fusion.19 = f32[256,2048]{1,0:T(8,128)S(1)} fusion(bf16[2048,2048]{0,1:T(8,128)(2,1)} %bitcast.61, bf16[128,2048]{1,0:T(8,128)(2,1)S(1)} %get-tuple-element.14, bf16[128,2048]{1,0:T(8,128)(2,1)S(1)} %get-tuple-element.13), kind=kOutput, calls=%fused_computation.42 | convolution fusion | flops 2149580800 | bytes 11534336 | tf_op jit(solution)/shard_map/dot_general | solution.py:90
  69.7 2.4 %fusion.18 = f32[256,2048]{1,0:T(8,128)S(1)} fusion(bf16[2048,2048]{0,1:T(8,128)(2,1)S(1)} %bitcast.59, bf16[128,2048]{1,0:T(8,128)(2,1)S(1)} %get-tuple-element.14, bf16[128,2048]{1,0:T(8,128)(2,1)S(1)} %get-tuple-element.13), kind=kOutput, calls=%fused_computation.41 | convolution fusion | flops 2149580800 | bytes 11534336 | tf_op jit(solution)/shard_map/dot_general | solution.py:91
  72.5 2.4 %fusion.17 = f32[256,2048]{1,0:T(8,128)S(1)} fusion(bf16[2048,2048]{0,1:T(8,128)(2,1)S(1)} %bitcast.64, bf16[128,2048]{1,0:T(8,128)(2,1)S(1)} %get-tuple-element.10, bf16[128,2048]{1,0:T(8,128)(2,1)S(1)} %get-tuple-element.9), kind=kOutput, calls=%fused_computation.40 | convolution fusion | flops 2149580800 | bytes 11534336 | tf_op jit(solution)/shard_map/dot_general | solution.py:99
  74.9 2.6 %fusion.16 = f32[256,2048]{1,0:T(8,128)S(1)} fusion(bf16[2048,2048]{0,1:T(8,128)(2,1)S(1)} %bitcast.60, bf16[128,2048]{1,0:T(8,128)(2,1)S(1)} %get-tuple-element.10, bf16[128,2048]{1,0:T(8,128)(2,1)S(1)} %get-tuple-element.9), kind=kOutput, calls=%fused_computation.39 | convolution fusion | flops 2149580800 | bytes 11534336 | tf_op jit(solution)/shard_map/dot_general | solution.py:100
  78.0 1.3 %copy.30 = bf16[2048,256]{1,0:T(8,128)(2,1)} copy(bf16[2048,256]{0,1:T(8,128)(2,1)S(1)} %maximum_bitcast_fusion) | data formatting | bytes 2097152 | tf_op jit(solution)/shard_map/transpose | solution.py:104
  79.3 4.8 %all-to-all-start.2 = ((bf16[64,32,256]{2,1,0:T(8,128)(2,1)}), bf16[64,32,256]{2,1,0:T(8,128)(2,1)S(1)}, u32[]{:S(2)}, u32[]{:S(2)}) async-start(bf16[64,32,256]{2,1,0:T(8,128)(2,1)} %bitcast.13), calls=%async_computation.2 | async-start | bytes 2097152 | tf_op jit(solution)/shard_map/all_to_all | solution.py:105
  85.9 0.7 dynamic-slice_convert_fusion
  86.6 15.8 %all-to-all-done.2 = bf16[64,32,256]{2,1,0:T(8,128)(2,1)S(1)} async-done(((bf16[64,32,256]{2,1,0:T(8,128)(2,1)}), bf16[64,32,256]{2,1,0:T(8,128)(2,1)S(1)}, u32[]{:S(2)}, u32[]{:S(2)}) %all-to-all-start.2) | async-done | bytes 1048608 | tf_op jit(solution)/shard_map/all_to_all | solution.py:105
  103.0 1.3 %fusion.48 = f32[2048,2,2,256]{3,0,2,1:T(8,128)S(1)} fusion(bf16[2048,256,1,1]{1,0,3,2:T(8,128)(2,1)S(1)} %bitcast.67, bf16[2,2,256,256]{3,2,1,0:T(8,128)(2,1)S(1)} %bitcast.71), kind=kOutput, calls=%fused_computation.94 | convolution fusion | flops 1073741824 | bytes 9961472 | tf_op jit(solution)/shard_map/dot_general | solution.py:116
  104.3 2.6 %fusion = f32[2048,2,1,256]{3,0,2,1:T(8,128)} fusion(f32[2048,2,2,256]{3,0,2,1:T(8,128)S(1)} %fusion.48), kind=kLoop, calls=%fused_computation.3 | loop fusion | flops 3145728 | bytes 12582912 | tf_op jit(solution)/shard_map/add | solution.py:125
  106.8 1.1 %fusion.2 = f32[2048,2]{0,1:T(2,128)S(1)} fusion(f32[128,2]{1,0:T(8,128)S(1)} %copy-done.5, bf16[2048,256]{1,0:T(8,128)(2,1)S(1)} %bitcast.68), kind=kOutput, calls=%fused_computation.9 | convolution fusion | flops 7614464 | bytes 1065984 | tf_op jit(solution)/shard_map/dot_general | solution.py:123
  108.1 2.6 %divide_bitcast_fusion = f32[32,2,64,256]{3,2,0,1:T(8,128)S(1)} fusion(f32[32,64,2,256]{3,1,0,2:T(8,128)} %bitcast.56, f32[32,64,2]{1,0,2:T(8,128)S(1)} %div.33), kind=kLoop, calls=%fused_computation.6 | loop fusion | flops 1048576 | bytes 8404992 | tf_op jit(solution)/shard_map/transpose | solution.py:128
  111.2 2.6 %bitcast_multiply_fusion = f32[32,128,256]{2,1,0:T(8,128)} fusion(f32[32,2,64,256]{3,2,1,0:T(8,128)S(1)} %copy.33, f32[32,128]{1,0:T(8,128)S(1)} %dynamic-slice_convert_fusion), kind=kLoop, calls=%fused_computation.5 | loop fusion | flops 1048576 | bytes 8404992 | tf_op jit(solution)/shard_map/mul | solution.py:131
  (49 shorter events, 6.5 us)
Async XLA Ops:
  4.7 28.6 %all-to-all-start.1 = ((f32[256,1,1]{2,1,0:T(1,128)}), f32[256,1,1]{2,1,0:T(1,128)S(1)}, u32[]{:S(2)}, u32[]{:S(2)}) async-start(f32[256,1,1]{2,1,0:T(1,128)} %broadcast_in_dim.4), calls=%async_computation.1 | async-start | bytes 262144 | tf_op jit(solution)/shard_map/all_to_all | solution.py:64
  33.3 23.4 %all-to-all-start = ((bf16[64,4,2048]{2,1,0:T(4,128)(2,1)}), bf16[64,4,2048]{2,1,0:T(4,128)(2,1)S(1)}, u32[]{:S(2)}, u32[]{:S(2)}) async-start(bf16[64,4,2048]{2,1,0:T(4,128)(2,1)} %copy.27), calls=%async_computation | async-start | bytes 2097152 | tf_op jit(solution)/shard_map/all_to_all | solution.py:70
  58.4 0.9 copy-start
  58.6 0.8 copy-start.1
  61.9 7.8 %slice-start = ((s8[8388608]{0:T(1024)(128)(4,1)}), s8[4194304]{0:T(1024)(128)(4,1)S(1)}, s32[]{:S(2)}) async-start(s8[8388608]{0:T(1024)(128)(4,1)} %bitcast.57), calls=%async_computation.3 | async-start | bytes 8388608
  63.7 5.9 %slice-start.1 = ((s8[8388608]{0:T(1024)(128)(4,1)}), s8[4194304]{0:T(1024)(128)(4,1)S(1)}, s32[]{:S(2)}) async-start(s8[8388608]{0:T(1024)(128)(4,1)} %bitcast.57), calls=%async_computation.4 | async-start | bytes 8388608
  63.7 8.7 %slice-start.2 = ((s8[8388608]{0:T(1024)(128)(4,1)}), s8[4194304]{0:T(1024)(128)(4,1)S(1)}, s32[]{:S(2)}) async-start(s8[8388608]{0:T(1024)(128)(4,1)} %bitcast.62), calls=%async_computation.5 | async-start | bytes 8388608
  69.7 2.4 %copy-start.2 = (f32[2048]{0:T(1024)S(1)}, f32[2048]{0:T(1024)}, u32[]{:S(2)}) copy-start(f32[2048]{0:T(1024)} %param.11) | copy-start | bytes 24580
  69.7 2.8 %slice-start.3 = ((s8[8388608]{0:T(1024)(128)(4,1)}), s8[4194304]{0:T(1024)(128)(4,1)S(1)}, s32[]{:S(2)}) async-start(s8[8388608]{0:T(1024)(128)(4,1)} %bitcast.62), calls=%async_computation.6 | async-start | bytes 8388608
  77.9 6.2 %copy-start.3 = (s32[64]{0:T(128)S(1)}, s32[64]{0:T(128)}, u32[]{:S(2)}) copy-start(s32[64]{0:T(128)} %param.13) | copy-start | bytes 772
  77.9 6.2 %copy-start.4 = (s32[64]{0:T(128)S(1)}, s32[64]{0:T(128)}, u32[]{:S(2)}) copy-start(s32[64]{0:T(128)} %param.12) | copy-start | bytes 772
  79.3 23.1 %all-to-all-start.2 = ((bf16[64,32,256]{2,1,0:T(8,128)(2,1)}), bf16[64,32,256]{2,1,0:T(8,128)(2,1)S(1)}, u32[]{:S(2)}, u32[]{:S(2)}) async-start(bf16[64,32,256]{2,1,0:T(8,128)(2,1)} %bitcast.13), calls=%async_computation.2 | async-start | bytes 2097152 | tf_op jit(solution)/shard_map/all_to_all | solution.py:105
  104.3 2.6 %copy-start.5 = (f32[128,2]{1,0:T(8,128)S(1)}, f32[128,2]{1,0:T(8,128)}, u32[]{:S(2)}) copy-start(f32[128,2]{1,0:T(8,128)} %constant.105.clone) | copy-start | bytes 3076

commit v3 on v2

--- a/solution.py
+++ b/solution.py
@@ -2,7 +2,6 @@
 
 import jax
 import jax.numpy as jnp
-import numpy as np
 from jax import lax
 from jax.sharding import PartitionSpec as P
 
@@ -60,15 +59,22 @@
     wide_re = own_re.astype(f32)
     wide_im = own_im.astype(f32)
     local = jnp.sum(wide_re * wide_re + wide_im * wide_im)
-    spread = jnp.broadcast_to(local, (n_date * n_rng, 1))
-    gathered = lax.all_to_all(spread, ("date", "rng"), split_axis=0, concat_axis=0, tiled=True)
-    date_sums = jnp.sum(gathered.reshape(n_date, n_rng), axis=1)
-    scales = lax.rsqrt(date_sums / pixel_total + 1e-06)
+    spread = jnp.broadcast_to(local, (n_rng, 1))
+    own_sum = jnp.sum(lax.all_to_all(spread, "rng", split_axis=0, concat_axis=0, tiled=True))
+    hi = lax.reduce_precision(own_sum, exponent_bits=8, mantissa_bits=7)
+    mid = lax.reduce_precision(own_sum - hi, exponent_bits=8, mantissa_bits=7)
+    lo = lax.reduce_precision(own_sum - hi - mid, exponent_bits=8, mantissa_bits=7)
+    words = jnp.zeros((128,), f32).at[0].set(hi).at[1].set(mid).at[2].set(lo)
+    words = jnp.broadcast_to(words.astype(jnp.bfloat16), (n_date, 128))
 
     both = jnp.stack([own_re.T, own_im.T]).reshape(2, cols, n_date, lines)
-    both = both.transpose(2, 0, 1, 3).reshape(n_date * 2 * cols, lines)
+    both = both.transpose(2, 0, 1, 3).reshape(n_date, 2 * cols * lines)
+    both = jnp.concatenate([both, words], axis=1)
     got = lax.all_to_all(both, "date", split_axis=0, concat_axis=0, tiled=True)
-    got = got.reshape(n_date, 2, cols, lines)
+    sums = got[:, 2 * cols * lines:2 * cols * lines + 3].astype(f32)
+    date_sums = (sums[:, 0] + sums[:, 1]) + sums[:, 2]
+    scales = lax.rsqrt(date_sums / pixel_total + 1e-06)
+    got = got[:, :2 * cols * lines].reshape(n_date, 2, cols, lines)
     x_re = got[:, 0].reshape(n_date * cols, lines)
     x_im = got[:, 1].reshape(n_date * cols, lines)
 
@@ -101,34 +107,26 @@
     filt_re = ((bc[:rows] - bs[rows:]) * (1.0 / lines)).astype(jnp.bfloat16)
     filt_im = ((bs[:rows] + bc[rows:]) * (1.0 / lines)).astype(jnp.bfloat16)
 
-    pair = jnp.concatenate([filt_re, filt_im], axis=0).T
+    pair = jnp.concatenate([filt_re, filt_im], axis=0).reshape(2, n_date, cols, lines)
+    pair = pair.transpose(2, 0, 1, 3).reshape(2 * rows, lines).T
     got = lax.all_to_all(pair, "date", split_axis=0, concat_axis=0, tiled=True)
-    ys = got.reshape(n_date, lines_dev, 2 * rows).transpose(1, 0, 2).reshape(-1, 2 * rows)
-    y_re = ys[:, :rows]
-    y_im = ys[:, rows:]
+    z = got.reshape(n_date, lines_dev, cols, 2 * n_date).transpose(1, 2, 0, 3)
+    z = z.reshape(lines_dev * cols * n_date, 2 * n_date)
 
     grid_size = HGRID * VGRID
-    phase = phase_tables(bperp, tdays).reshape(2, n_date, 2, grid_size)
-    eye = jnp.eye(cols, dtype=jnp.bfloat16)
-    big = (phase[:, :, None, None, :, :] * eye[None, None, :, :, None, None]).reshape(
-        2 * rows, cols * 2 * grid_size
-    )
-    spectra = jnp.dot(ys, big, preferred_element_type=f32).reshape(-1, cols, 2, grid_size)
-    peri_re = spectra[:, :, 0, :]
-    peri_im = spectra[:, :, 1, :]
-    wr = y_re.astype(f32)
-    wi = y_im.astype(f32)
-    sel = jnp.asarray(np.tile(np.eye(cols, dtype=np.float32), (n_date, 1)))
-    pixel_power = (
-        jnp.dot(wr * wr + wi * wi, sel, precision=lax.Precision.HIGHEST) / n_date
-    )
+    phase = phase_tables(bperp, tdays)
+    spectra = jnp.dot(z, phase, preferred_element_type=f32)
+    peri_re = spectra[:, :grid_size]
+    peri_im = spectra[:, grid_size:]
+    wide = z.astype(f32)
+    pixel_power = jnp.sum(wide * wide, axis=1) / n_date
+    mask_rows = lax.dynamic_slice_in_dim(mask, me * lines_dev, lines_dev, 0)
+    mask_px = mask_rows.reshape(-1).astype(f32)
     result = (peri_re * peri_re + peri_im * peri_im) / (
         n_date * jnp.maximum(pixel_power, 1.0)
-    )[:, :, None]
-    result = result.reshape(lines_dev, n_date, cols, grid_size).transpose(0, 2, 1, 3)
-    result = result.reshape(lines_dev, cols * n_date, grid_size)
-    mask_rows = lax.dynamic_slice_in_dim(mask, me * lines_dev, lines_dev, 0)
-    return result * mask_rows.astype(f32)[:, :, None]
+    )[:, None]
+    result = result * mask_px[:, None]
+    return result.reshape(lines_dev, cols * n_date, grid_size)
 
 
 def solution(mesh):

time: 114 us -> 116 us (1.018)
  local copies, waits for them, and re-layouts: 14.1 us -> 20.3 us
  between operations: 1.11 us -> 5.3 us
  waiting for transfers between devices: 30.8 us -> 28 us
  other arithmetic: 26.6 us -> 24.2 us
  starting transfers between devices: 25.6 us -> 23.7 us
  matrix products: 15.6 us -> 14.4 us
    all_to_all x1, starting transfers between devices: 15.6 us -> 9 us  [shards(): lax.all_to_all(spread, 'rng', split_axis=0, concat_axis=0, tiled=True)]
    all_to_all x1, waiting for transfers between devices: 11 us -> 4.44 us  [shards(): lax.all_to_all(spread, 'rng', split_axis=0, concat_axis=0, tiled=True)]
    all_to_all x1, starting transfers between devices: 5.13 us -> 10 us  [shards(): got = lax.all_to_all(both, 'date', split_axis=0, concat_axis=0, tiled=True)]
    reshape x2 -> x6, local copies, waits for them, and re-layouts: 0.83 us -> 4.36 us  [the longest x2 1.49 us: shards(): z = got.reshape(n_date, lines_dev, cols, 2 * n_date).transpose(1, 2, 0, 3)]
    transpose x2 -> x1, other arithmetic: 2.66 us -> 0.1 us  [shards(): both = both.transpose(2, 0, 1, 3).reshape(n_date, 2 * cols * lines)]
    add x1 -> x0, other arithmetic: 2.56 us -> none  [shards(): peri_re * peri_re + peri_im * peri_im]
    all_to_all x1, waiting for transfers between devices: 4.07 us -> 6.57 us  [shards(): got = lax.all_to_all(both, 'date', split_axis=0, concat_axis=0, tiled=True)]
    unnamed x23, local copies, waits for them, and re-layouts: 3.33 us -> 5.44 us
  transfers between devices with their start and end apart: 3 -> 3, of which waited for: 3 -> 3; matrix products, arithmetic and copies ran while one was open for 16% -> 13% of each run, Pallas kernels for 0% -> 0%
where the time goes in v3:
time: 116 us
  waiting for transfers between devices  28 us (24%)
  other arithmetic  24.2 us (21%)
  starting transfers between devices  23.7 us (20%)
  local copies, waits for them, and re-layouts  20.3 us (18%)
  matrix products  14.4 us (12%)
  between operations  5.3 us (5%)
    all_to_all x1, waiting for transfers between devices, shards(): got = lax.all_to_all(pair, 'date', split_axis=0, concat_axis=0, tiled=True)  17 us
    all_to_all x1, starting transfers between devices, shards(): got = lax.all_to_all(both, 'date', split_axis=0, concat_axis=0, tiled=True)  10 us
    all_to_all x1, starting transfers between devices, shards(): lax.all_to_all(spread, 'rng', split_axis=0, concat_axis=0, tiled=True)  9 us
    convert_element_type x1, other arithmetic, dft_table(): (hi_c * lo_s + hi_s * lo_c).reshape(length, length).astype(jnp.bfloat16)  8.26 us
    all_to_all x1, waiting for transfers between devices, shards(): got = lax.all_to_all(both, 'date', split_axis=0, concat_axis=0, tiled=True)  6.57 us
    dot_general x1, matrix products, shards(): fc = jnp.dot(stacked, cos_t, preferred_element_type=f32)  5.89 us
    unnamed x23, local copies, waits for them, and re-layouts  5.44 us
    all_to_all x1, starting transfers between devices, shards(): got = lax.all_to_all(pair, 'date', split_axis=0, concat_axis=0, tiled=True)  4.7 us
  transfers between devices with their start and end apart: 3, of which 3 were waited for; matrix products, arithmetic and copies ran while one was open for 13% of the time, Pallas kernels for 0%

profile of v3, /device:TPU:1, one launch (start us, length us, event | category | flops | bytes accessed | tf_op | source)
XLA Modules:
  0.0 115.9 jit_solution(7938306581665530546)
XLA Ops:
  0.0 1.2 %copy.47 = bf16[1,2048,128]{1,2,0:T(8,128)(2,1)S(1)} copy(bf16[1,2048,128]{2,1,0:T(8,128)(2,1)} %param.13) | data formatting | bytes 1048576 | tf_op args[0]
  1.3 1.2 %copy.48 = bf16[1,2048,128]{1,2,0:T(8,128)(2,1)S(1)} copy(bf16[1,2048,128]{2,1,0:T(8,128)(2,1)} %param.14) | data formatting | bytes 1048576 | tf_op args[1]
  2.5 0.9 add_reduce_fusion
  3.4 1.2 %broadcast_in_dim.6 = f32[4,1,1]{2,1,0:T(1,128)} broadcast(f32[]{:T(128)} %add_reduce_fusion), dimensions={} | broadcast | bytes 20 | tf_op jit(solution)/shard_map/broadcast_in_dim | solution.py:62
  4.6 9.0 %all-to-all-start = ((f32[4,1,1]{2,1,0:T(1,128)}), f32[4,1,1]{2,1,0:T(1,128)S(1)}, u32[]{:S(2)}, u32[]{:S(2)}) async-start(f32[4,1,1]{2,1,0:T(1,128)} %broadcast_in_dim.6), calls=%async_computation | async-start | bytes 4096 | tf_op jit(solution)/shard_map/all_to_all | solution.py:63
  13.7 1.1 copy.49
  14.8 0.8 reshape.274
  15.7 4.4 %all-to-all-done = f32[4,1,1]{2,1,0:T(1,128)S(1)} async-done(((f32[4,1,1]{2,1,0:T(1,128)}), f32[4,1,1]{2,1,0:T(1,128)S(1)}, u32[]{:S(2)}, u32[]{:S(2)}) %all-to-all-start) | async-done | bytes 48 | tf_op jit(solution)/shard_map/all_to_all | solution.py:63
  27.6 1.5 %reduce.11 = bf16[64,8320]{1,0:T(8,128)(2,1)S(1)} reduce(bf16[64,1,8320]{2,0,1:T(8,128)(2,1)S(1)} %maximum_bitcast_fusion, bf16[]{:T(256)} %broadcast.294), dimensions={1}, to_apply=%copy.51.reduce_sub_computation | reduce | bytes 2129922 | tf_op jit(solution)/shard_map/all_to_all | solution.py:73
  29.0 1.6 %reshape.289 = bf16[64,2,4160]{2,1,0:T(2,128)(2,1)} reshape(bf16[64,8320]{1,0:T(8,128)(2,1)S(1)} %reduce.11) | data formatting | bytes 2129920
  30.6 10.0 %all-to-all-start.1 = ((bf16[64,2,4160]{2,1,0:T(2,128)(2,1)}), bf16[64,2,4160]{2,1,0:T(2,128)(2,1)S(1)}, u32[]{:S(2)}, u32[]{:S(2)}) async-start(bf16[64,2,4160]{2,1,0:T(2,128)(2,1)} %reshape.289), calls=%async_computation.1 | async-start | bytes 2162688 | tf_op jit(solution)/shard_map/all_to_all | solution.py:73
  41.3 2.0 %fusion.24 = (f32[2048,64]{0,1:T(8,128)S(1)}, f32[2048,64]{0,1:T(8,128)S(1)}) fusion(), kind=kLoop, calls=%fused_computation.50 | loop fusion | flops 1835008 | bytes 1048576 | tf_op jit(solution)/shard_map/sin | solution.py:25
  43.4 1.1 fusion.38
  44.5 8.3 %add_convert_fusion = (bf16[2048,32,64]{0,2,1:T(8,128)(2,1)}, bf16[2048,32,64]{0,2,1:T(8,128)(2,1)}) fusion(f32[2048,64]{0,1:T(8,128)S(1)} %get-tuple-element.61, f32[2048,32]{0,1:T(8,128)S(1)} %get-tuple-element.60, f32[2048,64]{0,1:T(8,128)S(1)} %get-tuple-element.62, f32[2048,32]{0,1:T(8,128)S(1)} %get-tuple-element.59), kind=kLoop, calls=%fused_computation | loop fusion | flops 33554432 | bytes 18350080 | tf_op jit(solution)/shard_map/convert_element_type | solution.py:27
  52.7 6.6 %all-to-all-done.1 = bf16[64,2,4160]{2,1,0:T(2,128)(2,1)S(1)} async-done(((bf16[64,2,4160]{2,1,0:T(2,128)(2,1)}), bf16[64,2,4160]{2,1,0:T(2,128)(2,1)S(1)}, u32[]{:S(2)}, u32[]{:S(2)}) %all-to-all-start.1) | async-done | bytes 1064992 | tf_op jit(solution)/shard_map/all_to_all | solution.py:73
  59.3 1.2 %reshape.290 = bf16[64,1,8320]{2,1,0:T(2,128)(2,1)S(1)} reshape(bf16[64,2,4160]{2,1,0:T(2,128)(2,1)S(1)} %all-to-all-done.1) | data formatting | bytes 2129920
  60.9 1.0 reshape.278
  64.7 0.7 tile.21
  65.9 0.7 tile.9
  66.9 1.8 %add_convert_fusion.1 = (bf16[128,2048]{1,0:T(8,128)(2,1)S(1)}, bf16[128,2048]{1,0:T(8,128)(2,1)S(1)}) fusion(f32[128,2048]{1,0:T(8,128)S(1)} %tile.21, bf16[128,2048]{1,0:T(8,128)(2,1)} %copy-done.1, f32[128,2048]{1,0:T(8,128)S(1)} %tile.9, bf16[128,2048]{1,0:T(8,128)(2,1)} %copy-done, f32[128]{0:T(128)S(1)} %mul.288), kind=kLoop, calls=%fused_computation.27 | loop fusion | flops 3145728 | bytes 4194816 | tf_op jit(solution)/shard_map/convert_element_type | solution.py:90
  68.7 5.9 %fusion.14 = f32[256,2048]{1,0:T(8,128)S(1)} fusion(bf16[2048,2048]{0,1:T(8,128)(2,1)} %bitcast.52, bf16[128,2048]{1,0:T(8,128)(2,1)S(1)} %get-tuple-element.52, bf16[128,2048]{1,0:T(8,128)(2,1)S(1)} %get-tuple-element.51), kind=kOutput, calls=%fused_computation.37 | convolution fusion | flops 2149580800 | bytes 11534336 | tf_op jit(solution)/shard_map/dot_general | solution.py:96
  74.7 2.4 %fusion.13 = f32[256,2048]{1,0:T(8,128)S(1)} fusion(bf16[2048,2048]{0,1:T(8,128)(2,1)S(1)} %bitcast.50, bf16[128,2048]{1,0:T(8,128)(2,1)S(1)} %get-tuple-element.52, bf16[128,2048]{1,0:T(8,128)(2,1)S(1)} %get-tuple-element.51), kind=kOutput, calls=%fused_computation.36 | convolution fusion | flops 2149580800 | bytes 11534336 | tf_op jit(solution)/shard_map/dot_general | solution.py:97
  77.5 2.4 %fusion.12 = f32[256,2048]{1,0:T(8,128)S(1)} fusion(bf16[2048,2048]{0,1:T(8,128)(2,1)S(1)} %bitcast.55, bf16[128,2048]{1,0:T(8,128)(2,1)S(1)} %get-tuple-element.48, bf16[128,2048]{1,0:T(8,128)(2,1)S(1)} %get-tuple-element.47), kind=kOutput, calls=%fused_computation.35 | convolution fusion | flops 2149580800 | bytes 11534336 | tf_op jit(solution)/shard_map/dot_general | solution.py:105
  79.8 2.6 %fusion.11 = f32[256,2048]{1,0:T(8,128)S(1)} fusion(bf16[2048,2048]{0,1:T(8,128)(2,1)S(1)} %bitcast.51, bf16[128,2048]{1,0:T(8,128)(2,1)S(1)} %get-tuple-element.48, bf16[128,2048]{1,0:T(8,128)(2,1)S(1)} %get-tuple-element.47), kind=kOutput, calls=%fused_computation.34 | convolution fusion | flops 2149580800 | bytes 11534336 | tf_op jit(solution)/shard_map/dot_general | solution.py:106
  84.0 1.3 %copy.53 = bf16[2048,256]{1,0:T(8,128)(2,1)} copy(bf16[2048,256]{0,1:T(8,128)(2,1)S(1)} %bitcast.61) | data formatting | bytes 2097152 | tf_op jit(solution)/shard_map/transpose | solution.py:111
  85.3 4.7 %all-to-all-start.2 = ((bf16[64,32,256]{2,1,0:T(8,128)(2,1)}), bf16[64,32,256]{2,1,0:T(8,128)(2,1)S(1)}, u32[]{:S(2)}, u32[]{:S(2)}) async-start(bf16[64,32,256]{2,1,0:T(8,128)(2,1)} %bitcast.18), calls=%async_computation.2 | async-start | bytes 2097152 | tf_op jit(solution)/shard_map/all_to_all | solution.py:112
  90.0 0.7 convert_bitcast_fusion
  91.5 17.0 %all-to-all-done.2 = bf16[64,32,256]{2,1,0:T(8,128)(2,1)S(1)} async-done(((bf16[64,32,256]{2,1,0:T(8,128)(2,1)}), bf16[64,32,256]{2,1,0:T(8,128)(2,1)S(1)}, u32[]{:S(2)}, u32[]{:S(2)}) %all-to-all-start.2) | async-done | bytes 1048608 | tf_op jit(solution)/shard_map/all_to_all | solution.py:112
  108.7 1.2 %copy.54 = bf16[64,32,2,128]{3,0,2,1:T(8,128)(2,1)S(1)} copy(bf16[64,32,2,128]{3,2,1,0:T(2,128)(2,1)S(1)} %reshape.281) | data formatting | bytes 2097152 | tf_op jit(solution)/shard_map/reshape | solution.py:113
  109.9 0.9 multiply_reduce_fusion
  111.0 1.2 %fusion.29 = f32[4096,512]{1,0:T(8,128)S(1)} fusion(bf16[4096,128]{1,0:T(8,128)(2,1)S(1)} %bitcast.56, bf16[64,256]{1,0:T(8,128)(2,1)S(1)} %get-tuple-element.58, bf16[64,256]{1,0:T(8,128)(2,1)S(1)} %get-tuple-element.57, bf16[64,256]{1,0:T(8,128)(2,1)S(1)} %fusion.52), kind=kOutput, calls=%fused_computation.55 | convolution fusion | flops 537395200 | bytes 9535488 | tf_op jit(solution)/shard_map/dot_general | solution.py:118
  112.2 3.7 %fusion.2 = f32[4096,256]{1,0:T(8,128)} fusion(f32[4096,512]{1,0:T(8,128)S(1)} %fusion.29, f32[4096]{0:T(1024)S(1)} %convert_bitcast_fusion, f32[4096]{0:T(1024)S(1)} %mul.337), kind=kLoop, calls=%fused_computation.5 | loop fusion | flops 5242880 | bytes 12615680 | tf_op jit(solution)/shard_map/mul | solution.py:128
  (54 shorter events, 10.2 us)
Async XLA Ops:
  4.6 15.5 %all-to-all-start = ((f32[4,1,1]{2,1,0:T(1,128)}), f32[4,1,1]{2,1,0:T(1,128)S(1)}, u32[]{:S(2)}, u32[]{:S(2)}) async-start(f32[4,1,1]{2,1,0:T(1,128)} %broadcast_in_dim.6), calls=%async_computation | async-start | bytes 4096 | tf_op jit(solution)/shard_map/all_to_all | solution.py:63
  30.6 28.7 %all-to-all-start.1 = ((bf16[64,2,4160]{2,1,0:T(2,128)(2,1)}), bf16[64,2,4160]{2,1,0:T(2,128)(2,1)S(1)}, u32[]{:S(2)}, u32[]{:S(2)}) async-start(bf16[64,2,4160]{2,1,0:T(2,128)(2,1)} %reshape.289), calls=%async_computation.1 | async-start | bytes 2162688 | tf_op jit(solution)/shard_map/all_to_all | solution.py:73
  62.8 1.3 %copy-start = (bf16[128,2048]{1,0:T(8,128)(2,1)}, bf16[128,2048]{1,0:T(8,128)(2,1)S(1)}, u32[]{:S(2)}) copy-start(bf16[128,2048]{1,0:T(8,128)(2,1)S(1)} %reshape_squeeze.6) | copy-start | bytes 1572868
  63.0 1.1 copy-start.1
  66.8 7.8 %slice-start = ((s8[8388608]{0:T(1024)(128)(4,1)}), s8[4194304]{0:T(1024)(128)(4,1)S(1)}, s32[]{:S(2)}) async-start(s8[8388608]{0:T(1024)(128)(4,1)} %bitcast.48), calls=%async_computation.3 | async-start | bytes 8388608
  68.7 5.9 %slice-start.1 = ((s8[8388608]{0:T(1024)(128)(4,1)}), s8[4194304]{0:T(1024)(128)(4,1)S(1)}, s32[]{:S(2)}) async-start(s8[8388608]{0:T(1024)(128)(4,1)} %bitcast.48), calls=%async_computation.4 | async-start | bytes 8388608
  68.7 8.7 %slice-start.2 = ((s8[8388608]{0:T(1024)(128)(4,1)}), s8[4194304]{0:T(1024)(128)(4,1)S(1)}, s32[]{:S(2)}) async-start(s8[8388608]{0:T(1024)(128)(4,1)} %bitcast.53), calls=%async_computation.5 | async-start | bytes 8388608
  74.6 2.4 %copy-start.2 = (f32[2048]{0:T(1024)S(1)}, f32[2048]{0:T(1024)}, u32[]{:S(2)}) copy-start(f32[2048]{0:T(1024)} %param.16) | copy-start | bytes 24580
  74.6 2.8 %slice-start.3 = ((s8[8388608]{0:T(1024)(128)(4,1)}), s8[4194304]{0:T(1024)(128)(4,1)S(1)}, s32[]{:S(2)}) async-start(s8[8388608]{0:T(1024)(128)(4,1)} %bitcast.53), calls=%async_computation.6 | async-start | bytes 8388608
  84.0 6.8 %copy-start.3 = (s32[64]{0:T(128)S(1)}, s32[64]{0:T(128)}, u32[]{:S(2)}) copy-start(s32[64]{0:T(128)} %param.18) | copy-start | bytes 772
  84.0 6.8 %copy-start.4 = (s32[64]{0:T(128)S(1)}, s32[64]{0:T(128)}, u32[]{:S(2)}) copy-start(s32[64]{0:T(128)} %param.17) | copy-start | bytes 772
  85.3 23.1 %all-to-all-start.2 = ((bf16[64,32,256]{2,1,0:T(8,128)(2,1)}), bf16[64,32,256]{2,1,0:T(8,128)(2,1)S(1)}, u32[]{:S(2)}, u32[]{:S(2)}) async-start(bf16[64,32,256]{2,1,0:T(8,128)(2,1)} %bitcast.18), calls=%async_computation.2 | async-start | bytes 2097152 | tf_op jit(solution)/shard_map/all_to_all | solution.py:112

commit v4 on v3

--- a/solution.py
+++ b/solution.py
@@ -59,39 +59,37 @@
     wide_re = own_re.astype(f32)
     wide_im = own_im.astype(f32)
     local = jnp.sum(wide_re * wide_re + wide_im * wide_im)
-    spread = jnp.broadcast_to(local, (n_rng, 1))
-    own_sum = jnp.sum(lax.all_to_all(spread, "rng", split_axis=0, concat_axis=0, tiled=True))
-    hi = lax.reduce_precision(own_sum, exponent_bits=8, mantissa_bits=7)
-    mid = lax.reduce_precision(own_sum - hi, exponent_bits=8, mantissa_bits=7)
-    lo = lax.reduce_precision(own_sum - hi - mid, exponent_bits=8, mantissa_bits=7)
-    words = jnp.zeros((128,), f32).at[0].set(hi).at[1].set(mid).at[2].set(lo)
-    words = jnp.broadcast_to(words.astype(jnp.bfloat16), (n_date, 128))
+    lane = jnp.arange(lines)
+    word = jnp.full((lines,), local)
+    hi = lax.reduce_precision(word, exponent_bits=8, mantissa_bits=7)
+    mid = lax.reduce_precision(word - hi, exponent_bits=8, mantissa_bits=7)
+    lo = lax.reduce_precision(word - hi - mid, exponent_bits=8, mantissa_bits=7)
+    word = jnp.where(lane == 0, hi, jnp.where(lane == 1, mid, jnp.where(lane == 2, lo, 0.0)))
+    word = jnp.broadcast_to(word.astype(jnp.bfloat16), (n_date, 1, lines))
 
     both = jnp.stack([own_re.T, own_im.T]).reshape(2, cols, n_date, lines)
-    both = both.transpose(2, 0, 1, 3).reshape(n_date, 2 * cols * lines)
-    both = jnp.concatenate([both, words], axis=1)
+    both = both.transpose(2, 0, 1, 3).reshape(n_date, 2 * cols, lines)
+    both = jnp.concatenate([both, word], axis=1)
     got = lax.all_to_all(both, "date", split_axis=0, concat_axis=0, tiled=True)
-    sums = got[:, 2 * cols * lines:2 * cols * lines + 3].astype(f32)
-    date_sums = (sums[:, 0] + sums[:, 1]) + sums[:, 2]
+    sums = got[:, 2 * cols, :3].astype(f32)
+    part = (sums[:, 0] + sums[:, 1]) + sums[:, 2]
+    spread = jnp.broadcast_to(part, (n_rng, n_date))
+    date_sums = jnp.sum(
+        lax.all_to_all(spread, "rng", split_axis=0, concat_axis=0, tiled=True), axis=0
+    )
     scales = lax.rsqrt(date_sums / pixel_total + 1e-06)
-    got = got[:, :2 * cols * lines].reshape(n_date, 2, cols, lines)
-    x_re = got[:, 0].reshape(n_date * cols, lines)
-    x_im = got[:, 1].reshape(n_date * cols, lines)
+    rows = n_date * cols
+    x_re = got[:, :cols].reshape(rows, lines).astype(f32)
+    x_im = got[:, cols:2 * cols].reshape(rows, lines).astype(f32)
 
     ref_index = ref_date[0]
-    ref_scale = scales[ref_index]
-    ref_re = lax.dynamic_slice_in_dim(x_re, ref_index * cols, cols, 0).astype(f32) * ref_scale
-    ref_im = lax.dynamic_slice_in_dim(x_im, ref_index * cols, cols, 0).astype(f32) * ref_scale
-    ref_re = jnp.tile(ref_re, (n_date, 1))
-    ref_im = jnp.tile(ref_im, (n_date, 1))
-    row_scale = jnp.repeat(scales, cols)[:, None]
-    a_re = x_re.astype(f32) * row_scale
-    a_im = x_im.astype(f32) * row_scale
-    ifg_re = (a_re * ref_re + a_im * ref_im).astype(jnp.bfloat16)
-    ifg_im = (a_im * ref_re - a_re * ref_im).astype(jnp.bfloat16)
+    ref_re = jnp.tile(lax.dynamic_slice_in_dim(x_re, ref_index * cols, cols, 0), (n_date, 1))
+    ref_im = jnp.tile(lax.dynamic_slice_in_dim(x_im, ref_index * cols, cols, 0), (n_date, 1))
+    ifg_re = (x_re * ref_re + x_im * ref_im).astype(jnp.bfloat16)
+    ifg_im = (x_im * ref_re - x_re * ref_im).astype(jnp.bfloat16)
+    row_scale = (jnp.repeat(scales, cols) * scales[ref_index])[:, None] * (1.0 / lines)
 
     cos_t, sin_t = dft_table(lines)
-    rows = n_date * cols
     stacked = jnp.concatenate([ifg_re, ifg_im], axis=0)
     fc = jnp.dot(stacked, cos_t, preferred_element_type=f32)
     fs = jnp.dot(stacked, sin_t, preferred_element_type=f32)
@@ -104,8 +102,8 @@
     )
     bc = jnp.dot(held, cos_t, preferred_element_type=f32)
     bs = jnp.dot(held, sin_t, preferred_element_type=f32)
-    filt_re = ((bc[:rows] - bs[rows:]) * (1.0 / lines)).astype(jnp.bfloat16)
-    filt_im = ((bs[:rows] + bc[rows:]) * (1.0 / lines)).astype(jnp.bfloat16)
+    filt_re = ((bc[:rows] - bs[rows:]) * row_scale).astype(jnp.bfloat16)
+    filt_im = ((bs[:rows] + bc[rows:]) * row_scale).astype(jnp.bfloat16)
 
     pair = jnp.concatenate([filt_re, filt_im], axis=0).reshape(2, n_date, cols, lines)
     pair = pair.transpose(2, 0, 1, 3).reshape(2 * rows, lines).T

time: 116 us -> 129 us (1.11)
  waiting for transfers between devices: 28 us -> 34.2 us
  other arithmetic: 24.2 us -> 29.9 us
  matrix products: 14.4 us -> 15.8 us
    all_to_all x1, waiting for transfers between devices: 6.57 us -> 17.3 us  [shards(): got = lax.all_to_all(both, 'date', split_axis=0, concat_axis=0, tiled=True)]
    convert_element_type x4 -> x5, other arithmetic: 2.23 us -> 7.85 us  [the longest x1 2.14 us: shards(): x_im = got[:, cols:2 * cols].reshape(rows, lines).astype(f32)]
    another operation x6 -> x4, local copies, waits for them, and re-layouts: 2.84 us -> 7.82 us  [the longest x2 4.4 us: shards(): jnp.tile(lax.dynamic_slice_in_dim(x_re, ref_index * cols, cols, 0), (n_da...]
    all_to_all x1, waiting for transfers between devices: 4.44 us -> 0.01 us  [shards(): lax.all_to_all(spread, 'rng', split_axis=0, concat_axis=0, tiled=True)]
    convert_element_type x0 -> x2, local copies, waits for them, and re-layouts: none -> 2.66 us  [the longest x1 1.94 us: shards(): x_im = got[:, cols:2 * cols].reshape(rows, lines).astype(f32)]
    concatenate x0 -> x1, other arithmetic: none -> 2.36 us  [shards(): both = jnp.concatenate([both, word], axis=1)]
    unnamed x23 -> x16, local copies, waits for them, and re-layouts: 5.44 us -> 3.3 us
    scatter x3 -> x0, local copies, waits for them, and re-layouts: 1.93 us -> none  [shards(): words = jnp.zeros((128,), f32).at[0].set(hi).at[1].set(mid).at[2].set(lo)]
  transfers between devices with their start and end apart: 3 -> 3, of which waited for: 3 -> 2; matrix products, arithmetic and copies ran while one was open for 13% -> 30% of each run, Pallas kernels for 0% -> 0%
where the time goes in v4:
time: 129 us; the launch traced here: 128 us
  waiting for transfers between devices  34.2 us (27%)
  other arithmetic  29.9 us (23%)
  starting transfers between devices  23.1 us (18%)
  local copies, waits for them, and re-layouts  20.3 us (16%)
  matrix products  15.8 us (12%)
  between operations  5.14 us (4%)
    all_to_all x1, waiting for transfers between devices, shards(): got = lax.all_to_all(both, 'date', split_axis=0, concat_axis=0, tiled=True)  17.3 us
    all_to_all x1, waiting for transfers between devices, shards(): got = lax.all_to_all(pair, 'date', split_axis=0, concat_axis=0, tiled=True)  16.9 us
    all_to_all x1, starting transfers between devices, shards(): got = lax.all_to_all(both, 'date', split_axis=0, concat_axis=0, tiled=True)  10.3 us
    convert_element_type x1, other arithmetic, dft_table(): (hi_c * lo_s + hi_s * lo_c).reshape(length, length).astype(jnp.bfloat16)  8.26 us
    all_to_all x1, starting transfers between devices, shards(): lax.all_to_all(spread, 'rng', split_axis=0, concat_axis=0, tiled=True)  7.28 us
    dot_general x1, matrix products, shards(): fc = jnp.dot(stacked, cos_t, preferred_element_type=f32)  5.9 us
    all_to_all x1, starting transfers between devices, shards(): got = lax.all_to_all(pair, 'date', split_axis=0, concat_axis=0, tiled=True)  5.45 us
    another operation x2, local copies, waits for them, and re-layouts, shards(): jnp.tile(lax.dynamic_slice_in_dim(x_re, ref_index * cols, cols, 0), (n_da...  4.4 us
  transfers between devices with their start and end apart: 3, of which 2 were waited for; matrix products, arithmetic and copies ran while one was open for 30% of the time, Pallas kernels for 0%

profile of v4, /device:TPU:1, one launch (start us, length us, event | category | flops | bytes accessed | tf_op | source)
XLA Modules:
  0.0 128.4 jit_solution(3405321500603794245)
XLA Ops:
  0.0 1.2 copy.35
  1.3 1.2 copy.36
  2.5 0.9 add_reduce_fusion
  7.7 0.8 copy.37
  8.5 1.9 %select_convert_fusion = bf16[2048]{0:T(1024)(128)(2,1)S(1)} fusion(bf16[]{:T(256)} %reduce_precision.14, f32[]{:T(128)} %reduce_precision.13, f32[]{:T(128)} %reduce_precision.12), kind=kLoop, calls=%fused_computation.78 | loop fusion | flops 12288 | bytes 4106 | tf_op jit(solution)/shard_map/convert_element_type | solution.py:68
  10.7 2.4 %pad_maximum_fusion = bf16[64,5,2048]{2,1,0:T(8,128)(2,1)} fusion(bf16[64,1,2048]{2,1,0:T(2,128)(2,1)S(1)} %broadcast_in_dim.20, bf16[64,4,2048]{2,1,0:T(4,128)(2,1)S(1)} %copy.37), kind=kLoop, calls=%fused_computation.7 | loop fusion | flops 2621440 | bytes 2621440 | tf_op jit(solution)/shard_map/concatenate | solution.py:72
  13.0 10.3 %all-to-all-start = ((bf16[64,5,2048]{2,1,0:T(8,128)(2,1)}), bf16[64,5,2048]{2,1,0:T(8,128)(2,1)S(1)}, u32[]{:S(2)}, u32[]{:S(2)}) async-start(bf16[64,5,2048]{2,1,0:T(8,128)(2,1)} %pad_maximum_fusion), calls=%async_computation | async-start | bytes 4194304 | tf_op jit(solution)/shard_map/all_to_all | solution.py:73
  24.0 2.0 %fusion.24 = (f32[2048,64]{0,1:T(8,128)S(1)}, f32[2048,64]{0,1:T(8,128)S(1)}) fusion(), kind=kLoop, calls=%fused_computation.49 | loop fusion | flops 1835008 | bytes 1048576 | tf_op jit(solution)/shard_map/sin | solution.py:25
  26.1 1.1 fusion.38
  27.2 8.3 %add_convert_fusion = (bf16[2048,32,64]{0,2,1:T(8,128)(2,1)}, bf16[2048,32,64]{0,2,1:T(8,128)(2,1)}) fusion(f32[2048,64]{0,1:T(8,128)S(1)} %get-tuple-element.23, f32[2048,32]{0,1:T(8,128)S(1)} %get-tuple-element.22, f32[2048,64]{0,1:T(8,128)S(1)} %get-tuple-element.24, f32[2048,32]{0,1:T(8,128)S(1)} %get-tuple-element.21), kind=kLoop, calls=%fused_computation | loop fusion | flops 33554432 | bytes 18350080 | tf_op jit(solution)/shard_map/convert_element_type | solution.py:27
  35.4 17.3 %all-to-all-done = bf16[64,5,2048]{2,1,0:T(8,128)(2,1)S(1)} async-done(((bf16[64,5,2048]{2,1,0:T(8,128)(2,1)}), bf16[64,5,2048]{2,1,0:T(8,128)(2,1)S(1)}, u32[]{:S(2)}, u32[]{:S(2)}) %all-to-all-start) | async-done | bytes 1310752 | tf_op jit(solution)/shard_map/all_to_all | solution.py:73
  53.0 2.1 %slice_convert_fusion = (f32[64,2,2048]{2,1,0:T(2,128)}, f32[64,2,2048]{2,1,0:T(2,128)S(1)}) fusion(bf16[64,5,2048]{2,1,0:T(8,128)(2,1)S(1)} %all-to-all-done), kind=kLoop, calls=%fused_computation.38 | loop fusion | flops 524288 | bytes 3145728 | tf_op jit(solution)/shard_map/convert_element_type | solution.py:83
  55.1 1.9 %reshape.222 = f32[128,2048]{1,0:T(8,128)S(1)} reshape(f32[64,2,2048]{2,1,0:T(2,128)} %get-tuple-element.15) | data formatting | bytes 2097152 | tf_op jit(solution)/shard_map/convert_element_type | solution.py:83
  57.7 7.3 %all-to-all-start.1 = ((f32[4,1,64]{2,1,0:T(1,128)}), f32[4,1,64]{2,1,0:T(1,128)S(1)}, u32[]{:S(2)}, u32[]{:S(2)}) async-start(f32[4,1,64]{2,1,0:T(1,128)} %broadcast_in_dim.40), calls=%async_computation.1 | async-start | bytes 4096 | tf_op jit(solution)/shard_map/all_to_all | solution.py:78
  65.7 1.5 %tile.20 = f32[64,2,2048]{2,1,0:T(2,128)} broadcast(f32[2,2048]{1,0:T(2,128)S(1)} %get-tuple-element.27), dimensions={1,2} | broadcast | bytes 1064960 | tf_op jit(solution)/shard_map/tile | solution.py:87
  67.2 1.9 %tile.21 = f32[128,2048]{1,0:T(8,128)S(1)} reshape(f32[64,2,2048]{2,1,0:T(2,128)} %tile.20) | data formatting | bytes 2097152 | tf_op jit(solution)/shard_map/tile | solution.py:87
  69.1 1.5 %tile.8 = f32[64,2,2048]{2,1,0:T(2,128)} broadcast(f32[2,2048]{1,0:T(2,128)S(1)} %get-tuple-element.28), dimensions={1,2} | broadcast | bytes 1064960 | tf_op jit(solution)/shard_map/tile | solution.py:86
  70.6 2.9 %tile.9 = f32[128,2048]{1,0:T(8,128)} reshape(f32[64,2,2048]{2,1,0:T(2,128)} %tile.8) | data formatting | bytes 2097152 | tf_op jit(solution)/shard_map/tile | solution.py:86
  73.5 1.8 %add_convert_fusion.1 = (bf16[128,2048]{1,0:T(8,128)(2,1)S(1)}, bf16[128,2048]{1,0:T(8,128)(2,1)S(1)}) fusion(f32[128,2048]{1,0:T(8,128)S(1)} %reshape.222, f32[128,2048]{1,0:T(8,128)S(1)} %tile.21, f32[128,2048]{1,0:T(8,128)S(1)} %reshape.221, f32[128,2048]{1,0:T(8,128)} %tile.9), kind=kLoop, calls=%fused_computation.26 | loop fusion | flops 2097152 | bytes 5242880 | tf_op jit(solution)/shard_map/convert_element_type | solution.py:88
  75.3 5.9 %fusion.14 = f32[256,2048]{1,0:T(8,128)S(1)} fusion(bf16[2048,2048]{0,1:T(8,128)(2,1)} %bitcast.43, bf16[128,2048]{1,0:T(8,128)(2,1)S(1)} %get-tuple-element.14, bf16[128,2048]{1,0:T(8,128)(2,1)S(1)} %get-tuple-element.13), kind=kOutput, calls=%fused_computation.34 | convolution fusion | flops 2149580800 | bytes 11534336 | tf_op jit(solution)/shard_map/dot_general | solution.py:94
  81.3 2.4 %fusion.13 = f32[256,2048]{1,0:T(8,128)S(1)} fusion(bf16[2048,2048]{0,1:T(8,128)(2,1)S(1)} %bitcast.49, bf16[128,2048]{1,0:T(8,128)(2,1)S(1)} %get-tuple-element.14, bf16[128,2048]{1,0:T(8,128)(2,1)S(1)} %get-tuple-element.13), kind=kOutput, calls=%fused_computation.33 | convolution fusion | flops 2149580800 | bytes 11534336 | tf_op jit(solution)/shard_map/dot_general | solution.py:95
  84.1 2.4 %fusion.11 = f32[256,2048]{1,0:T(8,128)S(1)} fusion(bf16[2048,2048]{0,1:T(8,128)(2,1)S(1)} %bitcast.50, bf16[128,2048]{1,0:T(8,128)(2,1)S(1)} %get-tuple-element.10, bf16[128,2048]{1,0:T(8,128)(2,1)S(1)} %get-tuple-element.9), kind=kOutput, calls=%fused_computation.31 | convolution fusion | flops 2149580800 | bytes 11534336 | tf_op jit(solution)/shard_map/dot_general | solution.py:104
  86.4 0.8 slice-done.1
  87.2 3.9 %fusion.12 = f32[256,2048]{1,0:T(8,128)} fusion(bf16[2048,2048]{0,1:T(8,128)(2,1)S(1)} %bitcast.46, bf16[128,2048]{1,0:T(8,128)(2,1)S(1)} %get-tuple-element.10, bf16[128,2048]{1,0:T(8,128)(2,1)S(1)} %get-tuple-element.9), kind=kOutput, calls=%fused_computation.32 | convolution fusion | flops 2149580800 | bytes 11534336 | tf_op jit(solution)/shard_map/dot_general | solution.py:103
  92.7 2.0 %fusion.6 = (bf16[128,2048]{1,0:T(8,128)(2,1)S(1)}, bf16[128,2048]{1,0:T(8,128)(2,1)S(1)}) fusion(f32[256,2048]{1,0:T(8,128)S(1)} %fusion.11, f32[256,2048]{1,0:T(8,128)} %fusion.12, f32[128]{0:T(128)S(1)} %mul.329), kind=kLoop, calls=%fused_computation.14 | loop fusion | flops 1572864 | bytes 5243392 | tf_op jit(solution)/shard_map/convert_element_type | solution.py:105
  95.8 1.3 %copy.40 = bf16[2048,256]{1,0:T(8,128)(2,1)} copy(bf16[2048,256]{0,1:T(8,128)(2,1)S(1)} %bitcast.55) | data formatting | bytes 2097152 | tf_op jit(solution)/shard_map/transpose | solution.py:109
  97.1 5.4 %all-to-all-start.2 = ((bf16[64,32,256]{2,1,0:T(8,128)(2,1)}), bf16[64,32,256]{2,1,0:T(8,128)(2,1)S(1)}, u32[]{:S(2)}, u32[]{:S(2)}) async-start(bf16[64,32,256]{2,1,0:T(8,128)(2,1)} %bitcast.17), calls=%async_computation.2 | async-start | bytes 2097152 | tf_op jit(solution)/shard_map/all_to_all | solution.py:110
  104.0 16.9 %all-to-all-done.2 = bf16[64,32,256]{2,1,0:T(8,128)(2,1)S(1)} async-done(((bf16[64,32,256]{2,1,0:T(8,128)(2,1)}), bf16[64,32,256]{2,1,0:T(8,128)(2,1)S(1)}, u32[]{:S(2)}, u32[]{:S(2)}) %all-to-all-start.2) | async-done | bytes 1048608 | tf_op jit(solution)/shard_map/all_to_all | solution.py:110
  121.2 0.9 multiply_reduce_fusion
  122.1 1.2 copy.41
  123.4 1.2 fusion.29
  124.7 3.7 %fusion.2 = f32[4096,256]{1,0:T(8,128)} fusion(f32[4096,512]{1,0:T(8,128)S(1)} %fusion.29, f32[4096]{0:T(1024)S(1)} %convert_bitcast_fusion, f32[4096]{0:T(1024)S(1)} %mul.345), kind=kLoop, calls=%fused_computation.5 | loop fusion | flops 5242880 | bytes 12615680 | tf_op jit(solution)/shard_map/mul | solution.py:126
  (41 shorter events, 6.8 us)
Async XLA Ops:
  13.0 39.8 %all-to-all-start = ((bf16[64,5,2048]{2,1,0:T(8,128)(2,1)}), bf16[64,5,2048]{2,1,0:T(8,128)(2,1)S(1)}, u32[]{:S(2)}, u32[]{:S(2)}) async-start(bf16[64,5,2048]{2,1,0:T(8,128)(2,1)} %pad_maximum_fusion), calls=%async_computation | async-start | bytes 4194304 | tf_op jit(solution)/shard_map/all_to_all | solution.py:73
  57.7 33.5 %all-to-all-start.1 = ((f32[4,1,64]{2,1,0:T(1,128)}), f32[4,1,64]{2,1,0:T(1,128)S(1)}, u32[]{:S(2)}, u32[]{:S(2)}) async-start(f32[4,1,64]{2,1,0:T(1,128)} %broadcast_in_dim.40), calls=%async_computation.1 | async-start | bytes 4096 | tf_op jit(solution)/shard_map/all_to_all | solution.py:78
  73.5 7.7 %slice-start.2 = ((s8[8388608]{0:T(1024)(128)(4,1)}), s8[4194304]{0:T(1024)(128)(4,1)S(1)}, s32[]{:S(2)}) async-start(s8[8388608]{0:T(1024)(128)(4,1)} %bitcast.47), calls=%async_computation.5 | async-start | bytes 8388608
  75.3 5.9 %slice-start.3 = ((s8[8388608]{0:T(1024)(128)(4,1)}), s8[4194304]{0:T(1024)(128)(4,1)S(1)}, s32[]{:S(2)}) async-start(s8[8388608]{0:T(1024)(128)(4,1)} %bitcast.47), calls=%async_computation.6 | async-start | bytes 8388608
  81.3 2.4 %copy-start = (f32[2048]{0:T(1024)S(1)}, f32[2048]{0:T(1024)}, u32[]{:S(2)}) copy-start(f32[2048]{0:T(1024)} %param.10) | copy-start | bytes 24580
  83.6 2.8 %slice-start = ((s8[8388608]{0:T(1024)(128)(4,1)}), s8[4194304]{0:T(1024)(128)(4,1)S(1)}, s32[]{:S(2)}) async-start(s8[8388608]{0:T(1024)(128)(4,1)} %bitcast.44), calls=%async_computation.3 | async-start | bytes 8388608
  84.0 3.2 %slice-start.1 = ((s8[8388608]{0:T(1024)(128)(4,1)}), s8[4194304]{0:T(1024)(128)(4,1)S(1)}, s32[]{:S(2)}) async-start(s8[8388608]{0:T(1024)(128)(4,1)} %bitcast.44), calls=%async_computation.4 | async-start | bytes 8388608
  94.7 8.6 %copy-start.1 = (s32[64]{0:T(128)S(1)}, s32[64]{0:T(128)}, u32[]{:S(2)}) copy-start(s32[64]{0:T(128)} %param.12) | copy-start | bytes 772
  94.7 8.6 %copy-start.2 = (s32[64]{0:T(128)S(1)}, s32[64]{0:T(128)}, u32[]{:S(2)}) copy-start(s32[64]{0:T(128)} %param.11) | copy-start | bytes 772
  97.1 23.8 %all-to-all-start.2 = ((bf16[64,32,256]{2,1,0:T(8,128)(2,1)}), bf16[64,32,256]{2,1,0:T(8,128)(2,1)S(1)}, u32[]{:S(2)}, u32[]{:S(2)}) async-start(bf16[64,32,256]{2,1,0:T(8,128)(2,1)} %bitcast.17), calls=%async_computation.2 | async-start | bytes 2097152 | tf_op jit(solution)/shard_map/all_to_all | solution.py:110

commit v5 on v3

--- a/solution.py
+++ b/solution.py
@@ -59,22 +59,28 @@
     wide_re = own_re.astype(f32)
     wide_im = own_im.astype(f32)
     local = jnp.sum(wide_re * wide_re + wide_im * wide_im)
-    spread = jnp.broadcast_to(local, (n_rng, 1))
-    own_sum = jnp.sum(lax.all_to_all(spread, "rng", split_axis=0, concat_axis=0, tiled=True))
-    hi = lax.reduce_precision(own_sum, exponent_bits=8, mantissa_bits=7)
-    mid = lax.reduce_precision(own_sum - hi, exponent_bits=8, mantissa_bits=7)
-    lo = lax.reduce_precision(own_sum - hi - mid, exponent_bits=8, mantissa_bits=7)
-    words = jnp.zeros((128,), f32).at[0].set(hi).at[1].set(mid).at[2].set(lo)
-    words = jnp.broadcast_to(words.astype(jnp.bfloat16), (n_date, 128))
+    own_sum = local
+    shift = 1
+    while shift < n_rng:
+        pairs = [(r, r ^ shift) for r in range(n_rng)]
+        own_sum = own_sum + lax.ppermute(own_sum, "rng", pairs)
+        shift *= 2
+    lane = jnp.arange(128)
+    word = jnp.full((128,), own_sum)
+    hi = lax.reduce_precision(word, exponent_bits=8, mantissa_bits=7)
+    mid = lax.reduce_precision(word - hi, exponent_bits=8, mantissa_bits=7)
+    lo = lax.reduce_precision(word - hi - mid, exponent_bits=8, mantissa_bits=7)
+    word = jnp.where(lane == 0, hi, jnp.where(lane == 1, mid, jnp.where(lane == 2, lo, 0.0)))
+    word = jnp.broadcast_to(word.astype(jnp.bfloat16), (n_date, 2 * cols, 128))
 
     both = jnp.stack([own_re.T, own_im.T]).reshape(2, cols, n_date, lines)
-    both = both.transpose(2, 0, 1, 3).reshape(n_date, 2 * cols * lines)
-    both = jnp.concatenate([both, words], axis=1)
+    both = both.transpose(2, 0, 1, 3).reshape(n_date, 2 * cols, lines)
+    both = jnp.concatenate([both, word], axis=2)
     got = lax.all_to_all(both, "date", split_axis=0, concat_axis=0, tiled=True)
-    sums = got[:, 2 * cols * lines:2 * cols * lines + 3].astype(f32)
+    sums = got[:, 0, lines:lines + 3].astype(f32)
     date_sums = (sums[:, 0] + sums[:, 1]) + sums[:, 2]
     scales = lax.rsqrt(date_sums / pixel_total + 1e-06)
-    got = got[:, :2 * cols * lines].reshape(n_date, 2, cols, lines)
+    got = got[:, :, :lines].reshape(n_date, 2, cols, lines)
     x_re = got[:, 0].reshape(n_date * cols, lines)
     x_im = got[:, 1].reshape(n_date * cols, lines)
 

time: 116 us -> 110 us (0.948)
  local copies, waits for them, and re-layouts: 20.3 us -> 13.3 us
  waiting for transfers between devices: 28 us -> 24.2 us
  starting transfers between devices: 23.7 us -> 26.5 us
  other arithmetic: 24.2 us -> 25.5 us
    ppermute x0 -> x2, starting transfers between devices: none -> 10.9 us  [shards(): own_sum = own_sum + lax.ppermute(own_sum, 'rng', pairs)]
    all_to_all x1 -> x0, starting transfers between devices: 9 us -> none  [shards(): lax.all_to_all(spread, 'rng', split_axis=0, concat_axis=0, tiled=True)]
    all_to_all x1 -> x0, waiting for transfers between devices: 4.44 us -> none  [shards(): lax.all_to_all(spread, 'rng', split_axis=0, concat_axis=0, tiled=True)]
    unnamed x23 -> x21, local copies, waits for them, and re-layouts: 5.44 us -> 3.12 us
    scatter x3 -> x0, local copies, waits for them, and re-layouts: 1.93 us -> none  [shards(): words = jnp.zeros((128,), f32).at[0].set(hi).at[1].set(mid).at[2].set(lo)]
    convert_element_type x2, other arithmetic: 0.01 us -> 1.93 us  [the longest x1 1.9 us: shards(): word = jnp.broadcast_to(word.astype(jnp.bfloat16), (n_date, 2 * cols, 128))]
    all_to_all x2 -> x0, other arithmetic: 1.64 us -> none  [shards(): got = lax.all_to_all(both, 'date', split_axis=0, concat_axis=0, tiled=True)]
    concatenate x0 -> x1, other arithmetic: none -> 1.56 us  [shards(): both = jnp.concatenate([both, word], axis=2)]
  transfers between devices with their start and end apart: 3 -> 4, of which waited for: 3 -> 4; matrix products, arithmetic and copies ran while one was open for 13% -> 12% of each run, Pallas kernels for 0% -> 0%
where the time goes in v5:
time: 110 us
  starting transfers between devices  26.5 us (24%)
  other arithmetic  25.5 us (23%)
  waiting for transfers between devices  24.2 us (22%)
  matrix products  14.4 us (13%)
  local copies, waits for them, and re-layouts  13.3 us (12%)
  between operations  5.85 us (5%)
    all_to_all x1, waiting for transfers between devices, shards(): got = lax.all_to_all(pair, 'date', split_axis=0, concat_axis=0, tiled=True)  17 us
    all_to_all x1, starting transfers between devices, shards(): got = lax.all_to_all(both, 'date', split_axis=0, concat_axis=0, tiled=True)  10.9 us
    ppermute x2, starting transfers between devices, shards(): own_sum = own_sum + lax.ppermute(own_sum, 'rng', pairs)  10.9 us
    convert_element_type x1, other arithmetic, dft_table(): (hi_c * lo_s + hi_s * lo_c).reshape(length, length).astype(jnp.bfloat16)  8.27 us
    all_to_all x1, waiting for transfers between devices, shards(): got = lax.all_to_all(both, 'date', split_axis=0, concat_axis=0, tiled=True)  6.91 us
    dot_general x1, matrix products, shards(): fc = jnp.dot(stacked, cos_t, preferred_element_type=f32)  5.89 us
    all_to_all x1, starting transfers between devices, shards(): got = lax.all_to_all(pair, 'date', split_axis=0, concat_axis=0, tiled=True)  4.7 us
    mul x1, other arithmetic, shards(): result = result * mask_px[:, None]  3.69 us
  transfers between devices with their start and end apart: 4, of which 4 were waited for; matrix products, arithmetic and copies ran while one was open for 12% of the time, Pallas kernels for 0%

profile of v5, /device:TPU:1, one launch (start us, length us, event | category | flops | bytes accessed | tf_op | source)
XLA Modules:
  0.0 109.8 jit_solution(9373547295088427989)
XLA Ops:
  0.0 1.2 %copy.29 = bf16[1,2048,128]{1,2,0:T(8,128)(2,1)S(1)} copy(bf16[1,2048,128]{2,1,0:T(8,128)(2,1)} %param.7) | data formatting | bytes 1048576 | tf_op args[0]
  1.3 1.2 %copy.30 = bf16[1,2048,128]{1,2,0:T(8,128)(2,1)S(1)} copy(bf16[1,2048,128]{2,1,0:T(8,128)(2,1)} %param.8) | data formatting | bytes 1048576 | tf_op args[1]
  2.5 0.9 add_reduce_fusion
  3.4 3.8 %collective-permute-start = (f32[]{:T(128)}, f32[]{:T(128)}, u32[]{:S(2)}, u32[]{:S(2)}) collective-permute-start(f32[]{:T(128)} %add_reduce_fusion), channel_id=1, source_target_pairs={{0,1},{1,0},{2,3},{3,2},{4,5},{5,4},{6,7},{7,6},{8,9},{9,8},{10,11... | collective-permute-start | bytes 20 | tf_op jit(solution)/shard_map/ppermute | solution.py:66
  7.3 0.8 copy.31
  9.5 7.1 %collective-permute-start.1 = (f32[]{:T(128)}, f32[]{:T(128)}, u32[]{:S(2)}, u32[]{:S(2)}) collective-permute-start(f32[]{:T(128)} %add.108), channel_id=1, source_target_pairs={{0,2},{1,3},{2,0},{3,1},{4,6},{5,7},{6,4},{7,5},{8,10},{9,11},{10,... | collective-permute-start | bytes 20 | tf_op jit(solution)/shard_map/ppermute | solution.py:66
  20.3 1.9 %fusion.47 = bf16[128]{0:T(256)(128)(2,1)S(1)} fusion(bf16[]{:T(256)} %reduce_precision.14, f32[]{:T(128)} %reduce_precision.13, f32[]{:T(128)} %reduce_precision.12), kind=kLoop, calls=%fused_computation.93 | loop fusion | flops 768 | bytes 266 | tf_op jit(solution)/shard_map/convert_element_type | solution.py:74
  22.2 1.6 %pad_maximum_fusion = bf16[64,4,2176]{2,1,0:T(4,128)(2,1)} fusion(bf16[64,4,2048]{2,1,0:T(4,128)(2,1)S(1)} %copy.31, bf16[2176]{0:T(1024)(128)(2,1)S(1)} %pad.11.clone), kind=kLoop, calls=%fused_computation.8 | loop fusion | flops 2228224 | bytes 2167040 | tf_op jit(solution)/shard_map/concatenate | solution.py:78
  23.7 10.9 %all-to-all-start = ((bf16[64,4,2176]{2,1,0:T(4,128)(2,1)}), bf16[64,4,2176]{2,1,0:T(4,128)(2,1)S(1)}, u32[]{:S(2)}, u32[]{:S(2)}) async-start(bf16[64,4,2176]{2,1,0:T(4,128)(2,1)} %pad_maximum_fusion), calls=%async_computation | async-start | bytes 2228224 | tf_op jit(solution)/shard_map/all_to_all | solution.py:79
  35.4 2.0 %fusion.24 = (f32[2048,64]{0,1:T(8,128)S(1)}, f32[2048,64]{0,1:T(8,128)S(1)}) fusion(), kind=kLoop, calls=%fused_computation.49 | loop fusion | flops 1835008 | bytes 1048576 | tf_op jit(solution)/shard_map/sin | solution.py:25
  37.4 1.1 %fusion.38 = (f32[2048,32]{0,1:T(8,128)S(1)}, f32[2048,32]{0,1:T(8,128)S(1)}) fusion(s32[32]{0:T(128)S(1)} %iota_multiply_fusion), kind=kLoop, calls=%fused_computation.63 | loop fusion | flops 917504 | bytes 524416 | tf_op jit(solution)/shard_map/cos | solution.py:24
  38.5 8.3 %add_convert_fusion = (bf16[2048,32,64]{0,2,1:T(8,128)(2,1)}, bf16[2048,32,64]{0,2,1:T(8,128)(2,1)}) fusion(f32[2048,64]{0,1:T(8,128)S(1)} %get-tuple-element.25, f32[2048,32]{0,1:T(8,128)S(1)} %get-tuple-element.24, f32[2048,64]{0,1:T(8,128)S(1)} %get-tuple-element.26, f32[2048,32]{0,1:T(8,128)S(1)} %get-tuple-element.23), kind=kLoop, calls=%fused_computation | loop fusion | flops 33554432 | bytes 18350080 | tf_op jit(solution)/shard_map/convert_element_type | solution.py:27
  46.8 6.9 %all-to-all-done = bf16[64,4,2176]{2,1,0:T(4,128)(2,1)S(1)} async-done(((bf16[64,4,2176]{2,1,0:T(4,128)(2,1)}), bf16[64,4,2176]{2,1,0:T(4,128)(2,1)S(1)}, u32[]{:S(2)}, u32[]{:S(2)}) %all-to-all-start) | async-done | bytes 1114144 | tf_op jit(solution)/shard_map/all_to_all | solution.py:79
  54.5 0.6 copy.38
  56.7 0.6 constant_dynamic-slice_fusion
  57.3 0.7 convert_multiply_fusion.2
  58.6 0.7 tile.21
  59.8 0.7 tile.9
  60.8 1.8 %add_convert_fusion.1 = (bf16[128,2048]{1,0:T(8,128)(2,1)S(1)}, bf16[128,2048]{1,0:T(8,128)(2,1)S(1)}) fusion(f32[128,2048]{1,0:T(8,128)S(1)} %tile.21, bf16[128,2048]{1,0:T(8,128)(2,1)} %copy-done.1, f32[128,2048]{1,0:T(8,128)S(1)} %tile.9, bf16[128,2048]{1,0:T(8,128)(2,1)} %copy-done, f32[128]{0:T(128)S(1)} %mul.288), kind=kLoop, calls=%fused_computation.26 | loop fusion | flops 3145728 | bytes 4194816 | tf_op jit(solution)/shard_map/convert_element_type | solution.py:96
  62.6 5.9 %fusion.14 = f32[256,2048]{1,0:T(8,128)S(1)} fusion(bf16[2048,2048]{0,1:T(8,128)(2,1)} %bitcast.51, bf16[128,2048]{1,0:T(8,128)(2,1)S(1)} %get-tuple-element.16, bf16[128,2048]{1,0:T(8,128)(2,1)S(1)} %get-tuple-element.15), kind=kOutput, calls=%fused_computation.36 | convolution fusion | flops 2149580800 | bytes 11534336 | tf_op jit(solution)/shard_map/dot_general | solution.py:102
  68.6 2.4 %fusion.13 = f32[256,2048]{1,0:T(8,128)S(1)} fusion(bf16[2048,2048]{0,1:T(8,128)(2,1)S(1)} %bitcast.49, bf16[128,2048]{1,0:T(8,128)(2,1)S(1)} %get-tuple-element.16, bf16[128,2048]{1,0:T(8,128)(2,1)S(1)} %get-tuple-element.15), kind=kOutput, calls=%fused_computation.35 | convolution fusion | flops 2149580800 | bytes 11534336 | tf_op jit(solution)/shard_map/dot_general | solution.py:103
  71.4 2.6 %fusion.12 = f32[256,2048]{1,0:T(8,128)S(1)} fusion(bf16[2048,2048]{0,1:T(8,128)(2,1)S(1)} %bitcast.54, bf16[128,2048]{1,0:T(8,128)(2,1)S(1)} %get-tuple-element.12, bf16[128,2048]{1,0:T(8,128)(2,1)S(1)} %get-tuple-element.11), kind=kOutput, calls=%fused_computation.34 | convolution fusion | flops 2149580800 | bytes 11534336 | tf_op jit(solution)/shard_map/dot_general | solution.py:111
  74.0 2.4 %fusion.11 = f32[256,2048]{1,0:T(8,128)S(1)} fusion(bf16[2048,2048]{0,1:T(8,128)(2,1)S(1)} %bitcast.50, bf16[128,2048]{1,0:T(8,128)(2,1)S(1)} %get-tuple-element.12, bf16[128,2048]{1,0:T(8,128)(2,1)S(1)} %get-tuple-element.11), kind=kOutput, calls=%fused_computation.33 | convolution fusion | flops 2149580800 | bytes 11534336 | tf_op jit(solution)/shard_map/dot_general | solution.py:112
  76.8 0.7 reshape.203
  77.9 1.3 %copy.36 = bf16[2048,256]{1,0:T(8,128)(2,1)} copy(bf16[2048,256]{0,1:T(8,128)(2,1)S(1)} %bitcast.60) | data formatting | bytes 2097152 | tf_op jit(solution)/shard_map/transpose | solution.py:117
  79.2 4.7 %all-to-all-start.1 = ((bf16[64,32,256]{2,1,0:T(8,128)(2,1)}), bf16[64,32,256]{2,1,0:T(8,128)(2,1)S(1)}, u32[]{:S(2)}, u32[]{:S(2)}) async-start(bf16[64,32,256]{2,1,0:T(8,128)(2,1)} %bitcast.17), calls=%async_computation.1 | async-start | bytes 2097152 | tf_op jit(solution)/shard_map/all_to_all | solution.py:118
  84.0 0.7 convert_bitcast_fusion
  85.4 17.0 %all-to-all-done.1 = bf16[64,32,256]{2,1,0:T(8,128)(2,1)S(1)} async-done(((bf16[64,32,256]{2,1,0:T(8,128)(2,1)}), bf16[64,32,256]{2,1,0:T(8,128)(2,1)S(1)}, u32[]{:S(2)}, u32[]{:S(2)}) %all-to-all-start.1) | async-done | bytes 1048608 | tf_op jit(solution)/shard_map/all_to_all | solution.py:118
  102.6 1.2 %copy.37 = bf16[64,32,2,128]{3,0,2,1:T(8,128)(2,1)S(1)} copy(bf16[64,32,2,128]{3,2,1,0:T(2,128)(2,1)S(1)} %reshape.205) | data formatting | bytes 2097152 | tf_op jit(solution)/shard_map/reshape | solution.py:119
  103.9 0.9 multiply_reduce_fusion
  104.9 1.2 %fusion.29 = f32[4096,512]{1,0:T(8,128)S(1)} fusion(bf16[4096,128]{1,0:T(8,128)(2,1)S(1)} %bitcast.55, bf16[64,256]{1,0:T(8,128)(2,1)S(1)} %get-tuple-element.22, bf16[64,256]{1,0:T(8,128)(2,1)S(1)} %get-tuple-element.21, bf16[64,256]{1,0:T(8,128)(2,1)S(1)} %fusion.53), kind=kOutput, calls=%fused_computation.54 | convolution fusion | flops 537395200 | bytes 9535488 | tf_op jit(solution)/shard_map/dot_general | solution.py:124
  106.1 3.7 %fusion.2 = f32[4096,256]{1,0:T(8,128)} fusion(f32[4096,512]{1,0:T(8,128)S(1)} %fusion.29, f32[4096]{0:T(1024)S(1)} %convert_bitcast_fusion, f32[4096]{0:T(1024)S(1)} %mul.337), kind=kLoop, calls=%fused_computation.5 | loop fusion | flops 5242880 | bytes 12615680 | tf_op jit(solution)/shard_map/mul | solution.py:134
  (47 shorter events, 6.3 us)
Async XLA Ops:
  3.4 4.9 %collective-permute-start = (f32[]{:T(128)}, f32[]{:T(128)}, u32[]{:S(2)}, u32[]{:S(2)}) collective-permute-start(f32[]{:T(128)} %add_reduce_fusion), channel_id=1, source_target_pairs={{0,1},{1,0},{2,3},{3,2},{4,5},{5,4},{6,7},{7,6},{8,9},{9,8},{10,11... | collective-permute-start | bytes 20 | tf_op jit(solution)/shard_map/ppermute | solution.py:66
  9.5 7.3 %collective-permute-start.1 = (f32[]{:T(128)}, f32[]{:T(128)}, u32[]{:S(2)}, u32[]{:S(2)}) collective-permute-start(f32[]{:T(128)} %add.108), channel_id=1, source_target_pairs={{0,2},{1,3},{2,0},{3,1},{4,6},{5,7},{6,4},{7,5},{8,10},{9,11},{10,... | collective-permute-start | bytes 20 | tf_op jit(solution)/shard_map/ppermute | solution.py:66
  23.7 29.9 %all-to-all-start = ((bf16[64,4,2176]{2,1,0:T(4,128)(2,1)}), bf16[64,4,2176]{2,1,0:T(4,128)(2,1)S(1)}, u32[]{:S(2)}, u32[]{:S(2)}) async-start(bf16[64,4,2176]{2,1,0:T(4,128)(2,1)} %pad_maximum_fusion), calls=%async_computation | async-start | bytes 2228224 | tf_op jit(solution)/shard_map/all_to_all | solution.py:79
  55.9 2.1 %copy-start = (bf16[128,2048]{1,0:T(8,128)(2,1)}, bf16[128,2048]{1,0:T(8,128)(2,1)S(1)}, u32[]{:S(2)}) copy-start(bf16[128,2048]{1,0:T(8,128)(2,1)S(1)} %reshape_squeeze.6) | copy-start | bytes 1572868
  56.7 1.4 %copy-start.1 = (bf16[128,2048]{1,0:T(8,128)(2,1)}, bf16[128,2048]{1,0:T(8,128)(2,1)S(1)}, u32[]{:S(2)}) copy-start(bf16[128,2048]{1,0:T(8,128)(2,1)S(1)} %reshape_squeeze.7) | copy-start | bytes 1572868
  60.8 7.8 %slice-start = ((s8[8388608]{0:T(1024)(128)(4,1)}), s8[4194304]{0:T(1024)(128)(4,1)S(1)}, s32[]{:S(2)}) async-start(s8[8388608]{0:T(1024)(128)(4,1)} %bitcast.47), calls=%async_computation.2 | async-start | bytes 8388608
  62.6 5.9 %slice-start.1 = ((s8[8388608]{0:T(1024)(128)(4,1)}), s8[4194304]{0:T(1024)(128)(4,1)S(1)}, s32[]{:S(2)}) async-start(s8[8388608]{0:T(1024)(128)(4,1)} %bitcast.47), calls=%async_computation.3 | async-start | bytes 8388608
  62.6 8.7 %slice-start.2 = ((s8[8388608]{0:T(1024)(128)(4,1)}), s8[4194304]{0:T(1024)(128)(4,1)S(1)}, s32[]{:S(2)}) async-start(s8[8388608]{0:T(1024)(128)(4,1)} %bitcast.52), calls=%async_computation.4 | async-start | bytes 8388608
  68.5 2.4 %copy-start.2 = (f32[2048]{0:T(1024)S(1)}, f32[2048]{0:T(1024)}, u32[]{:S(2)}) copy-start(f32[2048]{0:T(1024)} %param.10) | copy-start | bytes 24580
  68.6 2.8 %slice-start.3 = ((s8[8388608]{0:T(1024)(128)(4,1)}), s8[4194304]{0:T(1024)(128)(4,1)S(1)}, s32[]{:S(2)}) async-start(s8[8388608]{0:T(1024)(128)(4,1)} %bitcast.52), calls=%async_computation.5 | async-start | bytes 8388608
  76.8 7.9 %copy-start.3 = (s32[64]{0:T(128)S(1)}, s32[64]{0:T(128)}, u32[]{:S(2)}) copy-start(s32[64]{0:T(128)} %param.12) | copy-start | bytes 772
  76.8 7.9 %copy-start.4 = (s32[64]{0:T(128)S(1)}, s32[64]{0:T(128)}, u32[]{:S(2)}) copy-start(s32[64]{0:T(128)} %param.11) | copy-start | bytes 772
  79.2 23.1 %all-to-all-start.1 = ((bf16[64,32,256]{2,1,0:T(8,128)(2,1)}), bf16[64,32,256]{2,1,0:T(8,128)(2,1)S(1)}, u32[]{:S(2)}, u32[]{:S(2)}) async-start(bf16[64,32,256]{2,1,0:T(8,128)(2,1)} %bitcast.17), calls=%async_computation.1 | async-start | bytes 2097152 | tf_op jit(solution)/shard_map/all_to_all | solution.py:118

commit v6 on v5

--- a/solution.py
+++ b/solution.py
@@ -59,18 +59,22 @@
     wide_re = own_re.astype(f32)
     wide_im = own_im.astype(f32)
     local = jnp.sum(wide_re * wide_re + wide_im * wide_im)
-    own_sum = local
-    shift = 1
-    while shift < n_rng:
-        pairs = [(r, r ^ shift) for r in range(n_rng)]
-        own_sum = own_sum + lax.ppermute(own_sum, "rng", pairs)
-        shift *= 2
+    rng_me = lax.axis_index("rng")
+    received = [local] + [
+        lax.ppermute(local, "rng", [(r, (r + k) % n_rng) for r in range(n_rng)])
+        for k in range(1, n_rng)
+    ]
+    by_shift = jnp.stack(received)
+    by_source = by_shift[(rng_me - jnp.arange(n_rng)) % n_rng]
+    own_sum = by_source[0]
+    for k in range(1, n_rng):
+        own_sum = own_sum + by_source[k]
     lane = jnp.arange(128)
-    word = jnp.full((128,), own_sum)
+    word = jnp.where(lane < 3, own_sum, 0.0)
     hi = lax.reduce_precision(word, exponent_bits=8, mantissa_bits=7)
     mid = lax.reduce_precision(word - hi, exponent_bits=8, mantissa_bits=7)
     lo = lax.reduce_precision(word - hi - mid, exponent_bits=8, mantissa_bits=7)
-    word = jnp.where(lane == 0, hi, jnp.where(lane == 1, mid, jnp.where(lane == 2, lo, 0.0)))
+    word = jnp.where(lane == 0, hi, jnp.where(lane == 1, mid, lo))
     word = jnp.broadcast_to(word.astype(jnp.bfloat16), (n_date, 2 * cols, 128))
 
     both = jnp.stack([own_re.T, own_im.T]).reshape(2, cols, n_date, lines)

time: 110 us -> 110 us (level)
  between operations: 5.85 us -> 3.7 us
  starting transfers between devices: 26.5 us -> 25.2 us
  local copies, waits for them, and re-layouts: 13.3 us -> 14.6 us
  waiting for transfers between devices: 24.2 us -> 25.3 us
    another operation x0 -> x1, other arithmetic: none -> 2.65 us  [shards(): by_shift = jnp.stack(received)]
    convert_element_type x1, other arithmetic: 1.9 us -> 0.01 us  [shards(): word = jnp.broadcast_to(word.astype(jnp.bfloat16), (n_date, 2 * cols, 128))]
    ppermute x2 -> x3, waiting for transfers between devices: 0.31 us -> 1.45 us  [shards(): lax.ppermute(local, 'rng', [(r, (r + k) % n_rng) for r in range(n_rng)])]
    ppermute x2 -> x3, starting transfers between devices: 10.9 us -> 10.1 us  [shards(): lax.ppermute(local, 'rng', [(r, (r + k) % n_rng) for r in range(n_rng)])]
  transfers between devices with their start and end apart: 4 -> 5, of which waited for: 4 -> 4; matrix products, arithmetic and copies ran while one was open for 12% -> 13% of each run, Pallas kernels for 0% -> 0%
where the time goes in v6:
time: 110 us
  other arithmetic  26.2 us (24%)
  waiting for transfers between devices  25.3 us (23%)
  starting transfers between devices  25.2 us (23%)
  local copies, waits for them, and re-layouts  14.6 us (13%)
  matrix products  14.4 us (13%)
  between operations  3.7 us (3%)
    all_to_all x1, waiting for transfers between devices, shards(): got = lax.all_to_all(pair, 'date', split_axis=0, concat_axis=0, tiled=True)  17 us
    all_to_all x1, starting transfers between devices, shards(): got = lax.all_to_all(both, 'date', split_axis=0, concat_axis=0, tiled=True)  10.4 us
    ppermute x3, starting transfers between devices, shards(): lax.ppermute(local, 'rng', [(r, (r + k) % n_rng) for r in range(n_rng)])  10.1 us
    convert_element_type x1, other arithmetic, dft_table(): (hi_c * lo_s + hi_s * lo_c).reshape(length, length).astype(jnp.bfloat16)  8.26 us
    all_to_all x1, waiting for transfers between devices, shards(): got = lax.all_to_all(both, 'date', split_axis=0, concat_axis=0, tiled=True)  6.91 us
    dot_general x1, matrix products, shards(): fc = jnp.dot(stacked, cos_t, preferred_element_type=f32)  5.89 us
    all_to_all x1, starting transfers between devices, shards(): got = lax.all_to_all(pair, 'date', split_axis=0, concat_axis=0, tiled=True)  4.7 us
    mul x1, other arithmetic, shards(): result = result * mask_px[:, None]  3.69 us
  transfers between devices with their start and end apart: 5, of which 4 were waited for; matrix products, arithmetic and copies ran while one was open for 13% of the time, Pallas kernels for 0%

profile of v6, /device:TPU:1, one launch (start us, length us, event | category | flops | bytes accessed | tf_op | source)
XLA Modules:
  0.0 109.6 jit_solution(13343356237473180095)
XLA Ops:
  0.0 1.2 %copy.29 = bf16[1,2048,128]{1,2,0:T(8,128)(2,1)S(1)} copy(bf16[1,2048,128]{2,1,0:T(8,128)(2,1)} %param.7) | data formatting | bytes 1048576 | tf_op args[0]
  1.3 1.2 %copy.30 = bf16[1,2048,128]{1,2,0:T(8,128)(2,1)S(1)} copy(bf16[1,2048,128]{2,1,0:T(8,128)(2,1)} %param.8) | data formatting | bytes 1048576 | tf_op args[1]
  2.5 0.9 add_reduce_fusion
  3.4 7.7 %collective-permute-start.1 = (f32[]{:T(128)}, f32[]{:T(128)}, u32[]{:S(2)}, u32[]{:S(2)}) collective-permute-start(f32[]{:T(128)} %add_reduce_fusion), channel_id=1, source_target_pairs={{0,2},{1,3},{2,0},{3,1},{4,6},{5,7},{6,4},{7,5},{8,10},{9,11},{10,... | collective-permute-start | bytes 20 | tf_op jit(solution)/shard_map/ppermute | solution.py:64
  11.1 2.4 %collective-permute-start = (f32[]{:T(128)}, f32[]{:T(128)}, u32[]{:S(2)}, u32[]{:S(2)}) collective-permute-start(f32[]{:T(128)} %add_reduce_fusion), channel_id=1, source_target_pairs={{0,1},{1,2},{2,3},{3,0},{4,5},{5,6},{6,7},{7,4},{8,9},{9,10},{10,1... | collective-permute-start | bytes 20 | tf_op jit(solution)/shard_map/ppermute | solution.py:64
  13.6 0.8 copy.31
  14.7 1.2 %collective-permute-done = f32[]{:T(128)} collective-permute-done((f32[]{:T(128)}, f32[]{:T(128)}, u32[]{:S(2)}, u32[]{:S(2)}) %collective-permute-start) | collective-permute-done | bytes 36 | tf_op jit(solution)/shard_map/ppermute | solution.py:64
  15.9 2.7 %pad_maximum_fusion.9 = f32[4]{0:T(128)S(1)} fusion(f32[1]{0:T(128)} %bitcast.11, f32[1]{0:T(128)} %bitcast.10, f32[1]{0:T(128)} %bitcast.9, f32[1]{0:T(128)} %bitcast.8), kind=kLoop, calls=%fused_computation.104 | loop fusion | flops 12 | bytes 32 | tf_op jit(solution)/shard_map/stack | solution.py:67
  19.2 0.7 fusion.60
  22.4 1.6 %pad_maximum_fusion = bf16[64,4,2176]{2,1,0:T(4,128)(2,1)} fusion(bf16[64,4,2048]{2,1,0:T(4,128)(2,1)S(1)} %copy.31, bf16[2176]{0:T(1024)(128)(2,1)S(1)} %pad.11.clone), kind=kLoop, calls=%fused_computation.9 | loop fusion | flops 2228224 | bytes 2167040 | tf_op jit(solution)/shard_map/concatenate | solution.py:82
  24.0 10.4 %all-to-all-start = ((bf16[64,4,2176]{2,1,0:T(4,128)(2,1)}), bf16[64,4,2176]{2,1,0:T(4,128)(2,1)S(1)}, u32[]{:S(2)}, u32[]{:S(2)}) async-start(bf16[64,4,2176]{2,1,0:T(4,128)(2,1)} %pad_maximum_fusion), calls=%async_computation | async-start | bytes 2228224 | tf_op jit(solution)/shard_map/all_to_all | solution.py:83
  35.1 2.0 %fusion.24 = (f32[2048,64]{0,1:T(8,128)S(1)}, f32[2048,64]{0,1:T(8,128)S(1)}) fusion(), kind=kLoop, calls=%fused_computation.50 | loop fusion | flops 1835008 | bytes 1048576 | tf_op jit(solution)/shard_map/sin | solution.py:25
  37.2 1.1 %fusion.38 = (f32[2048,32]{0,1:T(8,128)S(1)}, f32[2048,32]{0,1:T(8,128)S(1)}) fusion(s32[32]{0:T(128)S(1)} %iota_multiply_fusion), kind=kLoop, calls=%fused_computation.64 | loop fusion | flops 917504 | bytes 524416 | tf_op jit(solution)/shard_map/cos | solution.py:24
  38.3 8.3 %add_convert_fusion = (bf16[2048,32,64]{0,2,1:T(8,128)(2,1)}, bf16[2048,32,64]{0,2,1:T(8,128)(2,1)}) fusion(f32[2048,64]{0,1:T(8,128)S(1)} %get-tuple-element.31, f32[2048,32]{0,1:T(8,128)S(1)} %get-tuple-element.28, f32[2048,64]{0,1:T(8,128)S(1)} %get-tuple-element.32, f32[2048,32]{0,1:T(8,128)S(1)} %get-tuple-element.27), kind=kLoop, calls=%fused_computation.1 | loop fusion | flops 33554432 | bytes 18350080 | tf_op jit(solution)/shard_map/convert_element_type | solution.py:27
  46.5 6.9 %all-to-all-done = bf16[64,4,2176]{2,1,0:T(4,128)(2,1)S(1)} async-done(((bf16[64,4,2176]{2,1,0:T(4,128)(2,1)}), bf16[64,4,2176]{2,1,0:T(4,128)(2,1)S(1)}, u32[]{:S(2)}, u32[]{:S(2)}) %all-to-all-start) | async-done | bytes 1114144 | tf_op jit(solution)/shard_map/all_to_all | solution.py:83
  57.1 0.7 convert_multiply_fusion.2
  58.3 0.7 tile.21
  59.5 0.7 tile.9
  60.5 1.8 %add_convert_fusion.1 = (bf16[128,2048]{1,0:T(8,128)(2,1)S(1)}, bf16[128,2048]{1,0:T(8,128)(2,1)S(1)}) fusion(f32[128,2048]{1,0:T(8,128)S(1)} %tile.21, bf16[128,2048]{1,0:T(8,128)(2,1)} %copy-done.1, f32[128,2048]{1,0:T(8,128)S(1)} %tile.9, bf16[128,2048]{1,0:T(8,128)(2,1)} %copy-done, f32[128]{0:T(128)S(1)} %mul.288), kind=kLoop, calls=%fused_computation.27 | loop fusion | flops 3145728 | bytes 4194816 | tf_op jit(solution)/shard_map/convert_element_type | solution.py:100
  62.4 5.9 %fusion.14 = f32[256,2048]{1,0:T(8,128)S(1)} fusion(bf16[2048,2048]{0,1:T(8,128)(2,1)} %bitcast.58, bf16[128,2048]{1,0:T(8,128)(2,1)S(1)} %get-tuple-element.16, bf16[128,2048]{1,0:T(8,128)(2,1)S(1)} %get-tuple-element.15), kind=kOutput, calls=%fused_computation.37 | convolution fusion | flops 2149580800 | bytes 11534336 | tf_op jit(solution)/shard_map/dot_general | solution.py:106
  68.3 2.4 %fusion.13 = f32[256,2048]{1,0:T(8,128)S(1)} fusion(bf16[2048,2048]{0,1:T(8,128)(2,1)S(1)} %bitcast.56, bf16[128,2048]{1,0:T(8,128)(2,1)S(1)} %get-tuple-element.16, bf16[128,2048]{1,0:T(8,128)(2,1)S(1)} %get-tuple-element.15), kind=kOutput, calls=%fused_computation.36 | convolution fusion | flops 2149580800 | bytes 11534336 | tf_op jit(solution)/shard_map/dot_general | solution.py:107
  71.1 2.6 %fusion.12 = f32[256,2048]{1,0:T(8,128)S(1)} fusion(bf16[2048,2048]{0,1:T(8,128)(2,1)S(1)} %bitcast.61, bf16[128,2048]{1,0:T(8,128)(2,1)S(1)} %get-tuple-element.12, bf16[128,2048]{1,0:T(8,128)(2,1)S(1)} %get-tuple-element.11), kind=kOutput, calls=%fused_computation.35 | convolution fusion | flops 2149580800 | bytes 11534336 | tf_op jit(solution)/shard_map/dot_general | solution.py:115
  73.7 2.4 %fusion.11 = f32[256,2048]{1,0:T(8,128)S(1)} fusion(bf16[2048,2048]{0,1:T(8,128)(2,1)S(1)} %bitcast.57, bf16[128,2048]{1,0:T(8,128)(2,1)S(1)} %get-tuple-element.12, bf16[128,2048]{1,0:T(8,128)(2,1)S(1)} %get-tuple-element.11), kind=kOutput, calls=%fused_computation.34 | convolution fusion | flops 2149580800 | bytes 11534336 | tf_op jit(solution)/shard_map/dot_general | solution.py:116
  76.6 0.7 reshape.255
  77.7 1.3 %copy.36 = bf16[2048,256]{1,0:T(8,128)(2,1)} copy(bf16[2048,256]{0,1:T(8,128)(2,1)S(1)} %bitcast.67) | data formatting | bytes 2097152 | tf_op jit(solution)/shard_map/transpose | solution.py:121
  79.0 4.7 %all-to-all-start.1 = ((bf16[64,32,256]{2,1,0:T(8,128)(2,1)}), bf16[64,32,256]{2,1,0:T(8,128)(2,1)S(1)}, u32[]{:S(2)}, u32[]{:S(2)}) async-start(bf16[64,32,256]{2,1,0:T(8,128)(2,1)} %bitcast.23), calls=%async_computation.1 | async-start | bytes 2097152 | tf_op jit(solution)/shard_map/all_to_all | solution.py:122
  83.7 0.7 convert_bitcast_fusion
  85.1 17.0 %all-to-all-done.1 = bf16[64,32,256]{2,1,0:T(8,128)(2,1)S(1)} async-done(((bf16[64,32,256]{2,1,0:T(8,128)(2,1)}), bf16[64,32,256]{2,1,0:T(8,128)(2,1)S(1)}, u32[]{:S(2)}, u32[]{:S(2)}) %all-to-all-start.1) | async-done | bytes 1048608 | tf_op jit(solution)/shard_map/all_to_all | solution.py:122
  102.4 1.2 %copy.37 = bf16[64,32,2,128]{3,0,2,1:T(8,128)(2,1)S(1)} copy(bf16[64,32,2,128]{3,2,1,0:T(2,128)(2,1)S(1)} %reshape.257) | data formatting | bytes 2097152 | tf_op jit(solution)/shard_map/reshape | solution.py:123
  103.6 0.9 multiply_reduce_fusion
  104.6 1.2 %fusion.29 = f32[4096,512]{1,0:T(8,128)S(1)} fusion(bf16[4096,128]{1,0:T(8,128)(2,1)S(1)} %bitcast.62, bf16[64,256]{1,0:T(8,128)(2,1)S(1)} %get-tuple-element.22, bf16[64,256]{1,0:T(8,128)(2,1)S(1)} %get-tuple-element.21, bf16[64,256]{1,0:T(8,128)(2,1)S(1)} %fusion.56), kind=kOutput, calls=%fused_computation.55 | convolution fusion | flops 537395200 | bytes 9535488 | tf_op jit(solution)/shard_map/dot_general | solution.py:128
  105.9 3.7 %fusion.2 = f32[4096,256]{1,0:T(8,128)} fusion(f32[4096,512]{1,0:T(8,128)S(1)} %fusion.29, f32[4096]{0:T(1024)S(1)} %convert_bitcast_fusion, f32[4096]{0:T(1024)S(1)} %mul.337), kind=kLoop, calls=%fused_computation.6 | loop fusion | flops 5242880 | bytes 12615680 | tf_op jit(solution)/shard_map/mul | solution.py:138
  (54 shorter events, 8.1 us)
Async XLA Ops:
  3.4 11.0 %collective-permute-start.1 = (f32[]{:T(128)}, f32[]{:T(128)}, u32[]{:S(2)}, u32[]{:S(2)}) collective-permute-start(f32[]{:T(128)} %add_reduce_fusion), channel_id=1, source_target_pairs={{0,2},{1,3},{2,0},{3,1},{4,6},{5,7},{6,4},{7,5},{8,10},{9,11},{10,... | collective-permute-start | bytes 20 | tf_op jit(solution)/shard_map/ppermute | solution.py:64
  11.1 3.6 %collective-permute-start.2 = (f32[]{:T(128)}, f32[]{:T(128)}, u32[]{:S(2)}, u32[]{:S(2)}) collective-permute-start(f32[]{:T(128)} %add_reduce_fusion), channel_id=1, source_target_pairs={{0,3},{1,0},{2,1},{3,2},{4,7},{5,4},{6,5},{7,6},{8,11},{9,8},{10,9... | collective-permute-start | bytes 20 | tf_op jit(solution)/shard_map/ppermute | solution.py:64
  11.1 4.8 %collective-permute-start = (f32[]{:T(128)}, f32[]{:T(128)}, u32[]{:S(2)}, u32[]{:S(2)}) collective-permute-start(f32[]{:T(128)} %add_reduce_fusion), channel_id=1, source_target_pairs={{0,1},{1,2},{2,3},{3,0},{4,5},{5,6},{6,7},{7,4},{8,9},{9,10},{10,1... | collective-permute-start | bytes 20 | tf_op jit(solution)/shard_map/ppermute | solution.py:64
  24.0 29.4 %all-to-all-start = ((bf16[64,4,2176]{2,1,0:T(4,128)(2,1)}), bf16[64,4,2176]{2,1,0:T(4,128)(2,1)S(1)}, u32[]{:S(2)}, u32[]{:S(2)}) async-start(bf16[64,4,2176]{2,1,0:T(4,128)(2,1)} %pad_maximum_fusion), calls=%async_computation | async-start | bytes 2228224 | tf_op jit(solution)/shard_map/all_to_all | solution.py:83
  55.7 2.1 %copy-start = (bf16[128,2048]{1,0:T(8,128)(2,1)}, bf16[128,2048]{1,0:T(8,128)(2,1)S(1)}, u32[]{:S(2)}) copy-start(bf16[128,2048]{1,0:T(8,128)(2,1)S(1)} %reshape_squeeze.6) | copy-start | bytes 1572868
  56.5 1.3 %copy-start.1 = (bf16[128,2048]{1,0:T(8,128)(2,1)}, bf16[128,2048]{1,0:T(8,128)(2,1)S(1)}, u32[]{:S(2)}) copy-start(bf16[128,2048]{1,0:T(8,128)(2,1)S(1)} %reshape_squeeze.7) | copy-start | bytes 1572868
  60.5 7.8 %slice-start = ((s8[8388608]{0:T(1024)(128)(4,1)}), s8[4194304]{0:T(1024)(128)(4,1)S(1)}, s32[]{:S(2)}) async-start(s8[8388608]{0:T(1024)(128)(4,1)} %bitcast.54), calls=%async_computation.2 | async-start | bytes 8388608
  62.3 5.9 %slice-start.1 = ((s8[8388608]{0:T(1024)(128)(4,1)}), s8[4194304]{0:T(1024)(128)(4,1)S(1)}, s32[]{:S(2)}) async-start(s8[8388608]{0:T(1024)(128)(4,1)} %bitcast.54), calls=%async_computation.3 | async-start | bytes 8388608
  62.3 8.7 %slice-start.2 = ((s8[8388608]{0:T(1024)(128)(4,1)}), s8[4194304]{0:T(1024)(128)(4,1)S(1)}, s32[]{:S(2)}) async-start(s8[8388608]{0:T(1024)(128)(4,1)} %bitcast.59), calls=%async_computation.4 | async-start | bytes 8388608
  68.3 2.4 %copy-start.2 = (f32[2048]{0:T(1024)S(1)}, f32[2048]{0:T(1024)}, u32[]{:S(2)}) copy-start(f32[2048]{0:T(1024)} %param.10) | copy-start | bytes 24580
  68.3 2.8 %slice-start.3 = ((s8[8388608]{0:T(1024)(128)(4,1)}), s8[4194304]{0:T(1024)(128)(4,1)S(1)}, s32[]{:S(2)}) async-start(s8[8388608]{0:T(1024)(128)(4,1)} %bitcast.59), calls=%async_computation.5 | async-start | bytes 8388608
  76.6 7.9 %copy-start.3 = (s32[64]{0:T(128)S(1)}, s32[64]{0:T(128)}, u32[]{:S(2)}) copy-start(s32[64]{0:T(128)} %param.12) | copy-start | bytes 772
  76.6 7.9 %copy-start.4 = (s32[64]{0:T(128)S(1)}, s32[64]{0:T(128)}, u32[]{:S(2)}) copy-start(s32[64]{0:T(128)} %param.11) | copy-start | bytes 772
  79.0 23.1 %all-to-all-start.1 = ((bf16[64,32,256]{2,1,0:T(8,128)(2,1)}), bf16[64,32,256]{2,1,0:T(8,128)(2,1)S(1)}, u32[]{:S(2)}, u32[]{:S(2)}) async-start(bf16[64,32,256]{2,1,0:T(8,128)(2,1)} %bitcast.23), calls=%async_computation.1 | async-start | bytes 2097152 | tf_op jit(solution)/shard_map/all_to_all | solution.py:122

commit v7 on v6

--- a/solution.py
+++ b/solution.py
@@ -1,8 +1,10 @@
+import functools
 import math
 
 import jax
 import jax.numpy as jnp
 from jax import lax
+from jax.experimental import pallas as pl
 from jax.sharding import PartitionSpec as P
 
 HGRID = 16
@@ -41,6 +43,38 @@
     upper = jnp.concatenate([phase_re, -phase_im], axis=1)
     lower = jnp.concatenate([phase_im, phase_re], axis=1)
     return jnp.concatenate([upper, lower], axis=0)
+
+
+def _tail_kernel(n_date, grid_size, z_ref, ph_ref, m_ref, o_ref):
+    z = z_ref[...]
+    spectra = jnp.dot(z, ph_ref[...], preferred_element_type=jnp.float32)
+    peri_re = spectra[:, :grid_size]
+    peri_im = spectra[:, grid_size:]
+    wide = z.astype(jnp.float32)
+    pixel_power = jnp.sum(wide * wide, axis=1, keepdims=True) / n_date
+    val = (peri_re * peri_re + peri_im * peri_im) / (n_date * jnp.maximum(pixel_power, 1.0))
+    o_ref[...] = val * m_ref[...]
+
+
+def periodogram(z, phase, mask_px, n_date, block=512):
+    rows, depth = z.shape
+    grid_size = phase.shape[1] // 2
+    return pl.pallas_call(
+        functools.partial(_tail_kernel, n_date, grid_size),
+        out_shape=jax.ShapeDtypeStruct((rows, grid_size), jnp.float32),
+        grid=(rows // block,),
+        in_specs=[
+            pl.BlockSpec((block, depth), lambda i: (i, 0)),
+            pl.BlockSpec(phase.shape, lambda i: (0, 0)),
+            pl.BlockSpec((block, 1), lambda i: (i, 0)),
+        ],
+        out_specs=pl.BlockSpec((block, grid_size), lambda i: (i, 0)),
+        cost_estimate=pl.CostEstimate(
+            flops=2 * rows * depth * 2 * grid_size,
+            transcendentals=0,
+            bytes_accessed=rows * depth * 2 + rows * grid_size * 4 + rows * 4,
+        ),
+    )(z, phase, mask_px)
 
 
 def shards(slc_re, slc_im, ref_date, gain, bperp, tdays, mask):
@@ -123,20 +157,11 @@
     z = got.reshape(n_date, lines_dev, cols, 2 * n_date).transpose(1, 2, 0, 3)
     z = z.reshape(lines_dev * cols * n_date, 2 * n_date)
 
-    grid_size = HGRID * VGRID
     phase = phase_tables(bperp, tdays)
-    spectra = jnp.dot(z, phase, preferred_element_type=f32)
-    peri_re = spectra[:, :grid_size]
-    peri_im = spectra[:, grid_size:]
-    wide = z.astype(f32)
-    pixel_power = jnp.sum(wide * wide, axis=1) / n_date
     mask_rows = lax.dynamic_slice_in_dim(mask, me * lines_dev, lines_dev, 0)
-    mask_px = mask_rows.reshape(-1).astype(f32)
-    result = (peri_re * peri_re + peri_im * peri_im) / (
-        n_date * jnp.maximum(pixel_power, 1.0)
-    )[:, None]
-    result = result * mask_px[:, None]
-    return result.reshape(lines_dev, cols * n_date, grid_size)
+    mask_px = mask_rows.reshape(-1, 1).astype(f32)
+    result = periodogram(z, phase, mask_px, n_date)
+    return result.reshape(lines_dev, cols * n_date, HGRID * VGRID)
 
 
 def solution(mesh):

time: 110 us -> 113 us (1.027)
  Pallas kernels: 0 us -> 7.4 us
  other arithmetic: 26.2 us -> 22.2 us
  local copies, waits for them, and re-layouts: 14.6 us -> 17.5 us
  waiting for transfers between devices: 25.3 us -> 22.7 us
  matrix products: 14.4 us -> 13.2 us
    pallas_call x0 -> x1, Pallas kernels: none -> 7.4 us  [periodogram(): pl.pallas_call(functools.partial(_tail_kernel, n_date, grid_size), out_sh...]
    mul x2 -> x0, other arithmetic: 3.71 us -> none  [the longest x1 3.69 us: shards(): result = result * mask_px[:, None]]
    all_to_all x1, waiting for transfers between devices: 17 us -> 14.3 us  [shards(): got = lax.all_to_all(pair, 'date', split_axis=0, concat_axis=0, tiled=True)]
    transpose x0 -> x1, local copies, waits for them, and re-layouts: none -> 2.2 us  [shards(): z = got.reshape(n_date, lines_dev, cols, 2 * n_date).transpose(1, 2, 0, 3)]
    convert_element_type x0 -> x1, local copies, waits for them, and re-layouts: none -> 1.98 us  [shards(): mask_px = mask_rows.reshape(-1, 1).astype(f32)]
    dot_general x1 -> x0, matrix products: 1.24 us -> none  [shards(): spectra = jnp.dot(z, phase, preferred_element_type=f32)]
    reshape x2 -> x1, local copies, waits for them, and re-layouts: 1.49 us -> 0.27 us  [shards(): z = got.reshape(n_date, lines_dev, cols, 2 * n_date).transpose(1, 2, 0, 3)]
  transfers between devices with their start and end apart: 5 -> 5, of which waited for: 4 -> 4; matrix products, arithmetic and copies ran while one was open for 13% -> 15% of each run, Pallas kernels for 0% -> 0%
where the time goes in v7:
time: 113 us; the launch traced here: 112 us
  starting transfers between devices  25.4 us (22%)
  waiting for transfers between devices  22.7 us (20%)
  other arithmetic  22.2 us (20%)
  local copies, waits for them, and re-layouts  17.5 us (15%)
  matrix products  13.2 us (12%)
  Pallas kernels  7.4 us (7%)
  between operations  3.66 us (3%)
    all_to_all x1, waiting for transfers between devices, shards(): got = lax.all_to_all(pair, 'date', split_axis=0, concat_axis=0, tiled=True)  14.3 us
    all_to_all x1, starting transfers between devices, shards(): got = lax.all_to_all(both, 'date', split_axis=0, concat_axis=0, tiled=True)  10.4 us
    ppermute x3, starting transfers between devices, shards(): lax.ppermute(local, 'rng', [(r, (r + k) % n_rng) for r in range(n_rng)])  10.1 us
    convert_element_type x1, other arithmetic, dft_table(): (hi_c * lo_s + hi_s * lo_c).reshape(length, length).astype(jnp.bfloat16)  8.22 us
    pallas_call x1, Pallas kernels, periodogram(): pl.pallas_call(functools.partial(_tail_kernel, n_date, grid_size), out_sh...  7.4 us
    all_to_all x1, waiting for transfers between devices, shards(): got = lax.all_to_all(both, 'date', split_axis=0, concat_axis=0, tiled=True)  6.95 us
    dot_general x1, matrix products, shards(): fc = jnp.dot(stacked, cos_t, preferred_element_type=f32)  5.89 us
    all_to_all x1, starting transfers between devices, shards(): got = lax.all_to_all(pair, 'date', split_axis=0, concat_axis=0, tiled=True)  4.84 us
  transfers between devices with their start and end apart: 5, of which 4 were waited for; matrix products, arithmetic and copies ran while one was open for 15% of the time, Pallas kernels for 0%

profile of v7, /device:TPU:1, one launch (start us, length us, event | category | flops | bytes accessed | tf_op | source)
XLA Modules:
  0.0 112.1 jit_solution(18404830789285356103)
XLA Ops:
  0.0 1.2 %copy.32 = bf16[1,2048,128]{1,2,0:T(8,128)(2,1)S(1)} copy(bf16[1,2048,128]{2,1,0:T(8,128)(2,1)} %param.7) | data formatting | bytes 1048576 | tf_op args[0]
  1.3 1.2 %copy.33 = bf16[1,2048,128]{1,2,0:T(8,128)(2,1)S(1)} copy(bf16[1,2048,128]{2,1,0:T(8,128)(2,1)} %param.8) | data formatting | bytes 1048576 | tf_op args[1]
  2.5 0.9 add_reduce_fusion
  3.4 7.7 %collective-permute-start.1 = (f32[]{:T(128)}, f32[]{:T(128)}, u32[]{:S(2)}, u32[]{:S(2)}) collective-permute-start(f32[]{:T(128)} %add_reduce_fusion), channel_id=1, source_target_pairs={{0,2},{1,3},{2,0},{3,1},{4,6},{5,7},{6,4},{7,5},{8,10},{9,11},{10,... | collective-permute-start | bytes 20 | tf_op jit(solution)/shard_map/ppermute | solution.py:98
  11.1 2.4 %collective-permute-start = (f32[]{:T(128)}, f32[]{:T(128)}, u32[]{:S(2)}, u32[]{:S(2)}) collective-permute-start(f32[]{:T(128)} %add_reduce_fusion), channel_id=1, source_target_pairs={{0,1},{1,2},{2,3},{3,0},{4,5},{5,6},{6,7},{7,4},{8,9},{9,10},{10,1... | collective-permute-start | bytes 20 | tf_op jit(solution)/shard_map/ppermute | solution.py:98
  13.6 0.8 copy.34
  14.5 1.4 %collective-permute-done = f32[]{:T(128)} collective-permute-done((f32[]{:T(128)}, f32[]{:T(128)}, u32[]{:S(2)}, u32[]{:S(2)}) %collective-permute-start) | collective-permute-done | bytes 36 | tf_op jit(solution)/shard_map/ppermute | solution.py:98
  15.9 2.6 %pad_maximum_fusion.9 = f32[4]{0:T(128)S(1)} fusion(f32[1]{0:T(128)} %bitcast.11, f32[1]{0:T(128)} %bitcast.10, f32[1]{0:T(128)} %bitcast.9, f32[1]{0:T(128)} %bitcast.8), kind=kLoop, calls=%fused_computation.90 | loop fusion | flops 12 | bytes 32 | tf_op jit(solution)/shard_map/stack | solution.py:101
  19.2 0.7 fusion.48
  22.4 1.6 %pad_maximum_fusion = bf16[64,4,2176]{2,1,0:T(4,128)(2,1)} fusion(bf16[64,4,2048]{2,1,0:T(4,128)(2,1)S(1)} %copy.34, bf16[2176]{0:T(1024)(128)(2,1)S(1)} %pad.11.clone), kind=kLoop, calls=%fused_computation.3 | loop fusion | flops 2228224 | bytes 2167040 | tf_op jit(solution)/shard_map/concatenate | solution.py:116
  24.0 10.4 %all-to-all-start = ((bf16[64,4,2176]{2,1,0:T(4,128)(2,1)}), bf16[64,4,2176]{2,1,0:T(4,128)(2,1)S(1)}, u32[]{:S(2)}, u32[]{:S(2)}) async-start(bf16[64,4,2176]{2,1,0:T(4,128)(2,1)} %pad_maximum_fusion), calls=%async_computation | async-start | bytes 2228224 | tf_op jit(solution)/shard_map/all_to_all | solution.py:117
  35.1 2.0 %fusion.21 = (f32[2048,64]{0,1:T(8,128)S(1)}, f32[2048,64]{0,1:T(8,128)S(1)}) fusion(), kind=kLoop, calls=%fused_computation.44 | loop fusion | flops 1835008 | bytes 1048576 | tf_op jit(solution)/shard_map/sin | solution.py:27
  37.2 1.1 fusion.27
  38.3 8.2 %add_convert_fusion = (bf16[2048,32,64]{0,2,1:T(8,128)(2,1)}, bf16[2048,32,64]{0,2,1:T(8,128)(2,1)}) fusion(f32[2048,64]{0,1:T(8,128)S(1)} %get-tuple-element.31, f32[2048,32]{0,1:T(8,128)S(1)} %get-tuple-element.28, f32[2048,64]{0,1:T(8,128)S(1)} %get-tuple-element.32, f32[2048,32]{0,1:T(8,128)S(1)} %get-tuple-element.27), kind=kLoop, calls=%fused_computation.1 | loop fusion | flops 33554432 | bytes 18350080 | tf_op jit(solution)/shard_map/convert_element_type | solution.py:29
  46.5 7.0 %all-to-all-done = bf16[64,4,2176]{2,1,0:T(4,128)(2,1)S(1)} async-done(((bf16[64,4,2176]{2,1,0:T(4,128)(2,1)}), bf16[64,4,2176]{2,1,0:T(4,128)(2,1)S(1)}, u32[]{:S(2)}, u32[]{:S(2)}) %all-to-all-start) | async-done | bytes 1114144 | tf_op jit(solution)/shard_map/all_to_all | solution.py:117
  57.1 0.7 convert_multiply_fusion.2
  58.3 0.7 tile.21
  59.5 0.7 tile.9
  60.5 1.8 %add_convert_fusion.1 = (bf16[128,2048]{1,0:T(8,128)(2,1)S(1)}, bf16[128,2048]{1,0:T(8,128)(2,1)S(1)}) fusion(f32[128,2048]{1,0:T(8,128)S(1)} %tile.21, bf16[128,2048]{1,0:T(8,128)(2,1)} %copy-done.1, f32[128,2048]{1,0:T(8,128)S(1)} %tile.9, bf16[128,2048]{1,0:T(8,128)(2,1)} %copy-done, f32[128]{0:T(128)S(1)} %mul.260), kind=kLoop, calls=%fused_computation.21 | loop fusion | flops 3145728 | bytes 4194816 | tf_op jit(solution)/shard_map/convert_element_type | solution.py:134
  62.3 5.9 %fusion.11 = f32[256,2048]{1,0:T(8,128)S(1)} fusion(bf16[2048,2048]{0,1:T(8,128)(2,1)} %bitcast.54, bf16[128,2048]{1,0:T(8,128)(2,1)S(1)} %get-tuple-element.16, bf16[128,2048]{1,0:T(8,128)(2,1)S(1)} %get-tuple-element.15), kind=kOutput, calls=%fused_computation.31 | convolution fusion | flops 2149580800 | bytes 11534336 | tf_op jit(solution)/shard_map/dot_general | solution.py:140
  68.3 2.4 %fusion.10 = f32[256,2048]{1,0:T(8,128)S(1)} fusion(bf16[2048,2048]{0,1:T(8,128)(2,1)S(1)} %bitcast.52, bf16[128,2048]{1,0:T(8,128)(2,1)S(1)} %get-tuple-element.16, bf16[128,2048]{1,0:T(8,128)(2,1)S(1)} %get-tuple-element.15), kind=kOutput, calls=%fused_computation.30 | convolution fusion | flops 2149580800 | bytes 11534336 | tf_op jit(solution)/shard_map/dot_general | solution.py:141
  71.1 2.6 %fusion.9 = f32[256,2048]{1,0:T(8,128)S(1)} fusion(bf16[2048,2048]{0,1:T(8,128)(2,1)S(1)} %bitcast.57, bf16[128,2048]{1,0:T(8,128)(2,1)S(1)} %get-tuple-element.12, bf16[128,2048]{1,0:T(8,128)(2,1)S(1)} %get-tuple-element.11), kind=kOutput, calls=%fused_computation.29 | convolution fusion | flops 2149580800 | bytes 11534336 | tf_op jit(solution)/shard_map/dot_general | solution.py:149
  73.7 2.4 %fusion.8 = f32[256,2048]{1,0:T(8,128)S(1)} fusion(bf16[2048,2048]{0,1:T(8,128)(2,1)S(1)} %bitcast.53, bf16[128,2048]{1,0:T(8,128)(2,1)S(1)} %get-tuple-element.12, bf16[128,2048]{1,0:T(8,128)(2,1)S(1)} %get-tuple-element.11), kind=kOutput, calls=%fused_computation.28 | convolution fusion | flops 2149580800 | bytes 11534336 | tf_op jit(solution)/shard_map/dot_general | solution.py:150
  76.5 0.7 reshape.247
  77.6 1.3 %copy.39 = bf16[2048,256]{1,0:T(8,128)(2,1)} copy(bf16[2048,256]{0,1:T(8,128)(2,1)S(1)} %bitcast.63) | data formatting | bytes 2097152 | tf_op jit(solution)/shard_map/transpose | solution.py:155
  78.9 4.8 %all-to-all-start.1 = ((bf16[64,32,256]{2,1,0:T(8,128)(2,1)}), bf16[64,32,256]{2,1,0:T(8,128)(2,1)S(1)}, u32[]{:S(2)}, u32[]{:S(2)}) async-start(bf16[64,32,256]{2,1,0:T(8,128)(2,1)} %bitcast.23), calls=%async_computation.1 | async-start | bytes 2097152 | tf_op jit(solution)/shard_map/all_to_all | solution.py:156
  83.8 0.7 dynamic-slice_convert_fusion
  84.5 2.0 %copy.41.m_ref = f32[4096,1]{1,0:T(8,128)} copy(f32[4096,1]{0,1:T(1,128)S(1)} %bitcast.66) | data formatting | bytes 32768 | tf_op jit(solution)/shard_map/convert_element_type | solution.py:162
  87.2 0.7 maximum_maximum_fusion.ph_ref
  87.8 14.3 %all-to-all-done.1 = bf16[64,32,256]{2,1,0:T(8,128)(2,1)S(1)} async-done(((bf16[64,32,256]{2,1,0:T(8,128)(2,1)}), bf16[64,32,256]{2,1,0:T(8,128)(2,1)S(1)}, u32[]{:S(2)}, u32[]{:S(2)}) %all-to-all-start.1) | async-done | bytes 1048608 | tf_op jit(solution)/shard_map/all_to_all | solution.py:156
  102.4 2.2 %copy.40 = bf16[32,2,64,128]{3,2,1,0:T(8,128)(2,1)} copy(bf16[32,2,64,128]{3,1,0,2:T(2,128)(2,1)S(1)} %bitcast.64) | data formatting | bytes 2097152 | tf_op jit(solution)/shard_map/transpose | solution.py:157
  104.6 7.4 %shard_map.73 = f32[4096,256]{1,0:T(8,128)} custom-call(bf16[4096,128]{1,0:T(8,128)(2,1)} %bitcast.60, bf16[128,512]{1,0:T(8,128)(2,1)} %maximum_maximum_fusion.ph_ref, f32[4096,1]{1,0:T(8,128)} %copy.41.m_ref), custom_call_target="tpu_custom_call" | custom-call | flops 536870912 | bytes 5259264 | tf_op jit(solution)/shard_map/pallas_call | solution.py:62
  (52 shorter events, 7.8 us)
Async XLA Ops:
  3.4 11.0 %collective-permute-start.1 = (f32[]{:T(128)}, f32[]{:T(128)}, u32[]{:S(2)}, u32[]{:S(2)}) collective-permute-start(f32[]{:T(128)} %add_reduce_fusion), channel_id=1, source_target_pairs={{0,2},{1,3},{2,0},{3,1},{4,6},{5,7},{6,4},{7,5},{8,10},{9,11},{10,... | collective-permute-start | bytes 20 | tf_op jit(solution)/shard_map/ppermute | solution.py:98
  11.1 3.4 %collective-permute-start.2 = (f32[]{:T(128)}, f32[]{:T(128)}, u32[]{:S(2)}, u32[]{:S(2)}) collective-permute-start(f32[]{:T(128)} %add_reduce_fusion), channel_id=1, source_target_pairs={{0,3},{1,0},{2,1},{3,2},{4,7},{5,4},{6,5},{7,6},{8,11},{9,8},{10,9... | collective-permute-start | bytes 20 | tf_op jit(solution)/shard_map/ppermute | solution.py:98
  11.1 4.8 %collective-permute-start = (f32[]{:T(128)}, f32[]{:T(128)}, u32[]{:S(2)}, u32[]{:S(2)}) collective-permute-start(f32[]{:T(128)} %add_reduce_fusion), channel_id=1, source_target_pairs={{0,1},{1,2},{2,3},{3,0},{4,5},{5,6},{6,7},{7,4},{8,9},{9,10},{10,1... | collective-permute-start | bytes 20 | tf_op jit(solution)/shard_map/ppermute | solution.py:98
  24.0 29.4 %all-to-all-start = ((bf16[64,4,2176]{2,1,0:T(4,128)(2,1)}), bf16[64,4,2176]{2,1,0:T(4,128)(2,1)S(1)}, u32[]{:S(2)}, u32[]{:S(2)}) async-start(bf16[64,4,2176]{2,1,0:T(4,128)(2,1)} %pad_maximum_fusion), calls=%async_computation | async-start | bytes 2228224 | tf_op jit(solution)/shard_map/all_to_all | solution.py:117
  55.7 2.1 %copy-start = (bf16[128,2048]{1,0:T(8,128)(2,1)}, bf16[128,2048]{1,0:T(8,128)(2,1)S(1)}, u32[]{:S(2)}) copy-start(bf16[128,2048]{1,0:T(8,128)(2,1)S(1)} %reshape_squeeze.6) | copy-start | bytes 1572868
  56.4 1.3 %copy-start.1 = (bf16[128,2048]{1,0:T(8,128)(2,1)}, bf16[128,2048]{1,0:T(8,128)(2,1)S(1)}, u32[]{:S(2)}) copy-start(bf16[128,2048]{1,0:T(8,128)(2,1)S(1)} %reshape_squeeze.7) | copy-start | bytes 1572868
  60.5 7.8 %slice-start = ((s8[8388608]{0:T(1024)(128)(4,1)}), s8[4194304]{0:T(1024)(128)(4,1)S(1)}, s32[]{:S(2)}) async-start(s8[8388608]{0:T(1024)(128)(4,1)} %bitcast.50), calls=%async_computation.2 | async-start | bytes 8388608
  62.3 5.9 %slice-start.1 = ((s8[8388608]{0:T(1024)(128)(4,1)}), s8[4194304]{0:T(1024)(128)(4,1)S(1)}, s32[]{:S(2)}) async-start(s8[8388608]{0:T(1024)(128)(4,1)} %bitcast.50), calls=%async_computation.3 | async-start | bytes 8388608
  62.3 8.7 %slice-start.2 = ((s8[8388608]{0:T(1024)(128)(4,1)}), s8[4194304]{0:T(1024)(128)(4,1)S(1)}, s32[]{:S(2)}) async-start(s8[8388608]{0:T(1024)(128)(4,1)} %bitcast.55), calls=%async_computation.4 | async-start | bytes 8388608
  68.2 2.4 %copy-start.2 = (f32[2048]{0:T(1024)S(1)}, f32[2048]{0:T(1024)}, u32[]{:S(2)}) copy-start(f32[2048]{0:T(1024)} %param.10) | copy-start | bytes 24580
  68.3 2.8 %slice-start.3 = ((s8[8388608]{0:T(1024)(128)(4,1)}), s8[4194304]{0:T(1024)(128)(4,1)S(1)}, s32[]{:S(2)}) async-start(s8[8388608]{0:T(1024)(128)(4,1)} %bitcast.55), calls=%async_computation.5 | async-start | bytes 8388608
  78.9 7.6 %copy-start.3 = (s32[64]{0:T(128)S(1)}, s32[64]{0:T(128)}, u32[]{:S(2)}) copy-start(s32[64]{0:T(128)} %param.12) | copy-start | bytes 772
  78.9 7.6 %copy-start.4 = (s32[64]{0:T(128)S(1)}, s32[64]{0:T(128)}, u32[]{:S(2)}) copy-start(s32[64]{0:T(128)} %param.11) | copy-start | bytes 772
  78.9 23.3 %all-to-all-start.1 = ((bf16[64,32,256]{2,1,0:T(8,128)(2,1)}), bf16[64,32,256]{2,1,0:T(8,128)(2,1)S(1)}, u32[]{:S(2)}, u32[]{:S(2)}) async-start(bf16[64,32,256]{2,1,0:T(8,128)(2,1)} %bitcast.23), calls=%async_computation.1 | async-start | bytes 2097152 | tf_op jit(solution)/shard_map/all_to_all | solution.py:156

commit v8 on v7

--- a/solution.py
+++ b/solution.py
@@ -52,11 +52,11 @@
     peri_im = spectra[:, grid_size:]
     wide = z.astype(jnp.float32)
     pixel_power = jnp.sum(wide * wide, axis=1, keepdims=True) / n_date
-    val = (peri_re * peri_re + peri_im * peri_im) / (n_date * jnp.maximum(pixel_power, 1.0))
-    o_ref[...] = val * m_ref[...]
+    row_factor = m_ref[...] / (n_date * jnp.maximum(pixel_power, 1.0))
+    o_ref[...] = (peri_re * peri_re + peri_im * peri_im) * row_factor
 
 
-def periodogram(z, phase, mask_px, n_date, block=512):
+def periodogram(z, phase, mask_px, n_date, block=1024):
     rows, depth = z.shape
     grid_size = phase.shape[1] // 2
     return pl.pallas_call(

time: 113 us -> 110 us (0.973)
  Pallas kernels: 7.4 us -> 5.2 us
    pallas_call x1, Pallas kernels: 7.4 us -> 5.2 us  [periodogram(): pl.pallas_call(functools.partial(_tail_kernel, n_date, grid_size), out_sh...]
where the time goes in v8:
time: 110 us
  starting transfers between devices  25.4 us (23%)
  waiting for transfers between devices  22.7 us (21%)
  other arithmetic  22.2 us (20%)
  local copies, waits for them, and re-layouts  17.5 us (16%)
  matrix products  13.2 us (12%)
  Pallas kernels  5.2 us (5%)
  between operations  3.66 us (3%)
    all_to_all x1, waiting for transfers between devices, shards(): got = lax.all_to_all(pair, 'date', split_axis=0, concat_axis=0, tiled=True)  14.3 us
    all_to_all x1, starting transfers between devices, shards(): got = lax.all_to_all(both, 'date', split_axis=0, concat_axis=0, tiled=True)  10.4 us
    ppermute x3, starting transfers between devices, shards(): lax.ppermute(local, 'rng', [(r, (r + k) % n_rng) for r in range(n_rng)])  10.1 us
    convert_element_type x1, other arithmetic, dft_table(): (hi_c * lo_s + hi_s * lo_c).reshape(length, length).astype(jnp.bfloat16)  8.22 us
    all_to_all x1, waiting for transfers between devices, shards(): got = lax.all_to_all(both, 'date', split_axis=0, concat_axis=0, tiled=True)  6.95 us
    dot_general x1, matrix products, shards(): fc = jnp.dot(stacked, cos_t, preferred_element_type=f32)  5.89 us
    pallas_call x1, Pallas kernels, periodogram(): pl.pallas_call(functools.partial(_tail_kernel, n_date, grid_size), out_sh...  5.2 us
    all_to_all x1, starting transfers between devices, shards(): got = lax.all_to_all(pair, 'date', split_axis=0, concat_axis=0, tiled=True)  4.84 us
  transfers between devices with their start and end apart: 5, of which 4 were waited for; matrix products, arithmetic and copies ran while one was open for 15% of the time, Pallas kernels for 0%

profile of v8, /device:TPU:1, one launch (start us, length us, event | category | flops | bytes accessed | tf_op | source)
XLA Modules:
  0.0 109.9 jit_solution(17860946580647249593)
XLA Ops:
  0.0 1.2 %copy.32 = bf16[1,2048,128]{1,2,0:T(8,128)(2,1)S(1)} copy(bf16[1,2048,128]{2,1,0:T(8,128)(2,1)} %param.7) | data formatting | bytes 1048576 | tf_op args[0]
  1.3 1.2 %copy.33 = bf16[1,2048,128]{1,2,0:T(8,128)(2,1)S(1)} copy(bf16[1,2048,128]{2,1,0:T(8,128)(2,1)} %param.8) | data formatting | bytes 1048576 | tf_op args[1]
  2.5 0.9 add_reduce_fusion
  3.4 7.7 %collective-permute-start.1 = (f32[]{:T(128)}, f32[]{:T(128)}, u32[]{:S(2)}, u32[]{:S(2)}) collective-permute-start(f32[]{:T(128)} %add_reduce_fusion), channel_id=1, source_target_pairs={{0,2},{1,3},{2,0},{3,1},{4,6},{5,7},{6,4},{7,5},{8,10},{9,11},{10,... | collective-permute-start | bytes 20 | tf_op jit(solution)/shard_map/ppermute | solution.py:98
  11.1 2.4 %collective-permute-start = (f32[]{:T(128)}, f32[]{:T(128)}, u32[]{:S(2)}, u32[]{:S(2)}) collective-permute-start(f32[]{:T(128)} %add_reduce_fusion), channel_id=1, source_target_pairs={{0,1},{1,2},{2,3},{3,0},{4,5},{5,6},{6,7},{7,4},{8,9},{9,10},{10,1... | collective-permute-start | bytes 20 | tf_op jit(solution)/shard_map/ppermute | solution.py:98
  13.6 0.8 copy.34
  14.5 1.4 %collective-permute-done = f32[]{:T(128)} collective-permute-done((f32[]{:T(128)}, f32[]{:T(128)}, u32[]{:S(2)}, u32[]{:S(2)}) %collective-permute-start) | collective-permute-done | bytes 36 | tf_op jit(solution)/shard_map/ppermute | solution.py:98
  15.9 2.6 %pad_maximum_fusion.9 = f32[4]{0:T(128)S(1)} fusion(f32[1]{0:T(128)} %bitcast.11, f32[1]{0:T(128)} %bitcast.10, f32[1]{0:T(128)} %bitcast.9, f32[1]{0:T(128)} %bitcast.8), kind=kLoop, calls=%fused_computation.90 | loop fusion | flops 12 | bytes 32 | tf_op jit(solution)/shard_map/stack | solution.py:101
  19.2 0.7 fusion.48
  22.4 1.6 %pad_maximum_fusion = bf16[64,4,2176]{2,1,0:T(4,128)(2,1)} fusion(bf16[64,4,2048]{2,1,0:T(4,128)(2,1)S(1)} %copy.34, bf16[2176]{0:T(1024)(128)(2,1)S(1)} %pad.11.clone), kind=kLoop, calls=%fused_computation.3 | loop fusion | flops 2228224 | bytes 2167040 | tf_op jit(solution)/shard_map/concatenate | solution.py:116
  24.0 10.4 %all-to-all-start = ((bf16[64,4,2176]{2,1,0:T(4,128)(2,1)}), bf16[64,4,2176]{2,1,0:T(4,128)(2,1)S(1)}, u32[]{:S(2)}, u32[]{:S(2)}) async-start(bf16[64,4,2176]{2,1,0:T(4,128)(2,1)} %pad_maximum_fusion), calls=%async_computation | async-start | bytes 2228224 | tf_op jit(solution)/shard_map/all_to_all | solution.py:117
  35.1 2.0 %fusion.21 = (f32[2048,64]{0,1:T(8,128)S(1)}, f32[2048,64]{0,1:T(8,128)S(1)}) fusion(), kind=kLoop, calls=%fused_computation.44 | loop fusion | flops 1835008 | bytes 1048576 | tf_op jit(solution)/shard_map/sin | solution.py:27
  37.2 1.1 fusion.27
  38.3 8.2 %add_convert_fusion = (bf16[2048,32,64]{0,2,1:T(8,128)(2,1)}, bf16[2048,32,64]{0,2,1:T(8,128)(2,1)}) fusion(f32[2048,64]{0,1:T(8,128)S(1)} %get-tuple-element.31, f32[2048,32]{0,1:T(8,128)S(1)} %get-tuple-element.28, f32[2048,64]{0,1:T(8,128)S(1)} %get-tuple-element.32, f32[2048,32]{0,1:T(8,128)S(1)} %get-tuple-element.27), kind=kLoop, calls=%fused_computation.1 | loop fusion | flops 33554432 | bytes 18350080 | tf_op jit(solution)/shard_map/convert_element_type | solution.py:29
  46.5 7.0 %all-to-all-done = bf16[64,4,2176]{2,1,0:T(4,128)(2,1)S(1)} async-done(((bf16[64,4,2176]{2,1,0:T(4,128)(2,1)}), bf16[64,4,2176]{2,1,0:T(4,128)(2,1)S(1)}, u32[]{:S(2)}, u32[]{:S(2)}) %all-to-all-start) | async-done | bytes 1114144 | tf_op jit(solution)/shard_map/all_to_all | solution.py:117
  57.1 0.7 convert_multiply_fusion.2
  58.3 0.7 tile.21
  59.5 0.7 tile.9
  60.5 1.8 %add_convert_fusion.1 = (bf16[128,2048]{1,0:T(8,128)(2,1)S(1)}, bf16[128,2048]{1,0:T(8,128)(2,1)S(1)}) fusion(f32[128,2048]{1,0:T(8,128)S(1)} %tile.21, bf16[128,2048]{1,0:T(8,128)(2,1)} %copy-done.1, f32[128,2048]{1,0:T(8,128)S(1)} %tile.9, bf16[128,2048]{1,0:T(8,128)(2,1)} %copy-done, f32[128]{0:T(128)S(1)} %mul.260), kind=kLoop, calls=%fused_computation.21 | loop fusion | flops 3145728 | bytes 4194816 | tf_op jit(solution)/shard_map/convert_element_type | solution.py:134
  62.3 5.9 %fusion.11 = f32[256,2048]{1,0:T(8,128)S(1)} fusion(bf16[2048,2048]{0,1:T(8,128)(2,1)} %bitcast.54, bf16[128,2048]{1,0:T(8,128)(2,1)S(1)} %get-tuple-element.16, bf16[128,2048]{1,0:T(8,128)(2,1)S(1)} %get-tuple-element.15), kind=kOutput, calls=%fused_computation.31 | convolution fusion | flops 2149580800 | bytes 11534336 | tf_op jit(solution)/shard_map/dot_general | solution.py:140
  68.3 2.4 %fusion.10 = f32[256,2048]{1,0:T(8,128)S(1)} fusion(bf16[2048,2048]{0,1:T(8,128)(2,1)S(1)} %bitcast.52, bf16[128,2048]{1,0:T(8,128)(2,1)S(1)} %get-tuple-element.16, bf16[128,2048]{1,0:T(8,128)(2,1)S(1)} %get-tuple-element.15), kind=kOutput, calls=%fused_computation.30 | convolution fusion | flops 2149580800 | bytes 11534336 | tf_op jit(solution)/shard_map/dot_general | solution.py:141
  71.1 2.6 %fusion.9 = f32[256,2048]{1,0:T(8,128)S(1)} fusion(bf16[2048,2048]{0,1:T(8,128)(2,1)S(1)} %bitcast.57, bf16[128,2048]{1,0:T(8,128)(2,1)S(1)} %get-tuple-element.12, bf16[128,2048]{1,0:T(8,128)(2,1)S(1)} %get-tuple-element.11), kind=kOutput, calls=%fused_computation.29 | convolution fusion | flops 2149580800 | bytes 11534336 | tf_op jit(solution)/shard_map/dot_general | solution.py:149
  73.7 2.4 %fusion.8 = f32[256,2048]{1,0:T(8,128)S(1)} fusion(bf16[2048,2048]{0,1:T(8,128)(2,1)S(1)} %bitcast.53, bf16[128,2048]{1,0:T(8,128)(2,1)S(1)} %get-tuple-element.12, bf16[128,2048]{1,0:T(8,128)(2,1)S(1)} %get-tuple-element.11), kind=kOutput, calls=%fused_computation.28 | convolution fusion | flops 2149580800 | bytes 11534336 | tf_op jit(solution)/shard_map/dot_general | solution.py:150
  76.5 0.7 reshape.247
  77.6 1.3 %copy.39 = bf16[2048,256]{1,0:T(8,128)(2,1)} copy(bf16[2048,256]{0,1:T(8,128)(2,1)S(1)} %bitcast.63) | data formatting | bytes 2097152 | tf_op jit(solution)/shard_map/transpose | solution.py:155
  78.9 4.8 %all-to-all-start.1 = ((bf16[64,32,256]{2,1,0:T(8,128)(2,1)}), bf16[64,32,256]{2,1,0:T(8,128)(2,1)S(1)}, u32[]{:S(2)}, u32[]{:S(2)}) async-start(bf16[64,32,256]{2,1,0:T(8,128)(2,1)} %bitcast.23), calls=%async_computation.1 | async-start | bytes 2097152 | tf_op jit(solution)/shard_map/all_to_all | solution.py:156
  83.8 0.7 dynamic-slice_convert_fusion
  84.5 2.0 %copy.41.m_ref = f32[4096,1]{1,0:T(8,128)} copy(f32[4096,1]{0,1:T(1,128)S(1)} %bitcast.66) | data formatting | bytes 32768 | tf_op jit(solution)/shard_map/convert_element_type | solution.py:162
  87.2 0.7 maximum_maximum_fusion.ph_ref
  87.8 14.3 %all-to-all-done.1 = bf16[64,32,256]{2,1,0:T(8,128)(2,1)S(1)} async-done(((bf16[64,32,256]{2,1,0:T(8,128)(2,1)}), bf16[64,32,256]{2,1,0:T(8,128)(2,1)S(1)}, u32[]{:S(2)}, u32[]{:S(2)}) %all-to-all-start.1) | async-done | bytes 1048608 | tf_op jit(solution)/shard_map/all_to_all | solution.py:156
  102.4 2.2 %copy.40 = bf16[32,2,64,128]{3,2,1,0:T(8,128)(2,1)} copy(bf16[32,2,64,128]{3,1,0,2:T(2,128)(2,1)S(1)} %bitcast.64) | data formatting | bytes 2097152 | tf_op jit(solution)/shard_map/transpose | solution.py:157
  104.6 5.2 %shard_map.73 = f32[4096,256]{1,0:T(8,128)} custom-call(bf16[4096,128]{1,0:T(8,128)(2,1)} %bitcast.60, bf16[128,512]{1,0:T(8,128)(2,1)} %maximum_maximum_fusion.ph_ref, f32[4096,1]{1,0:T(8,128)} %copy.41.m_ref), custom_call_target="tpu_custom_call" | custom-call | flops 536870912 | bytes 5259264 | tf_op jit(solution)/shard_map/pallas_call | solution.py:62
  (52 shorter events, 7.8 us)
Async XLA Ops:
  3.4 11.0 %collective-permute-start.1 = (f32[]{:T(128)}, f32[]{:T(128)}, u32[]{:S(2)}, u32[]{:S(2)}) collective-permute-start(f32[]{:T(128)} %add_reduce_fusion), channel_id=1, source_target_pairs={{0,2},{1,3},{2,0},{3,1},{4,6},{5,7},{6,4},{7,5},{8,10},{9,11},{10,... | collective-permute-start | bytes 20 | tf_op jit(solution)/shard_map/ppermute | solution.py:98
  11.1 3.4 %collective-permute-start.2 = (f32[]{:T(128)}, f32[]{:T(128)}, u32[]{:S(2)}, u32[]{:S(2)}) collective-permute-start(f32[]{:T(128)} %add_reduce_fusion), channel_id=1, source_target_pairs={{0,3},{1,0},{2,1},{3,2},{4,7},{5,4},{6,5},{7,6},{8,11},{9,8},{10,9... | collective-permute-start | bytes 20 | tf_op jit(solution)/shard_map/ppermute | solution.py:98
  11.1 4.8 %collective-permute-start = (f32[]{:T(128)}, f32[]{:T(128)}, u32[]{:S(2)}, u32[]{:S(2)}) collective-permute-start(f32[]{:T(128)} %add_reduce_fusion), channel_id=1, source_target_pairs={{0,1},{1,2},{2,3},{3,0},{4,5},{5,6},{6,7},{7,4},{8,9},{9,10},{10,1... | collective-permute-start | bytes 20 | tf_op jit(solution)/shard_map/ppermute | solution.py:98
  24.0 29.4 %all-to-all-start = ((bf16[64,4,2176]{2,1,0:T(4,128)(2,1)}), bf16[64,4,2176]{2,1,0:T(4,128)(2,1)S(1)}, u32[]{:S(2)}, u32[]{:S(2)}) async-start(bf16[64,4,2176]{2,1,0:T(4,128)(2,1)} %pad_maximum_fusion), calls=%async_computation | async-start | bytes 2228224 | tf_op jit(solution)/shard_map/all_to_all | solution.py:117
  55.7 2.1 %copy-start = (bf16[128,2048]{1,0:T(8,128)(2,1)}, bf16[128,2048]{1,0:T(8,128)(2,1)S(1)}, u32[]{:S(2)}) copy-start(bf16[128,2048]{1,0:T(8,128)(2,1)S(1)} %reshape_squeeze.6) | copy-start | bytes 1572868
  56.4 1.3 %copy-start.1 = (bf16[128,2048]{1,0:T(8,128)(2,1)}, bf16[128,2048]{1,0:T(8,128)(2,1)S(1)}, u32[]{:S(2)}) copy-start(bf16[128,2048]{1,0:T(8,128)(2,1)S(1)} %reshape_squeeze.7) | copy-start | bytes 1572868
  60.5 7.8 %slice-start = ((s8[8388608]{0:T(1024)(128)(4,1)}), s8[4194304]{0:T(1024)(128)(4,1)S(1)}, s32[]{:S(2)}) async-start(s8[8388608]{0:T(1024)(128)(4,1)} %bitcast.50), calls=%async_computation.2 | async-start | bytes 8388608
  62.3 5.9 %slice-start.1 = ((s8[8388608]{0:T(1024)(128)(4,1)}), s8[4194304]{0:T(1024)(128)(4,1)S(1)}, s32[]{:S(2)}) async-start(s8[8388608]{0:T(1024)(128)(4,1)} %bitcast.50), calls=%async_computation.3 | async-start | bytes 8388608
  62.3 8.7 %slice-start.2 = ((s8[8388608]{0:T(1024)(128)(4,1)}), s8[4194304]{0:T(1024)(128)(4,1)S(1)}, s32[]{:S(2)}) async-start(s8[8388608]{0:T(1024)(128)(4,1)} %bitcast.55), calls=%async_computation.4 | async-start | bytes 8388608
  68.2 2.4 %copy-start.2 = (f32[2048]{0:T(1024)S(1)}, f32[2048]{0:T(1024)}, u32[]{:S(2)}) copy-start(f32[2048]{0:T(1024)} %param.10) | copy-start | bytes 24580
  68.3 2.8 %slice-start.3 = ((s8[8388608]{0:T(1024)(128)(4,1)}), s8[4194304]{0:T(1024)(128)(4,1)S(1)}, s32[]{:S(2)}) async-start(s8[8388608]{0:T(1024)(128)(4,1)} %bitcast.55), calls=%async_computation.5 | async-start | bytes 8388608
  78.9 7.6 %copy-start.3 = (s32[64]{0:T(128)S(1)}, s32[64]{0:T(128)}, u32[]{:S(2)}) copy-start(s32[64]{0:T(128)} %param.12) | copy-start | bytes 772
  78.9 7.6 %copy-start.4 = (s32[64]{0:T(128)S(1)}, s32[64]{0:T(128)}, u32[]{:S(2)}) copy-start(s32[64]{0:T(128)} %param.11) | copy-start | bytes 772
  78.9 23.3 %all-to-all-start.1 = ((bf16[64,32,256]{2,1,0:T(8,128)(2,1)}), bf16[64,32,256]{2,1,0:T(8,128)(2,1)S(1)}, u32[]{:S(2)}, u32[]{:S(2)}) async-start(bf16[64,32,256]{2,1,0:T(8,128)(2,1)} %bitcast.23), calls=%async_computation.1 | async-start | bytes 2097152 | tf_op jit(solution)/shard_map/all_to_all | solution.py:156

commit v9 on v6

--- a/solution.py
+++ b/solution.py
@@ -10,22 +10,23 @@
 PHASE_Q = 1024
 
 
-def dft_table(length):
-    split = 64
+def wave_table(length, freqs):
+    split = 32
     hi_count = length // split
-    freq = jnp.arange(length, dtype=jnp.int32)[:, None]
     step = 2.0 * math.pi / length
-    hi_ang = ((freq * (split * jnp.arange(hi_count, dtype=jnp.int32)[None, :])) % length).astype(
+    cols = freqs[None, :]
+    hi_ang = ((split * jnp.arange(hi_count, dtype=jnp.int32)[:, None] * cols) % length).astype(
         jnp.float32
     ) * step
-    lo_ang = ((freq * jnp.arange(split, dtype=jnp.int32)[None, :]) % length).astype(
+    lo_ang = ((jnp.arange(split, dtype=jnp.int32)[:, None] * cols) % length).astype(
         jnp.float32
     ) * step
-    hi_c, hi_s = jnp.cos(hi_ang)[:, :, None], jnp.sin(hi_ang)[:, :, None]
-    lo_c, lo_s = jnp.cos(lo_ang)[:, None, :], jnp.sin(lo_ang)[:, None, :]
-    cos_t = (hi_c * lo_c - hi_s * lo_s).reshape(length, length).astype(jnp.bfloat16)
-    sin_t = (hi_c * lo_s + hi_s * lo_c).reshape(length, length).astype(jnp.bfloat16)
-    return lax.optimization_barrier((cos_t, sin_t))
+    hi_c, hi_s = jnp.cos(hi_ang)[:, None, :], jnp.sin(hi_ang)[:, None, :]
+    lo_c, lo_s = jnp.cos(lo_ang)[None, :, :], jnp.sin(lo_ang)[None, :, :]
+    count = freqs.shape[0]
+    cos_t = (hi_c * lo_c - hi_s * lo_s).reshape(length, count).astype(jnp.bfloat16)
+    sin_t = (hi_c * lo_s + hi_s * lo_c).reshape(length, count).astype(jnp.bfloat16)
+    return cos_t, sin_t
 
 
 def phase_tables(bperp, tdays):
@@ -77,7 +78,10 @@
     word = jnp.where(lane == 0, hi, jnp.where(lane == 1, mid, lo))
     word = jnp.broadcast_to(word.astype(jnp.bfloat16), (n_date, 2 * cols, 128))
 
-    both = jnp.stack([own_re.T, own_im.T]).reshape(2, cols, n_date, lines)
+    half = lines // 2
+    split_re = own_re.reshape(half, 2, rg_dev).transpose(1, 0, 2).reshape(lines, rg_dev)
+    split_im = own_im.reshape(half, 2, rg_dev).transpose(1, 0, 2).reshape(lines, rg_dev)
+    both = jnp.stack([split_re.T, split_im.T]).reshape(2, cols, n_date, lines)
     both = both.transpose(2, 0, 1, 3).reshape(n_date, 2 * cols, lines)
     both = jnp.concatenate([both, word], axis=2)
     got = lax.all_to_all(both, "date", split_axis=0, concat_axis=0, tiled=True)
@@ -100,22 +104,56 @@
     ifg_re = (a_re * ref_re + a_im * ref_im).astype(jnp.bfloat16)
     ifg_im = (a_im * ref_re - a_re * ref_im).astype(jnp.bfloat16)
 
-    cos_t, sin_t = dft_table(lines)
     rows = n_date * cols
+    quarter = half // 2
+    freq_order = jnp.concatenate(
+        [jnp.arange(0, half, 2, dtype=jnp.int32), jnp.arange(1, half, 2, dtype=jnp.int32)]
+    )
+    fwd_cos, fwd_sin = wave_table(half, freq_order)
+    inv_cos, inv_sin = wave_table(half, jnp.arange(half, dtype=jnp.int32))
+    fwd_cos, fwd_sin, inv_cos, inv_sin = lax.optimization_barrier(
+        (fwd_cos, fwd_sin, inv_cos, inv_sin)
+    )
+    fwd_ang = freq_order.astype(f32) * (2.0 * math.pi / lines)
+    inv_ang = jnp.arange(half, dtype=f32) * (2.0 * math.pi / lines)
+
+    def half_dft(x_even, x_odd, tab_cos, tab_sin, sign):
+        def one(x):
+            pc = jnp.dot(x, tab_cos, preferred_element_type=f32)
+            ps = jnp.dot(x, tab_sin, preferred_element_type=f32)
+            if sign < 0:
+                return pc[:rows] + ps[rows:], pc[rows:] - ps[:rows]
+            return pc[:rows] - ps[rows:], ps[:rows] + pc[rows:]
+
+        e_re, e_im = one(x_even)
+        o_re, o_im = one(x_odd)
+        ang = fwd_ang if sign < 0 else inv_ang
+        tw_re = jnp.cos(ang)[None, :]
+        tw_im = (sign * jnp.sin(ang))[None, :]
+        t_re = o_re * tw_re - o_im * tw_im
+        t_im = o_re * tw_im + o_im * tw_re
+        return (e_re + t_re, e_im + t_im), (e_re - t_re, e_im - t_im)
+
     stacked = jnp.concatenate([ifg_re, ifg_im], axis=0)
-    fc = jnp.dot(stacked, cos_t, preferred_element_type=f32)
-    fs = jnp.dot(stacked, sin_t, preferred_element_type=f32)
-    spec_re = fc[:rows] + fs[rows:]
-    spec_im = fc[rows:] - fs[:rows]
-    weights = gain[None, :]
-    held = jnp.concatenate(
-        [(spec_re * weights).astype(jnp.bfloat16), (spec_im * weights).astype(jnp.bfloat16)],
-        axis=0,
+    (lo_re, lo_im), (hi_re, hi_im) = half_dft(
+        stacked[:, :half], stacked[:, half:], fwd_cos, fwd_sin, -1
     )
-    bc = jnp.dot(held, cos_t, preferred_element_type=f32)
-    bs = jnp.dot(held, sin_t, preferred_element_type=f32)
-    filt_re = ((bc[:rows] - bs[rows:]) * (1.0 / lines)).astype(jnp.bfloat16)
-    filt_im = ((bs[:rows] + bc[rows:]) * (1.0 / lines)).astype(jnp.bfloat16)
+    spec_e_re = jnp.concatenate([lo_re[:, :quarter], hi_re[:, :quarter]], axis=1)
+    spec_e_im = jnp.concatenate([lo_im[:, :quarter], hi_im[:, :quarter]], axis=1)
+    spec_o_re = jnp.concatenate([lo_re[:, quarter:], hi_re[:, quarter:]], axis=1)
+    spec_o_im = jnp.concatenate([lo_im[:, quarter:], hi_im[:, quarter:]], axis=1)
+    gain_pairs = gain.reshape(half, 2)
+    w_e = gain_pairs[:, 0][None, :]
+    w_o = gain_pairs[:, 1][None, :]
+    held_e = jnp.concatenate(
+        [(spec_e_re * w_e).astype(jnp.bfloat16), (spec_e_im * w_e).astype(jnp.bfloat16)], axis=0
+    )
+    held_o = jnp.concatenate(
+        [(spec_o_re * w_o).astype(jnp.bfloat16), (spec_o_im * w_o).astype(jnp.bfloat16)], axis=0
+    )
+    (a_re, a_im), (b_re, b_im) = half_dft(held_e, held_o, inv_cos, inv_sin, 1)
+    filt_re = (jnp.concatenate([a_re, b_re], axis=1) * (1.0 / lines)).astype(jnp.bfloat16)
+    filt_im = (jnp.concatenate([a_im, b_im], axis=1) * (1.0 / lines)).astype(jnp.bfloat16)
 
     pair = jnp.concatenate([filt_re, filt_im], axis=0).reshape(2, n_date, cols, lines)
     pair = pair.transpose(2, 0, 1, 3).reshape(2 * rows, lines).T

time: 110 us -> 118 us (1.073)
  local copies, waits for them, and re-layouts: 14.6 us -> 27.2 us
  matrix products: 14.4 us -> 7.15 us
  waiting for transfers between devices: 25.3 us -> 26.7 us
    dot_general x4 -> x8, matrix products: 13.2 us -> 5.91 us  [the longest x4 3.07 us: one(): pc = jnp.dot(x, tab_cos, preferred_element_type=f32)]
    another operation x2, local copies, waits for them, and re-layouts: 1.22 us -> 4.43 us  [shards(): ref_re = jnp.tile(ref_re, (n_date, 1))]
    convert_element_type x4 -> x7, other arithmetic: 10.9 us -> 8.3 us  [the longest x2 5.83 us: wave_table(): (hi_c * lo_s + hi_s * lo_c).reshape(length, count).astype(jnp.bfloat16)]
    another operation x2, local copies, waits for them, and re-layouts: 1.22 us -> 3.45 us  [shards(): ref_im = jnp.tile(ref_im, (n_date, 1))]
    all_to_all x1, waiting for transfers between devices: 6.91 us -> 9.03 us  [shards(): got = lax.all_to_all(both, 'date', split_axis=0, concat_axis=0, tiled=True)]
    slice x1, local copies, waits for them, and re-layouts: 0.54 us -> 2.39 us  [shards(): x_im = got[:, 1].reshape(n_date * cols, lines)]
    transpose x0 -> x4, local copies, waits for them, and re-layouts: none -> 1.61 us  [the longest x1 1.11 us: shards(): own_im.reshape(half, 2, rg_dev).transpose(1, 0, 2).reshape(lines, rg_dev)]
    sin x1 -> x2, other arithmetic: 2.05 us -> 0.57 us  [the longest x1 0.53 us: wave_table(): lo_c, lo_s = (jnp.cos(lo_ang)[None, :, :], jnp.sin(lo_ang)[None, :, :])]
  transfers between devices with their start and end apart: 5 -> 5, of which waited for: 4 -> 3; matrix products, arithmetic and copies ran while one was open for 13% -> 11% of each run, Pallas kernels for 0% -> 0%
where the time goes in v9:
time: 118 us; the launch traced here: 117 us
  local copies, waits for them, and re-layouts  27.2 us (23%)
  other arithmetic  26.9 us (23%)
  waiting for transfers between devices  26.7 us (23%)
  starting transfers between devices  25 us (21%)
  matrix products  7.15 us (6%)
  between operations  3.75 us (3%)
    all_to_all x1, waiting for transfers between devices, shards(): got = lax.all_to_all(pair, 'date', split_axis=0, concat_axis=0, tiled=True)  17 us
    all_to_all x1, starting transfers between devices, shards(): got = lax.all_to_all(both, 'date', split_axis=0, concat_axis=0, tiled=True)  10.2 us
    ppermute x3, starting transfers between devices, shards(): lax.ppermute(local, 'rng', [(r, (r + k) % n_rng) for r in range(n_rng)])  10.1 us
    all_to_all x1, waiting for transfers between devices, shards(): got = lax.all_to_all(both, 'date', split_axis=0, concat_axis=0, tiled=True)  9.03 us
    convert_element_type x2, other arithmetic, wave_table(): (hi_c * lo_s + hi_s * lo_c).reshape(length, count).astype(jnp.bfloat16)  5.83 us
    all_to_all x1, starting transfers between devices, shards(): got = lax.all_to_all(pair, 'date', split_axis=0, concat_axis=0, tiled=True)  4.72 us
    another operation x2, local copies, waits for them, and re-layouts, shards(): ref_re = jnp.tile(ref_re, (n_date, 1))  4.43 us
    mul x1, other arithmetic, shards(): result = result * mask_px[:, None]  3.69 us
  transfers between devices with their start and end apart: 5, of which 3 were waited for; matrix products, arithmetic and copies ran while one was open for 11% of the time, Pallas kernels for 0%

profile of v9, /device:TPU:1, one launch (start us, length us, event | category | flops | bytes accessed | tf_op | source)
XLA Modules:
  0.0 116.7 jit_solution(17299556029114922886)
XLA Ops:
  0.0 2.1 %add_reduce_fusion = f32[]{:T(128)} fusion(bf16[1,2048,128]{2,1,0:T(8,128)(2,1)} %param.8, bf16[1,2048,128]{2,1,0:T(8,128)(2,1)} %param.7), kind=kLoop, calls=%fused_computation.24 | loop fusion | flops 1572863 | bytes 1048580 | tf_op jit(solution)/shard_map/reduce_sum | solution.py:62
  2.1 6.8 %collective-permute-start.2 = (f32[]{:T(128)}, f32[]{:T(128)}, u32[]{:S(2)}, u32[]{:S(2)}) collective-permute-start(f32[]{:T(128)} %add_reduce_fusion), channel_id=1, source_target_pairs={{0,3},{1,0},{2,1},{3,2},{4,7},{5,4},{6,5},{7,6},{8,11},{9,8},{10,9... | collective-permute-start | bytes 20 | tf_op jit(solution)/shard_map/ppermute | solution.py:65
  9.0 0.9 collective-permute-start.1
  9.9 2.4 %collective-permute-start = (f32[]{:T(128)}, f32[]{:T(128)}, u32[]{:S(2)}, u32[]{:S(2)}) collective-permute-start(f32[]{:T(128)} %add_reduce_fusion), channel_id=1, source_target_pairs={{0,1},{1,2},{2,3},{3,0},{4,5},{5,6},{6,7},{7,4},{8,9},{9,10},{10,1... | collective-permute-start | bytes 20 | tf_op jit(solution)/shard_map/ppermute | solution.py:65
  12.3 1.1 copy.34
  14.0 0.8 copy.36
  15.5 2.7 %pad_maximum_fusion.12 = f32[4]{0:T(128)S(1)} fusion(f32[1]{0:T(128)} %bitcast.15, f32[1]{0:T(128)} %bitcast.14, f32[1]{0:T(128)} %bitcast.13, f32[1]{0:T(128)} %bitcast.12), kind=kLoop, calls=%fused_computation.164 | loop fusion | flops 12 | bytes 32 | tf_op jit(solution)/shard_map/stack | solution.py:68
  22.1 1.6 %pad_maximum_fusion = bf16[64,4,2176]{2,1,0:T(4,128)(2,1)} fusion(bf16[64,4,2048]{2,1,0:T(4,128)(2,1)S(1)} %copy.36, bf16[2176]{0:T(1024)(128)(2,1)S(1)} %pad.27.clone), kind=kLoop, calls=%fused_computation.11 | loop fusion | flops 2228224 | bytes 2167040 | tf_op jit(solution)/shard_map/concatenate | solution.py:86
  23.7 10.2 %all-to-all-start = ((bf16[64,4,2176]{2,1,0:T(4,128)(2,1)}), bf16[64,4,2176]{2,1,0:T(4,128)(2,1)}, u32[]{:S(2)}, u32[]{:S(2)}) async-start(bf16[64,4,2176]{2,1,0:T(4,128)(2,1)} %pad_maximum_fusion), calls=%async_computation | async-start | bytes 2228224 | tf_op jit(solution)/shard_map/all_to_all | solution.py:87
  35.6 1.6 %fusion.61 = (f32[32,1024]{1,0:T(8,128)S(1)}, f32[32,1024]{1,0:T(8,128)S(1)}, f32[32,1024]{1,0:T(8,128)S(1)}, f32[32,1024]{1,0:T(8,128)S(1)}, f32[32,1024]{1,0:T(8,128)S(1)}, /*index=5*/f32[32,1024]{1,0:T(8,128)S(1)}) fusion(s32[32]{0:T(128)S(1)} %iota_multiply_fusion.2, s32[1024]{0:T(1024)S(1)} %pad_add_fusion), kind=kLoop, calls=%fused_computation.121 | loop fusion | flops 1376256 | bytes 790656 | tf_op jit(solution)/shard_map/cos | solution.py:24
  37.2 2.6 %add_convert_fusion = (bf16[32,32,1024]{2,1,0:T(8,128)(2,1)}, bf16[32,32,1024]{2,1,0:T(8,128)(2,1)S(1)}) fusion(f32[32,1024]{1,0:T(8,128)S(1)} %get-tuple-element.75, f32[32,1024]{1,0:T(8,128)S(1)} %get-tuple-element.66, f32[32,1024]{1,0:T(8,128)S(1)} %get-tuple-element.76, f32[32,1024]{1,0:T(8,128)S(1)} %get-tuple-element.65), kind=kLoop, calls=%fused_computation.6 | loop fusion | flops 8388608 | bytes 4718592 | tf_op jit(solution)/shard_map/convert_element_type | solution.py:28
  39.8 3.2 %add_convert_fusion.1 = (bf16[32,32,1024]{2,1,0:T(8,128)(2,1)}, bf16[32,32,1024]{2,1,0:T(8,128)(2,1)}) fusion(f32[32,1024]{1,0:T(8,128)S(1)} %get-tuple-element.68, f32[32,1024]{1,0:T(8,128)S(1)} %get-tuple-element.69, f32[32,1024]{1,0:T(8,128)S(1)} %get-tuple-element.67, f32[32,1024]{1,0:T(8,128)S(1)} %get-tuple-element.70), kind=kLoop, calls=%fused_computation.8 | loop fusion | flops 8388608 | bytes 4718592 | tf_op jit(solution)/shard_map/convert_element_type | solution.py:28
  43.7 9.0 %all-to-all-done = bf16[64,4,2176]{2,1,0:T(4,128)(2,1)} async-done(((bf16[64,4,2176]{2,1,0:T(4,128)(2,1)}), bf16[64,4,2176]{2,1,0:T(4,128)(2,1)}, u32[]{:S(2)}, u32[]{:S(2)}) %all-to-all-start) | async-done | bytes 1114144 | tf_op jit(solution)/shard_map/all_to_all | solution.py:87
  52.7 1.7 %slice.166 = bf16[64,4,2048]{2,1,0:T(4,128)(2,1)S(1)} slice(bf16[64,4,2176]{2,1,0:T(4,128)(2,1)} %all-to-all-done), slice={[0:64], [0:4], [0:2048]} | slice | bytes 2097152 | tf_op jit(solution)/shard_map/slice | solution.py:91
  55.0 0.9 fusion.90
  56.6 0.9 slice_convert_fusion
  58.0 2.4 %copy.39 = bf16[64,1,2,2048]{3,2,0,1:T(2,128)(2,1)} copy(bf16[64,1,2,2048]{3,0,2,1:T(8,128)(2,1)} %get-tuple-element.36) | data formatting | bytes 1048576 | tf_op jit(solution)/shard_map/slice | solution.py:93
  60.3 1.2 %reshape_squeeze.15 = bf16[128,2048]{1,0:T(8,128)(2,1)S(1)} reshape(bf16[64,1,2,2048]{3,2,0,1:T(2,128)(2,1)} %copy.39) | data formatting | bytes 1048576 | tf_op jit(solution)/shard_map/reshape;squeeze | solution.py:93
  62.9 1.5 %tile.20 = f32[64,2,2048]{2,1,0:T(2,128)} broadcast(f32[2,2048]{1,0:T(2,128)S(1)} %get-tuple-element.77), dimensions={1,2} | broadcast | bytes 1064960 | tf_op jit(solution)/shard_map/tile | solution.py:100
  64.4 1.9 %tile.21 = f32[128,2048]{1,0:T(8,128)S(1)} reshape(f32[64,2,2048]{2,1,0:T(2,128)} %tile.20) | data formatting | bytes 2097152 | tf_op jit(solution)/shard_map/tile | solution.py:100
  66.4 1.5 %tile.8 = f32[64,2,2048]{2,1,0:T(2,128)} broadcast(f32[2,2048]{1,0:T(2,128)S(1)} %get-tuple-element.78), dimensions={1,2} | broadcast | bytes 1064960 | tf_op jit(solution)/shard_map/tile | solution.py:99
  67.9 2.9 %tile.9 = f32[128,2048]{1,0:T(8,128)} reshape(f32[64,2,2048]{2,1,0:T(2,128)} %tile.8) | data formatting | bytes 2097152 | tf_op jit(solution)/shard_map/tile | solution.py:99
  70.8 2.1 %subtract_convert_fusion.2 = (bf16[128,2048]{1,0:T(8,128)(2,1)S(1)}, bf16[128,2048]{1,0:T(8,128)(2,1)S(1)}) fusion(f32[128,2048]{1,0:T(8,128)S(1)} %tile.21, f32[128,2048]{1,0:T(8,128)} %tile.9, bf16[128,2048]{1,0:T(8,128)(2,1)} %copy-done.4, bf16[128,2048]{1,0:T(8,128)(2,1)} %copy-done.3, f32[128]{0:T(128)S(1)} %mul.518), kind=kLoop, calls=%fused_computation.20 | loop fusion | flops 3145728 | bytes 4194816 | tf_op jit(solution)/shard_map/convert_element_type | solution.py:105
  73.7 0.9 fusion.51
  78.1 1.4 %copy-done = bf16[32,32,1024]{2,1,0:T(8,128)(2,1)S(1)} copy-done((bf16[32,32,1024]{2,1,0:T(8,128)(2,1)S(1)}, bf16[32,32,1024]{2,1,0:T(8,128)(2,1)}, u32[]{:S(2)}) %copy-start) | copy-done | bytes 2097176
  84.8 1.3 %copy.41 = bf16[2048,256]{1,0:T(8,128)(2,1)} copy(bf16[2048,256]{0,1:T(8,128)(2,1)S(1)} %bitcast.73) | data formatting | bytes 2097152 | tf_op jit(solution)/shard_map/transpose | solution.py:159
  86.1 4.7 %all-to-all-start.1 = ((bf16[64,32,256]{2,1,0:T(8,128)(2,1)}), bf16[64,32,256]{2,1,0:T(8,128)(2,1)S(1)}, u32[]{:S(2)}, u32[]{:S(2)}) async-start(bf16[64,32,256]{2,1,0:T(8,128)(2,1)} %bitcast.29), calls=%async_computation.1 | async-start | bytes 2097152 | tf_op jit(solution)/shard_map/all_to_all | solution.py:160
  92.2 17.0 %all-to-all-done.1 = bf16[64,32,256]{2,1,0:T(8,128)(2,1)S(1)} async-done(((bf16[64,32,256]{2,1,0:T(8,128)(2,1)}), bf16[64,32,256]{2,1,0:T(8,128)(2,1)S(1)}, u32[]{:S(2)}, u32[]{:S(2)}) %all-to-all-start.1) | async-done | bytes 1048608 | tf_op jit(solution)/shard_map/all_to_all | solution.py:160
  109.5 0.9 multiply_reduce_fusion
  110.4 1.2 %copy.42 = bf16[64,32,2,128]{3,0,2,1:T(8,128)(2,1)S(1)} copy(bf16[64,32,2,128]{3,2,1,0:T(2,128)(2,1)S(1)} %reshape.433) | data formatting | bytes 2097152 | tf_op jit(solution)/shard_map/reshape | solution.py:161
  111.8 1.2 %fusion.34 = f32[4096,512]{1,0:T(8,128)S(1)} fusion(bf16[4096,128]{1,0:T(8,128)(2,1)S(1)} %bitcast.70, bf16[64,256]{1,0:T(8,128)(2,1)S(1)} %get-tuple-element.60, bf16[64,256]{1,0:T(8,128)(2,1)S(1)} %get-tuple-element.59, bf16[64,256]{1,0:T(8,128)(2,1)S(1)} %fusion.83), kind=kOutput, calls=%fused_computation.89 | convolution fusion | flops 537395200 | bytes 9535488 | tf_op jit(solution)/shard_map/dot_general | solution.py:166
  113.0 3.7 %fusion.2 = f32[4096,256]{1,0:T(8,128)} fusion(f32[4096,512]{1,0:T(8,128)S(1)} %fusion.34, f32[4096]{0:T(1024)S(1)} %convert_bitcast_fusion, f32[4096]{0:T(1024)S(1)} %mul.600), kind=kLoop, calls=%fused_computation.4 | loop fusion | flops 5242880 | bytes 12615680 | tf_op jit(solution)/shard_map/mul | solution.py:176
  (75 shorter events, 18.4 us)
Async XLA Ops:
  0.0 13.6 %copy-start.5 = (bf16[1,2048,128]{2,1,0:T(8,128)(2,1)S(1)}, bf16[1,2048,128]{2,1,0:T(8,128)(2,1)}, u32[]{:S(2)}) copy-start(bf16[1,2048,128]{2,1,0:T(8,128)(2,1)} %param.7) | copy-start | bytes 1572868
  2.1 12.7 %collective-permute-start.2 = (f32[]{:T(128)}, f32[]{:T(128)}, u32[]{:S(2)}, u32[]{:S(2)}) collective-permute-start(f32[]{:T(128)} %add_reduce_fusion), channel_id=1, source_target_pairs={{0,3},{1,0},{2,1},{3,2},{4,7},{5,4},{6,5},{7,6},{8,11},{9,8},{10,9... | collective-permute-start | bytes 20 | tf_op jit(solution)/shard_map/ppermute | solution.py:65
  9.0 6.6 %collective-permute-start.1 = (f32[]{:T(128)}, f32[]{:T(128)}, u32[]{:S(2)}, u32[]{:S(2)}) collective-permute-start(f32[]{:T(128)} %add_reduce_fusion), channel_id=1, source_target_pairs={{0,2},{1,3},{2,0},{3,1},{4,6},{5,7},{6,4},{7,5},{8,10},{9,11},{10,... | collective-permute-start | bytes 20 | tf_op jit(solution)/shard_map/ppermute | solution.py:65
  9.9 5.7 %collective-permute-start = (f32[]{:T(128)}, f32[]{:T(128)}, u32[]{:S(2)}, u32[]{:S(2)}) collective-permute-start(f32[]{:T(128)} %add_reduce_fusion), channel_id=1, source_target_pairs={{0,1},{1,2},{2,3},{3,0},{4,5},{5,6},{6,7},{7,4},{8,9},{9,10},{10,1... | collective-permute-start | bytes 20 | tf_op jit(solution)/shard_map/ppermute | solution.py:65
  22.1 12.5 %copy-start.6 = (f32[2048]{0:T(1024)S(1)}, f32[2048]{0:T(1024)}, u32[]{:S(2)}) copy-start(f32[2048]{0:T(1024)} %param.10) | copy-start | bytes 24580
  23.7 29.0 %all-to-all-start = ((bf16[64,4,2176]{2,1,0:T(4,128)(2,1)}), bf16[64,4,2176]{2,1,0:T(4,128)(2,1)}, u32[]{:S(2)}, u32[]{:S(2)}) async-start(bf16[64,4,2176]{2,1,0:T(4,128)(2,1)} %pad_maximum_fusion), calls=%async_computation | async-start | bytes 2228224 | tf_op jit(solution)/shard_map/all_to_all | solution.py:87
  56.6 6.3 %copy-start.3 = (bf16[128,2048]{1,0:T(8,128)(2,1)}, bf16[128,2048]{1,0:T(8,128)(2,1)S(1)}, u32[]{:S(2)}) copy-start(bf16[128,2048]{1,0:T(8,128)(2,1)S(1)} %reshape_squeeze.14) | copy-start | bytes 1572868
  61.6 1.3 %copy-start.4 = (bf16[128,2048]{1,0:T(8,128)(2,1)}, bf16[128,2048]{1,0:T(8,128)(2,1)S(1)}, u32[]{:S(2)}) copy-start(bf16[128,2048]{1,0:T(8,128)(2,1)S(1)} %reshape_squeeze.15) | copy-start | bytes 1572868
  70.8 2.2 %copy-start.2 = (bf16[32,32,1024]{2,1,0:T(8,128)(2,1)S(1)}, bf16[32,32,1024]{2,1,0:T(8,128)(2,1)}, u32[]{:S(2)}) copy-start(bf16[32,32,1024]{2,1,0:T(8,128)(2,1)} %get-tuple-element.48) | copy-start | bytes 6291460
  73.7 1.6 %copy-start.1 = (bf16[32,32,1024]{2,1,0:T(8,128)(2,1)S(1)}, bf16[32,32,1024]{2,1,0:T(8,128)(2,1)}, u32[]{:S(2)}) copy-start(bf16[32,32,1024]{2,1,0:T(8,128)(2,1)} %get-tuple-element.47) | copy-start | bytes 6291460
  77.9 1.6 %copy-start = (bf16[32,32,1024]{2,1,0:T(8,128)(2,1)S(1)}, bf16[32,32,1024]{2,1,0:T(8,128)(2,1)}, u32[]{:S(2)}) copy-start(bf16[32,32,1024]{2,1,0:T(8,128)(2,1)} %get-tuple-element.45) | copy-start | bytes 6291460
  84.8 6.8 %copy-start.7 = (s32[64]{0:T(128)S(1)}, s32[64]{0:T(128)}, u32[]{:S(2)}) copy-start(s32[64]{0:T(128)} %param.12) | copy-start | bytes 772
  84.8 6.8 %copy-start.8 = (s32[64]{0:T(128)S(1)}, s32[64]{0:T(128)}, u32[]{:S(2)}) copy-start(s32[64]{0:T(128)} %param.11) | copy-start | bytes 772
  86.1 23.1 %all-to-all-start.1 = ((bf16[64,32,256]{2,1,0:T(8,128)(2,1)}), bf16[64,32,256]{2,1,0:T(8,128)(2,1)S(1)}, u32[]{:S(2)}, u32[]{:S(2)}) async-start(bf16[64,32,256]{2,1,0:T(8,128)(2,1)} %bitcast.29), calls=%async_computation.1 | async-start | bytes 2097152 | tf_op jit(solution)/shard_map/all_to_all | solution.py:160

commit v10 on v6

--- a/solution.py
+++ b/solution.py
@@ -59,16 +59,11 @@
     wide_re = own_re.astype(f32)
     wide_im = own_im.astype(f32)
     local = jnp.sum(wide_re * wide_re + wide_im * wide_im)
-    rng_me = lax.axis_index("rng")
-    received = [local] + [
-        lax.ppermute(local, "rng", [(r, (r + k) % n_rng) for r in range(n_rng)])
-        for k in range(1, n_rng)
-    ]
-    by_shift = jnp.stack(received)
-    by_source = by_shift[(rng_me - jnp.arange(n_rng)) % n_rng]
-    own_sum = by_source[0]
+    own_sum = local
     for k in range(1, n_rng):
-        own_sum = own_sum + by_source[k]
+        own_sum = own_sum + lax.ppermute(
+            local, "rng", [(r, (r + k) % n_rng) for r in range(n_rng)]
+        )
     lane = jnp.arange(128)
     word = jnp.where(lane < 3, own_sum, 0.0)
     hi = lax.reduce_precision(word, exponent_bits=8, mantissa_bits=7)

time: 110 us -> 105 us (0.955)
  other arithmetic: 26.2 us -> 23.4 us
  waiting for transfers between devices: 25.3 us -> 23.9 us
  local copies, waits for them, and re-layouts: 14.6 us -> 13.2 us
    another operation x1 -> x0, other arithmetic: 2.65 us -> none  [shards(): by_shift = jnp.stack(received)]
    ppermute x3, waiting for transfers between devices: 1.45 us -> 0.01 us  [shards(): lax.ppermute(local, 'rng', [(r, (r + k) % n_rng) for r in range(n_rng)])]
    ppermute x3, starting transfers between devices: 10.1 us -> 11.3 us  [shards(): lax.ppermute(local, 'rng', [(r, (r + k) % n_rng) for r in range(n_rng)])]
  transfers between devices with their start and end apart: 5 -> 5, of which waited for: 4 -> 2; matrix products, arithmetic and copies ran while one was open for 13% -> 13% of each run, Pallas kernels for 0% -> 0%
where the time goes in v10:
time: 105 us; the launch traced here: 104 us
  starting transfers between devices  25.5 us (24%)
  waiting for transfers between devices  23.9 us (23%)
  other arithmetic  23.4 us (22%)
  matrix products  14.4 us (14%)
  local copies, waits for them, and re-layouts  13.2 us (13%)
  between operations  3.64 us (3%)
    all_to_all x1, waiting for transfers between devices, shards(): got = lax.all_to_all(pair, 'date', split_axis=0, concat_axis=0, tiled=True)  17 us
    ppermute x3, starting transfers between devices, shards(): lax.ppermute(local, 'rng', [(r, (r + k) % n_rng) for r in range(n_rng)])  11.3 us
    all_to_all x1, starting transfers between devices, shards(): got = lax.all_to_all(both, 'date', split_axis=0, concat_axis=0, tiled=True)  9.45 us
    convert_element_type x1, other arithmetic, dft_table(): (hi_c * lo_s + hi_s * lo_c).reshape(length, length).astype(jnp.bfloat16)  8.23 us
    all_to_all x1, waiting for transfers between devices, shards(): got = lax.all_to_all(both, 'date', split_axis=0, concat_axis=0, tiled=True)  6.94 us
    dot_general x1, matrix products, shards(): fc = jnp.dot(stacked, cos_t, preferred_element_type=f32)  5.89 us
    all_to_all x1, starting transfers between devices, shards(): got = lax.all_to_all(pair, 'date', split_axis=0, concat_axis=0, tiled=True)  4.7 us
    mul x1, other arithmetic, shards(): result = result * mask_px[:, None]  3.69 us
  transfers between devices with their start and end apart: 5, of which 2 were waited for; matrix products, arithmetic and copies ran while one was open for 13% of the time, Pallas kernels for 0%

profile of v10, /device:TPU:1, one launch (start us, length us, event | category | flops | bytes accessed | tf_op | source)
XLA Modules:
  0.0 104.1 jit_solution(4304165682699852834)
XLA Ops:
  0.0 1.2 %copy.29 = bf16[1,2048,128]{1,2,0:T(8,128)(2,1)S(1)} copy(bf16[1,2048,128]{2,1,0:T(8,128)(2,1)} %param.7) | data formatting | bytes 1048576 | tf_op args[0]
  1.3 1.2 %copy.30 = bf16[1,2048,128]{1,2,0:T(8,128)(2,1)S(1)} copy(bf16[1,2048,128]{2,1,0:T(8,128)(2,1)} %param.8) | data formatting | bytes 1048576 | tf_op args[1]
  2.5 0.9 add_reduce_fusion
  3.4 3.8 %collective-permute-start = (f32[]{:T(128)}, f32[]{:T(128)}, u32[]{:S(2)}, u32[]{:S(2)}) collective-permute-start(f32[]{:T(128)} %add_reduce_fusion), channel_id=1, source_target_pairs={{0,1},{1,2},{2,3},{3,0},{4,5},{5,6},{6,7},{7,4},{8,9},{9,10},{10,1... | collective-permute-start | bytes 20 | tf_op jit(solution)/shard_map/ppermute | solution.py:64
  7.2 5.1 %collective-permute-start.1 = (f32[]{:T(128)}, f32[]{:T(128)}, u32[]{:S(2)}, u32[]{:S(2)}) collective-permute-start(f32[]{:T(128)} %add_reduce_fusion), channel_id=1, source_target_pairs={{0,2},{1,3},{2,0},{3,1},{4,6},{5,7},{6,4},{7,5},{8,10},{9,11},{10,... | collective-permute-start | bytes 20 | tf_op jit(solution)/shard_map/ppermute | solution.py:64
  12.3 2.4 %collective-permute-start.2 = (f32[]{:T(128)}, f32[]{:T(128)}, u32[]{:S(2)}, u32[]{:S(2)}) collective-permute-start(f32[]{:T(128)} %add_reduce_fusion), channel_id=1, source_target_pairs={{0,3},{1,0},{2,1},{3,2},{4,7},{5,4},{6,5},{7,6},{8,11},{9,8},{10,9... | collective-permute-start | bytes 20 | tf_op jit(solution)/shard_map/ppermute | solution.py:64
  14.8 0.8 copy.31
  18.2 1.6 %pad_maximum_fusion = bf16[64,4,2176]{2,1,0:T(4,128)(2,1)} fusion(bf16[64,4,2048]{2,1,0:T(4,128)(2,1)S(1)} %copy.31, bf16[2176]{0:T(1024)(128)(2,1)S(1)} %pad.11.clone), kind=kLoop, calls=%fused_computation.8 | loop fusion | flops 2228224 | bytes 2167040 | tf_op jit(solution)/shard_map/concatenate | solution.py:77
  19.7 9.5 %all-to-all-start = ((bf16[64,4,2176]{2,1,0:T(4,128)(2,1)}), bf16[64,4,2176]{2,1,0:T(4,128)(2,1)S(1)}, u32[]{:S(2)}, u32[]{:S(2)}) async-start(bf16[64,4,2176]{2,1,0:T(4,128)(2,1)} %pad_maximum_fusion), calls=%async_computation | async-start | bytes 2228224 | tf_op jit(solution)/shard_map/all_to_all | solution.py:78
  29.9 2.0 %fusion.24 = (f32[2048,64]{0,1:T(8,128)S(1)}, f32[2048,64]{0,1:T(8,128)S(1)}) fusion(), kind=kLoop, calls=%fused_computation.49 | loop fusion | flops 1835008 | bytes 1048576 | tf_op jit(solution)/shard_map/sin | solution.py:25
  31.9 1.1 %fusion.38 = (f32[2048,32]{0,1:T(8,128)S(1)}, f32[2048,32]{0,1:T(8,128)S(1)}) fusion(s32[32]{0:T(128)S(1)} %iota_multiply_fusion), kind=kLoop, calls=%fused_computation.63 | loop fusion | flops 917504 | bytes 524416 | tf_op jit(solution)/shard_map/cos | solution.py:24
  33.0 8.2 %add_convert_fusion = (bf16[2048,32,64]{0,2,1:T(8,128)(2,1)}, bf16[2048,32,64]{0,2,1:T(8,128)(2,1)}) fusion(f32[2048,64]{0,1:T(8,128)S(1)} %get-tuple-element.25, f32[2048,32]{0,1:T(8,128)S(1)} %get-tuple-element.24, f32[2048,64]{0,1:T(8,128)S(1)} %get-tuple-element.26, f32[2048,32]{0,1:T(8,128)S(1)} %get-tuple-element.23), kind=kLoop, calls=%fused_computation | loop fusion | flops 33554432 | bytes 18350080 | tf_op jit(solution)/shard_map/convert_element_type | solution.py:27
  41.2 6.9 %all-to-all-done = bf16[64,4,2176]{2,1,0:T(4,128)(2,1)S(1)} async-done(((bf16[64,4,2176]{2,1,0:T(4,128)(2,1)}), bf16[64,4,2176]{2,1,0:T(4,128)(2,1)S(1)}, u32[]{:S(2)}, u32[]{:S(2)}) %all-to-all-start) | async-done | bytes 1114144 | tf_op jit(solution)/shard_map/all_to_all | solution.py:78
  48.4 0.6 slice.68
  49.0 0.6 copy.38
  51.8 0.6 convert_multiply_fusion.2
  52.9 0.7 tile.21
  54.1 0.7 tile.9
  55.1 1.8 %add_convert_fusion.1 = (bf16[128,2048]{1,0:T(8,128)(2,1)S(1)}, bf16[128,2048]{1,0:T(8,128)(2,1)S(1)}) fusion(f32[128,2048]{1,0:T(8,128)S(1)} %tile.21, bf16[128,2048]{1,0:T(8,128)(2,1)} %copy-done.1, f32[128,2048]{1,0:T(8,128)S(1)} %tile.9, bf16[128,2048]{1,0:T(8,128)(2,1)} %copy-done, f32[128]{0:T(128)S(1)} %mul.288), kind=kLoop, calls=%fused_computation.26 | loop fusion | flops 3145728 | bytes 4194816 | tf_op jit(solution)/shard_map/convert_element_type | solution.py:95
  56.9 5.9 %fusion.14 = f32[256,2048]{1,0:T(8,128)S(1)} fusion(bf16[2048,2048]{0,1:T(8,128)(2,1)} %bitcast.51, bf16[128,2048]{1,0:T(8,128)(2,1)S(1)} %get-tuple-element.16, bf16[128,2048]{1,0:T(8,128)(2,1)S(1)} %get-tuple-element.15), kind=kOutput, calls=%fused_computation.36 | convolution fusion | flops 2149580800 | bytes 11534336 | tf_op jit(solution)/shard_map/dot_general | solution.py:101
  62.9 2.4 %fusion.13 = f32[256,2048]{1,0:T(8,128)S(1)} fusion(bf16[2048,2048]{0,1:T(8,128)(2,1)S(1)} %bitcast.49, bf16[128,2048]{1,0:T(8,128)(2,1)S(1)} %get-tuple-element.16, bf16[128,2048]{1,0:T(8,128)(2,1)S(1)} %get-tuple-element.15), kind=kOutput, calls=%fused_computation.35 | convolution fusion | flops 2149580800 | bytes 11534336 | tf_op jit(solution)/shard_map/dot_general | solution.py:102
  65.7 2.6 %fusion.12 = f32[256,2048]{1,0:T(8,128)S(1)} fusion(bf16[2048,2048]{0,1:T(8,128)(2,1)S(1)} %bitcast.54, bf16[128,2048]{1,0:T(8,128)(2,1)S(1)} %get-tuple-element.12, bf16[128,2048]{1,0:T(8,128)(2,1)S(1)} %get-tuple-element.11), kind=kOutput, calls=%fused_computation.34 | convolution fusion | flops 2149580800 | bytes 11534336 | tf_op jit(solution)/shard_map/dot_general | solution.py:110
  68.3 2.4 %fusion.11 = f32[256,2048]{1,0:T(8,128)S(1)} fusion(bf16[2048,2048]{0,1:T(8,128)(2,1)S(1)} %bitcast.50, bf16[128,2048]{1,0:T(8,128)(2,1)S(1)} %get-tuple-element.12, bf16[128,2048]{1,0:T(8,128)(2,1)S(1)} %get-tuple-element.11), kind=kOutput, calls=%fused_computation.33 | convolution fusion | flops 2149580800 | bytes 11534336 | tf_op jit(solution)/shard_map/dot_general | solution.py:111
  71.1 0.7 reshape.203
  72.2 1.3 %copy.36 = bf16[2048,256]{1,0:T(8,128)(2,1)} copy(bf16[2048,256]{0,1:T(8,128)(2,1)S(1)} %bitcast.60) | data formatting | bytes 2097152 | tf_op jit(solution)/shard_map/transpose | solution.py:116
  73.5 4.7 %all-to-all-start.1 = ((bf16[64,32,256]{2,1,0:T(8,128)(2,1)}), bf16[64,32,256]{2,1,0:T(8,128)(2,1)S(1)}, u32[]{:S(2)}, u32[]{:S(2)}) async-start(bf16[64,32,256]{2,1,0:T(8,128)(2,1)} %bitcast.17), calls=%async_computation.1 | async-start | bytes 2097152 | tf_op jit(solution)/shard_map/all_to_all | solution.py:117
  78.3 0.7 convert_bitcast_fusion
  79.7 17.0 %all-to-all-done.1 = bf16[64,32,256]{2,1,0:T(8,128)(2,1)S(1)} async-done(((bf16[64,32,256]{2,1,0:T(8,128)(2,1)}), bf16[64,32,256]{2,1,0:T(8,128)(2,1)S(1)}, u32[]{:S(2)}, u32[]{:S(2)}) %all-to-all-start.1) | async-done | bytes 1048608 | tf_op jit(solution)/shard_map/all_to_all | solution.py:117
  96.9 1.2 %copy.37 = bf16[64,32,2,128]{3,0,2,1:T(8,128)(2,1)S(1)} copy(bf16[64,32,2,128]{3,2,1,0:T(2,128)(2,1)S(1)} %reshape.205) | data formatting | bytes 2097152 | tf_op jit(solution)/shard_map/reshape | solution.py:118
  98.2 0.9 multiply_reduce_fusion
  99.2 1.2 %fusion.29 = f32[4096,512]{1,0:T(8,128)S(1)} fusion(bf16[4096,128]{1,0:T(8,128)(2,1)S(1)} %bitcast.55, bf16[64,256]{1,0:T(8,128)(2,1)S(1)} %get-tuple-element.22, bf16[64,256]{1,0:T(8,128)(2,1)S(1)} %get-tuple-element.21, bf16[64,256]{1,0:T(8,128)(2,1)S(1)} %fusion.54), kind=kOutput, calls=%fused_computation.54 | convolution fusion | flops 537395200 | bytes 9535488 | tf_op jit(solution)/shard_map/dot_general | solution.py:123
  100.4 3.7 %fusion.2 = f32[4096,256]{1,0:T(8,128)} fusion(f32[4096,512]{1,0:T(8,128)S(1)} %fusion.29, f32[4096]{0:T(1024)S(1)} %convert_bitcast_fusion, f32[4096]{0:T(1024)S(1)} %mul.337), kind=kLoop, calls=%fused_computation.5 | loop fusion | flops 5242880 | bytes 12615680 | tf_op jit(solution)/shard_map/mul | solution.py:133
  (49 shorter events, 6.0 us)
Async XLA Ops:
  3.4 12.2 %collective-permute-start = (f32[]{:T(128)}, f32[]{:T(128)}, u32[]{:S(2)}, u32[]{:S(2)}) collective-permute-start(f32[]{:T(128)} %add_reduce_fusion), channel_id=1, source_target_pairs={{0,1},{1,2},{2,3},{3,0},{4,5},{5,6},{6,7},{7,4},{8,9},{9,10},{10,1... | collective-permute-start | bytes 20 | tf_op jit(solution)/shard_map/ppermute | solution.py:64
  7.2 9.7 %collective-permute-start.1 = (f32[]{:T(128)}, f32[]{:T(128)}, u32[]{:S(2)}, u32[]{:S(2)}) collective-permute-start(f32[]{:T(128)} %add_reduce_fusion), channel_id=1, source_target_pairs={{0,2},{1,3},{2,0},{3,1},{4,6},{5,7},{6,4},{7,5},{8,10},{9,11},{10,... | collective-permute-start | bytes 20 | tf_op jit(solution)/shard_map/ppermute | solution.py:64
  12.3 5.2 %collective-permute-start.2 = (f32[]{:T(128)}, f32[]{:T(128)}, u32[]{:S(2)}, u32[]{:S(2)}) collective-permute-start(f32[]{:T(128)} %add_reduce_fusion), channel_id=1, source_target_pairs={{0,3},{1,0},{2,1},{3,2},{4,7},{5,4},{6,5},{7,6},{8,11},{9,8},{10,9... | collective-permute-start | bytes 20 | tf_op jit(solution)/shard_map/ppermute | solution.py:64
  19.7 28.4 %all-to-all-start = ((bf16[64,4,2176]{2,1,0:T(4,128)(2,1)}), bf16[64,4,2176]{2,1,0:T(4,128)(2,1)S(1)}, u32[]{:S(2)}, u32[]{:S(2)}) async-start(bf16[64,4,2176]{2,1,0:T(4,128)(2,1)} %pad_maximum_fusion), calls=%async_computation | async-start | bytes 2228224 | tf_op jit(solution)/shard_map/all_to_all | solution.py:78
  50.4 1.9 %copy-start = (bf16[128,2048]{1,0:T(8,128)(2,1)}, bf16[128,2048]{1,0:T(8,128)(2,1)S(1)}, u32[]{:S(2)}) copy-start(bf16[128,2048]{1,0:T(8,128)(2,1)S(1)} %reshape_squeeze.6) | copy-start | bytes 1572868
  51.2 1.2 %copy-start.1 = (bf16[128,2048]{1,0:T(8,128)(2,1)}, bf16[128,2048]{1,0:T(8,128)(2,1)S(1)}, u32[]{:S(2)}) copy-start(bf16[128,2048]{1,0:T(8,128)(2,1)S(1)} %reshape_squeeze.7) | copy-start | bytes 1572868
  55.1 7.8 %slice-start = ((s8[8388608]{0:T(1024)(128)(4,1)}), s8[4194304]{0:T(1024)(128)(4,1)S(1)}, s32[]{:S(2)}) async-start(s8[8388608]{0:T(1024)(128)(4,1)} %bitcast.47), calls=%async_computation.2 | async-start | bytes 8388608
  56.9 5.9 %slice-start.1 = ((s8[8388608]{0:T(1024)(128)(4,1)}), s8[4194304]{0:T(1024)(128)(4,1)S(1)}, s32[]{:S(2)}) async-start(s8[8388608]{0:T(1024)(128)(4,1)} %bitcast.47), calls=%async_computation.3 | async-start | bytes 8388608
  56.9 8.7 %slice-start.2 = ((s8[8388608]{0:T(1024)(128)(4,1)}), s8[4194304]{0:T(1024)(128)(4,1)S(1)}, s32[]{:S(2)}) async-start(s8[8388608]{0:T(1024)(128)(4,1)} %bitcast.52), calls=%async_computation.4 | async-start | bytes 8388608
  62.8 2.4 %copy-start.2 = (f32[2048]{0:T(1024)S(1)}, f32[2048]{0:T(1024)}, u32[]{:S(2)}) copy-start(f32[2048]{0:T(1024)} %param.10) | copy-start | bytes 24580
  62.9 2.8 %slice-start.3 = ((s8[8388608]{0:T(1024)(128)(4,1)}), s8[4194304]{0:T(1024)(128)(4,1)S(1)}, s32[]{:S(2)}) async-start(s8[8388608]{0:T(1024)(128)(4,1)} %bitcast.52), calls=%async_computation.5 | async-start | bytes 8388608
  71.1 7.9 %copy-start.3 = (s32[64]{0:T(128)S(1)}, s32[64]{0:T(128)}, u32[]{:S(2)}) copy-start(s32[64]{0:T(128)} %param.12) | copy-start | bytes 772
  71.1 7.9 %copy-start.4 = (s32[64]{0:T(128)S(1)}, s32[64]{0:T(128)}, u32[]{:S(2)}) copy-start(s32[64]{0:T(128)} %param.11) | copy-start | bytes 772
  73.5 23.1 %all-to-all-start.1 = ((bf16[64,32,256]{2,1,0:T(8,128)(2,1)}), bf16[64,32,256]{2,1,0:T(8,128)(2,1)S(1)}, u32[]{:S(2)}, u32[]{:S(2)}) async-start(bf16[64,32,256]{2,1,0:T(8,128)(2,1)} %bitcast.17), calls=%async_computation.1 | async-start | bytes 2097152 | tf_op jit(solution)/shard_map/all_to_all | solution.py:117

commit v11 on v10

--- a/solution.py
+++ b/solution.py
@@ -85,10 +85,12 @@
 
     ref_index = ref_date[0]
     ref_scale = scales[ref_index]
-    ref_re = lax.dynamic_slice_in_dim(x_re, ref_index * cols, cols, 0).astype(f32) * ref_scale
-    ref_im = lax.dynamic_slice_in_dim(x_im, ref_index * cols, cols, 0).astype(f32) * ref_scale
-    ref_re = jnp.tile(ref_re, (n_date, 1))
-    ref_im = jnp.tile(ref_im, (n_date, 1))
+    rows = n_date * cols
+    row_id = jnp.arange(rows, dtype=jnp.int32)[:, None]
+    col_id = jnp.arange(rows, dtype=jnp.int32)[None, :]
+    pick = (col_id == ref_index * cols + row_id % cols).astype(jnp.bfloat16)
+    ref_re = jnp.dot(pick, x_re, preferred_element_type=f32) * ref_scale
+    ref_im = jnp.dot(pick, x_im, preferred_element_type=f32) * ref_scale
     row_scale = jnp.repeat(scales, cols)[:, None]
     a_re = x_re.astype(f32) * row_scale
     a_im = x_im.astype(f32) * row_scale

time: 105 us -> 102 us (0.971)
  local copies, waits for them, and re-layouts: 13.2 us -> 10.7 us
  other arithmetic: 23.4 us -> 21.1 us
  matrix products: 14.4 us -> 16.6 us
    another operation x4 -> x0, local copies, waits for them, and re-layouts: 2.44 us -> none  [the longest x2 1.22 us: shards(): ref_re = jnp.tile(ref_re, (n_date, 1))]
    dot_general x0 -> x2, matrix products: none -> 2.36 us  [the longest x1 1.38 us: shards(): ref_im = jnp.dot(pick, x_im, preferred_element_type=f32) * ref_scale]
    convert_element_type x1 -> x0, other arithmetic: 1.82 us -> none  [shards(): ifg_re = (a_re * ref_re + a_im * ref_im).astype(jnp.bfloat16)]
    slice x3 -> x0, local copies, waits for them, and re-layouts: 1.18 us -> none  [the longest x2 0.64 us: shards(): x_re = got[:, 0].reshape(n_date * cols, lines)]
    unnamed x21 -> x17, local copies, waits for them, and re-layouts: 3.12 us -> 3.25 us
  transfers between devices with their start and end apart: 5 -> 5, of which waited for: 2 -> 2; matrix products, arithmetic and copies ran while one was open for 13% -> 14% of each run, Pallas kernels for 0% -> 0%
where the time goes in v11:
time: 102 us; the launch traced here: 101 us
  starting transfers between devices  25.5 us (25%)
  waiting for transfers between devices  23.9 us (23%)
  other arithmetic  21.1 us (21%)
  matrix products  16.6 us (16%)
  local copies, waits for them, and re-layouts  10.7 us (10%)
  between operations  3.55 us (3%)
    all_to_all x1, waiting for transfers between devices, shards(): got = lax.all_to_all(pair, 'date', split_axis=0, concat_axis=0, tiled=True)  17 us
    ppermute x3, starting transfers between devices, shards(): lax.ppermute(local, 'rng', [(r, (r + k) % n_rng) for r in range(n_rng)])  11.3 us
    all_to_all x1, starting transfers between devices, shards(): got = lax.all_to_all(both, 'date', split_axis=0, concat_axis=0, tiled=True)  9.45 us
    convert_element_type x1, other arithmetic, dft_table(): (hi_c * lo_s + hi_s * lo_c).reshape(length, length).astype(jnp.bfloat16)  8.27 us
    all_to_all x1, waiting for transfers between devices, shards(): got = lax.all_to_all(both, 'date', split_axis=0, concat_axis=0, tiled=True)  6.9 us
    dot_general x1, matrix products, shards(): fc = jnp.dot(stacked, cos_t, preferred_element_type=f32)  5.89 us
    all_to_all x1, starting transfers between devices, shards(): got = lax.all_to_all(pair, 'date', split_axis=0, concat_axis=0, tiled=True)  4.7 us
    mul x1, other arithmetic, shards(): result = result * mask_px[:, None]  3.69 us
  transfers between devices with their start and end apart: 5, of which 2 were waited for; matrix products, arithmetic and copies ran while one was open for 14% of the time, Pallas kernels for 0%

profile of v11, /device:TPU:1, one launch (start us, length us, event | category | flops | bytes accessed | tf_op | source)
XLA Modules:
  0.0 101.2 jit_solution(798828160322594880)
XLA Ops:
  0.0 1.2 %copy.27 = bf16[1,2048,128]{1,2,0:T(8,128)(2,1)S(1)} copy(bf16[1,2048,128]{2,1,0:T(8,128)(2,1)} %param.7) | data formatting | bytes 1048576 | tf_op args[0]
  1.3 1.2 %copy.28 = bf16[1,2048,128]{1,2,0:T(8,128)(2,1)S(1)} copy(bf16[1,2048,128]{2,1,0:T(8,128)(2,1)} %param.8) | data formatting | bytes 1048576 | tf_op args[1]
  2.5 0.9 add_reduce_fusion
  3.4 3.8 %collective-permute-start = (f32[]{:T(128)}, f32[]{:T(128)}, u32[]{:S(2)}, u32[]{:S(2)}) collective-permute-start(f32[]{:T(128)} %add_reduce_fusion), channel_id=1, source_target_pairs={{0,1},{1,2},{2,3},{3,0},{4,5},{5,6},{6,7},{7,4},{8,9},{9,10},{10,1... | collective-permute-start | bytes 20 | tf_op jit(solution)/shard_map/ppermute | solution.py:64
  7.2 5.1 %collective-permute-start.1 = (f32[]{:T(128)}, f32[]{:T(128)}, u32[]{:S(2)}, u32[]{:S(2)}) collective-permute-start(f32[]{:T(128)} %add_reduce_fusion), channel_id=1, source_target_pairs={{0,2},{1,3},{2,0},{3,1},{4,6},{5,7},{6,4},{7,5},{8,10},{9,11},{10,... | collective-permute-start | bytes 20 | tf_op jit(solution)/shard_map/ppermute | solution.py:64
  12.3 2.4 %collective-permute-start.2 = (f32[]{:T(128)}, f32[]{:T(128)}, u32[]{:S(2)}, u32[]{:S(2)}) collective-permute-start(f32[]{:T(128)} %add_reduce_fusion), channel_id=1, source_target_pairs={{0,3},{1,0},{2,1},{3,2},{4,7},{5,4},{6,5},{7,6},{8,11},{9,8},{10,9... | collective-permute-start | bytes 20 | tf_op jit(solution)/shard_map/ppermute | solution.py:64
  14.8 0.8 copy.29
  18.2 1.6 %pad_maximum_fusion = bf16[64,4,2176]{2,1,0:T(4,128)(2,1)} fusion(bf16[64,4,2048]{2,1,0:T(4,128)(2,1)S(1)} %copy.29, bf16[2176]{0:T(1024)(128)(2,1)S(1)} %pad.11.clone), kind=kLoop, calls=%fused_computation.10 | loop fusion | flops 2228224 | bytes 2167040 | tf_op jit(solution)/shard_map/concatenate | solution.py:77
  19.7 9.5 %all-to-all-start = ((bf16[64,4,2176]{2,1,0:T(4,128)(2,1)}), bf16[64,4,2176]{2,1,0:T(4,128)(2,1)S(1)}, u32[]{:S(2)}, u32[]{:S(2)}) async-start(bf16[64,4,2176]{2,1,0:T(4,128)(2,1)} %pad_maximum_fusion), calls=%async_computation | async-start | bytes 2228224 | tf_op jit(solution)/shard_map/all_to_all | solution.py:78
  29.9 2.0 %fusion.24 = (f32[2048,64]{0,1:T(8,128)S(1)}, f32[2048,64]{0,1:T(8,128)S(1)}) fusion(), kind=kLoop, calls=%fused_computation.53 | loop fusion | flops 1835008 | bytes 1048576 | tf_op jit(solution)/shard_map/sin | solution.py:25
  31.9 1.1 %fusion.38 = (f32[2048,32]{0,1:T(8,128)S(1)}, f32[2048,32]{0,1:T(8,128)S(1)}) fusion(s32[32]{0:T(128)S(1)} %iota_multiply_fusion), kind=kLoop, calls=%fused_computation.67 | loop fusion | flops 917504 | bytes 524416 | tf_op jit(solution)/shard_map/cos | solution.py:24
  33.0 8.3 %add_convert_fusion = (bf16[2048,32,64]{0,2,1:T(8,128)(2,1)}, bf16[2048,32,64]{0,2,1:T(8,128)(2,1)}) fusion(f32[2048,64]{0,1:T(8,128)S(1)} %get-tuple-element.25, f32[2048,32]{0,1:T(8,128)S(1)} %get-tuple-element.24, f32[2048,64]{0,1:T(8,128)S(1)} %get-tuple-element.26, f32[2048,32]{0,1:T(8,128)S(1)} %get-tuple-element.23), kind=kLoop, calls=%fused_computation | loop fusion | flops 33554432 | bytes 18350080 | tf_op jit(solution)/shard_map/convert_element_type | solution.py:27
  41.3 6.9 %all-to-all-done = bf16[64,4,2176]{2,1,0:T(4,128)(2,1)S(1)} async-done(((bf16[64,4,2176]{2,1,0:T(4,128)(2,1)}), bf16[64,4,2176]{2,1,0:T(4,128)(2,1)S(1)}, u32[]{:S(2)}, u32[]{:S(2)}) %all-to-all-start) | async-done | bytes 1114144 | tf_op jit(solution)/shard_map/all_to_all | solution.py:78
  48.4 0.6 slice.68
  49.0 0.7 reshape.211
  49.7 0.7 slice_bitcast_fusion.1
  51.1 0.5 constant_dynamic-slice_fusion
  51.6 1.0 convolution_multiply_fusion.1
  52.6 1.4 %add_convert_fusion.1 = (bf16[128,2048]{1,0:T(8,128)(2,1)S(1)}, bf16[128,2048]{1,0:T(8,128)(2,1)S(1)}) fusion(bf16[128,2048]{1,0:T(8,128)(2,1)S(1)} %reshape_squeeze.7, f32[128,2048]{1,0:T(8,128)S(1)} %convolution_multiply_fusion.1, bf16[128,2048]{1,0:T(8,128)(2,1)S(1)} %reshape_squeeze.6, f32[128]{0:T(128)S(1)} %mul.287, f32[]{:T(128)} %bitcast.10, ...), kind=kOutput, calls=%fused_computation.28 | convolution fusion | flops 70533120 | bytes 3146756 | tf_op jit(solution)/shard_map/dot_general | solution.py:93
  54.0 5.9 %fusion.14 = f32[256,2048]{1,0:T(8,128)S(1)} fusion(bf16[2048,2048]{0,1:T(8,128)(2,1)} %bitcast.56, bf16[128,2048]{1,0:T(8,128)(2,1)S(1)} %get-tuple-element.16, bf16[128,2048]{1,0:T(8,128)(2,1)S(1)} %get-tuple-element.15), kind=kOutput, calls=%fused_computation.38 | convolution fusion | flops 2149580800 | bytes 11534336 | tf_op jit(solution)/shard_map/dot_general | solution.py:103
  60.0 2.4 %fusion.13 = f32[256,2048]{1,0:T(8,128)S(1)} fusion(bf16[2048,2048]{0,1:T(8,128)(2,1)S(1)} %bitcast.54, bf16[128,2048]{1,0:T(8,128)(2,1)S(1)} %get-tuple-element.16, bf16[128,2048]{1,0:T(8,128)(2,1)S(1)} %get-tuple-element.15), kind=kOutput, calls=%fused_computation.37 | convolution fusion | flops 2149580800 | bytes 11534336 | tf_op jit(solution)/shard_map/dot_general | solution.py:104
  62.8 2.4 %fusion.12 = f32[256,2048]{1,0:T(8,128)S(1)} fusion(bf16[2048,2048]{0,1:T(8,128)(2,1)S(1)} %bitcast.59, bf16[128,2048]{1,0:T(8,128)(2,1)S(1)} %get-tuple-element.12, bf16[128,2048]{1,0:T(8,128)(2,1)S(1)} %get-tuple-element.11), kind=kOutput, calls=%fused_computation.36 | convolution fusion | flops 2149580800 | bytes 11534336 | tf_op jit(solution)/shard_map/dot_general | solution.py:112
  65.1 2.4 %fusion.11 = f32[256,2048]{1,0:T(8,128)S(1)} fusion(bf16[2048,2048]{0,1:T(8,128)(2,1)S(1)} %bitcast.55, bf16[128,2048]{1,0:T(8,128)(2,1)S(1)} %get-tuple-element.12, bf16[128,2048]{1,0:T(8,128)(2,1)S(1)} %get-tuple-element.11), kind=kOutput, calls=%fused_computation.35 | convolution fusion | flops 2149580800 | bytes 11534336 | tf_op jit(solution)/shard_map/dot_general | solution.py:113
  68.0 0.9 reshape.212
  69.3 1.3 %copy.33 = bf16[2048,256]{1,0:T(8,128)(2,1)} copy(bf16[2048,256]{0,1:T(8,128)(2,1)S(1)} %bitcast.64) | data formatting | bytes 2097152 | tf_op jit(solution)/shard_map/transpose | solution.py:118
  70.6 4.7 %all-to-all-start.1 = ((bf16[64,32,256]{2,1,0:T(8,128)(2,1)}), bf16[64,32,256]{2,1,0:T(8,128)(2,1)S(1)}, u32[]{:S(2)}, u32[]{:S(2)}) async-start(bf16[64,32,256]{2,1,0:T(8,128)(2,1)} %bitcast.16), calls=%async_computation.1 | async-start | bytes 2097152 | tf_op jit(solution)/shard_map/all_to_all | solution.py:119
  75.4 0.7 convert_bitcast_fusion
  76.8 17.0 %all-to-all-done.1 = bf16[64,32,256]{2,1,0:T(8,128)(2,1)S(1)} async-done(((bf16[64,32,256]{2,1,0:T(8,128)(2,1)}), bf16[64,32,256]{2,1,0:T(8,128)(2,1)S(1)}, u32[]{:S(2)}, u32[]{:S(2)}) %all-to-all-start.1) | async-done | bytes 1048608 | tf_op jit(solution)/shard_map/all_to_all | solution.py:119
  94.0 1.2 %copy.34 = bf16[64,32,2,128]{3,0,2,1:T(8,128)(2,1)S(1)} copy(bf16[64,32,2,128]{3,2,1,0:T(2,128)(2,1)S(1)} %reshape.214) | data formatting | bytes 2097152 | tf_op jit(solution)/shard_map/reshape | solution.py:120
  95.3 0.9 multiply_reduce_fusion
  96.3 1.2 %fusion.29 = f32[4096,512]{1,0:T(8,128)S(1)} fusion(bf16[4096,128]{1,0:T(8,128)(2,1)S(1)} %bitcast.60, bf16[64,256]{1,0:T(8,128)(2,1)S(1)} %get-tuple-element.22, bf16[64,256]{1,0:T(8,128)(2,1)S(1)} %get-tuple-element.21, bf16[64,256]{1,0:T(8,128)(2,1)S(1)} %fusion.57), kind=kOutput, calls=%fused_computation.58 | convolution fusion | flops 537395200 | bytes 9535488 | tf_op jit(solution)/shard_map/dot_general | solution.py:125
  97.5 3.7 %fusion.2 = f32[4096,256]{1,0:T(8,128)} fusion(f32[4096,512]{1,0:T(8,128)S(1)} %fusion.29, f32[4096]{0:T(1024)S(1)} %convert_bitcast_fusion, f32[4096]{0:T(1024)S(1)} %mul.336), kind=kLoop, calls=%fused_computation.5 | loop fusion | flops 5242880 | bytes 12615680 | tf_op jit(solution)/shard_map/mul | solution.py:135
  (40 shorter events, 3.2 us)
Async XLA Ops:
  3.4 12.2 %collective-permute-start = (f32[]{:T(128)}, f32[]{:T(128)}, u32[]{:S(2)}, u32[]{:S(2)}) collective-permute-start(f32[]{:T(128)} %add_reduce_fusion), channel_id=1, source_target_pairs={{0,1},{1,2},{2,3},{3,0},{4,5},{5,6},{6,7},{7,4},{8,9},{9,10},{10,1... | collective-permute-start | bytes 20 | tf_op jit(solution)/shard_map/ppermute | solution.py:64
  7.2 9.8 %collective-permute-start.1 = (f32[]{:T(128)}, f32[]{:T(128)}, u32[]{:S(2)}, u32[]{:S(2)}) collective-permute-start(f32[]{:T(128)} %add_reduce_fusion), channel_id=1, source_target_pairs={{0,2},{1,3},{2,0},{3,1},{4,6},{5,7},{6,4},{7,5},{8,10},{9,11},{10,... | collective-permute-start | bytes 20 | tf_op jit(solution)/shard_map/ppermute | solution.py:64
  12.3 5.2 %collective-permute-start.2 = (f32[]{:T(128)}, f32[]{:T(128)}, u32[]{:S(2)}, u32[]{:S(2)}) collective-permute-start(f32[]{:T(128)} %add_reduce_fusion), channel_id=1, source_target_pairs={{0,3},{1,0},{2,1},{3,2},{4,7},{5,4},{6,5},{7,6},{8,11},{9,8},{10,9... | collective-permute-start | bytes 20 | tf_op jit(solution)/shard_map/ppermute | solution.py:64
  19.7 28.4 %all-to-all-start = ((bf16[64,4,2176]{2,1,0:T(4,128)(2,1)}), bf16[64,4,2176]{2,1,0:T(4,128)(2,1)S(1)}, u32[]{:S(2)}, u32[]{:S(2)}) async-start(bf16[64,4,2176]{2,1,0:T(4,128)(2,1)} %pad_maximum_fusion), calls=%async_computation | async-start | bytes 2228224 | tf_op jit(solution)/shard_map/all_to_all | solution.py:78
  52.6 7.3 %slice-start = ((s8[8388608]{0:T(1024)(128)(4,1)}), s8[4194304]{0:T(1024)(128)(4,1)S(1)}, s32[]{:S(2)}) async-start(s8[8388608]{0:T(1024)(128)(4,1)} %bitcast.52), calls=%async_computation.2 | async-start | bytes 8388608
  54.0 5.9 %slice-start.1 = ((s8[8388608]{0:T(1024)(128)(4,1)}), s8[4194304]{0:T(1024)(128)(4,1)S(1)}, s32[]{:S(2)}) async-start(s8[8388608]{0:T(1024)(128)(4,1)} %bitcast.52), calls=%async_computation.3 | async-start | bytes 8388608
  54.0 8.7 %slice-start.2 = ((s8[8388608]{0:T(1024)(128)(4,1)}), s8[4194304]{0:T(1024)(128)(4,1)S(1)}, s32[]{:S(2)}) async-start(s8[8388608]{0:T(1024)(128)(4,1)} %bitcast.57), calls=%async_computation.4 | async-start | bytes 8388608
  60.0 2.4 %copy-start = (f32[2048]{0:T(1024)S(1)}, f32[2048]{0:T(1024)}, u32[]{:S(2)}) copy-start(f32[2048]{0:T(1024)} %param.10) | copy-start | bytes 24580
  60.0 2.8 %slice-start.3 = ((s8[8388608]{0:T(1024)(128)(4,1)}), s8[4194304]{0:T(1024)(128)(4,1)S(1)}, s32[]{:S(2)}) async-start(s8[8388608]{0:T(1024)(128)(4,1)} %bitcast.57), calls=%async_computation.5 | async-start | bytes 8388608
  68.0 8.1 %copy-start.1 = (s32[64]{0:T(128)S(1)}, s32[64]{0:T(128)}, u32[]{:S(2)}) copy-start(s32[64]{0:T(128)} %param.12) | copy-start | bytes 772
  68.0 8.1 %copy-start.2 = (s32[64]{0:T(128)S(1)}, s32[64]{0:T(128)}, u32[]{:S(2)}) copy-start(s32[64]{0:T(128)} %param.11) | copy-start | bytes 772
  70.6 23.1 %all-to-all-start.1 = ((bf16[64,32,256]{2,1,0:T(8,128)(2,1)}), bf16[64,32,256]{2,1,0:T(8,128)(2,1)S(1)}, u32[]{:S(2)}, u32[]{:S(2)}) async-start(bf16[64,32,256]{2,1,0:T(8,128)(2,1)} %bitcast.16), calls=%async_computation.1 | async-start | bytes 2097152 | tf_op jit(solution)/shard_map/all_to_all | solution.py:119

commit v12 on v11

--- a/solution.py
+++ b/solution.py
@@ -79,18 +79,19 @@
     sums = got[:, 0, lines:lines + 3].astype(f32)
     date_sums = (sums[:, 0] + sums[:, 1]) + sums[:, 2]
     scales = lax.rsqrt(date_sums / pixel_total + 1e-06)
-    got = got[:, :, :lines].reshape(n_date, 2, cols, lines)
-    x_re = got[:, 0].reshape(n_date * cols, lines)
-    x_im = got[:, 1].reshape(n_date * cols, lines)
-
     ref_index = ref_date[0]
     ref_scale = scales[ref_index]
     rows = n_date * cols
+    flat = got.reshape(n_date * 2 * cols, lines + 128)
     row_id = jnp.arange(rows, dtype=jnp.int32)[:, None]
-    col_id = jnp.arange(rows, dtype=jnp.int32)[None, :]
-    pick = (col_id == ref_index * cols + row_id % cols).astype(jnp.bfloat16)
-    ref_re = jnp.dot(pick, x_re, preferred_element_type=f32) * ref_scale
-    ref_im = jnp.dot(pick, x_im, preferred_element_type=f32) * ref_scale
+    col_id = jnp.arange(n_date * 2 * cols, dtype=jnp.int32)[None, :]
+    base = ref_index * 2 * cols + row_id % cols
+    pick_re = (col_id == base).astype(jnp.bfloat16)
+    pick_im = (col_id == base + cols).astype(jnp.bfloat16)
+    ref_re = jnp.dot(pick_re, flat, preferred_element_type=f32)[:, :lines] * ref_scale
+    ref_im = jnp.dot(pick_im, flat, preferred_element_type=f32)[:, :lines] * ref_scale
+    x_re = got[:, :cols, :lines].reshape(rows, lines)
+    x_im = got[:, cols:, :lines].reshape(rows, lines)
     row_scale = jnp.repeat(scales, cols)[:, None]
     a_re = x_re.astype(f32) * row_scale
     a_im = x_im.astype(f32) * row_scale

time: 102 us -> 104 us (1.020)
  local copies, waits for them, and re-layouts: 10.7 us -> 12.1 us
  other arithmetic: 21.1 us -> 22.2 us
    convert_element_type x0 -> x2, local copies, waits for them, and re-layouts: none -> 3.41 us  [the longest x1 1.72 us: shards(): a_re = x_re.astype(f32) * row_scale]
    convert_element_type x0 -> x1, other arithmetic: none -> 1.15 us  [shards(): a_re = x_re.astype(f32) * row_scale]
    unnamed x17 -> x20, local copies, waits for them, and re-layouts: 3.25 us -> 2.75 us
  transfers between devices with their start and end apart: 5 -> 5, of which waited for: 2 -> 2; matrix products, arithmetic and copies ran while one was open for 14% -> 13% of each run, Pallas kernels for 0% -> 0%
where the time goes in v12:
time: 104 us
  starting transfers between devices  25.5 us (25%)
  waiting for transfers between devices  23.9 us (23%)
  other arithmetic  22.2 us (21%)
  matrix products  16.5 us (16%)
  local copies, waits for them, and re-layouts  12.1 us (12%)
  between operations  3.54 us (3%)
    all_to_all x1, waiting for transfers between devices, shards(): got = lax.all_to_all(pair, 'date', split_axis=0, concat_axis=0, tiled=True)  17 us
    ppermute x3, starting transfers between devices, shards(): lax.ppermute(local, 'rng', [(r, (r + k) % n_rng) for r in range(n_rng)])  11.3 us
    all_to_all x1, starting transfers between devices, shards(): got = lax.all_to_all(both, 'date', split_axis=0, concat_axis=0, tiled=True)  9.46 us
    convert_element_type x1, other arithmetic, dft_table(): (hi_c * lo_s + hi_s * lo_c).reshape(length, length).astype(jnp.bfloat16)  8.23 us
    all_to_all x1, waiting for transfers between devices, shards(): got = lax.all_to_all(both, 'date', split_axis=0, concat_axis=0, tiled=True)  6.94 us
    dot_general x1, matrix products, shards(): fc = jnp.dot(stacked, cos_t, preferred_element_type=f32)  5.89 us
    all_to_all x1, starting transfers between devices, shards(): got = lax.all_to_all(pair, 'date', split_axis=0, concat_axis=0, tiled=True)  4.7 us
    mul x1, other arithmetic, shards(): result = result * mask_px[:, None]  3.69 us
  transfers between devices with their start and end apart: 5, of which 2 were waited for; matrix products, arithmetic and copies ran while one was open for 13% of the time, Pallas kernels for 0%

profile of v12, /device:TPU:1, one launch (start us, length us, event | category | flops | bytes accessed | tf_op | source)
XLA Modules:
  0.0 103.7 jit_solution(14078555154981488859)
XLA Ops:
  0.0 1.2 %copy.17 = bf16[1,2048,128]{1,2,0:T(8,128)(2,1)S(1)} copy(bf16[1,2048,128]{2,1,0:T(8,128)(2,1)} %param.7) | data formatting | bytes 1048576 | tf_op args[0]
  1.3 1.2 %copy.18 = bf16[1,2048,128]{1,2,0:T(8,128)(2,1)S(1)} copy(bf16[1,2048,128]{2,1,0:T(8,128)(2,1)} %param.8) | data formatting | bytes 1048576 | tf_op args[1]
  2.5 0.9 add_reduce_fusion
  3.4 3.8 %collective-permute-start = (f32[]{:T(128)}, f32[]{:T(128)}, u32[]{:S(2)}, u32[]{:S(2)}) collective-permute-start(f32[]{:T(128)} %add_reduce_fusion), channel_id=1, source_target_pairs={{0,1},{1,2},{2,3},{3,0},{4,5},{5,6},{6,7},{7,4},{8,9},{9,10},{10,1... | collective-permute-start | bytes 20 | tf_op jit(solution)/shard_map/ppermute | solution.py:64
  7.2 5.1 %collective-permute-start.1 = (f32[]{:T(128)}, f32[]{:T(128)}, u32[]{:S(2)}, u32[]{:S(2)}) collective-permute-start(f32[]{:T(128)} %add_reduce_fusion), channel_id=1, source_target_pairs={{0,2},{1,3},{2,0},{3,1},{4,6},{5,7},{6,4},{7,5},{8,10},{9,11},{10,... | collective-permute-start | bytes 20 | tf_op jit(solution)/shard_map/ppermute | solution.py:64
  12.3 2.4 %collective-permute-start.2 = (f32[]{:T(128)}, f32[]{:T(128)}, u32[]{:S(2)}, u32[]{:S(2)}) collective-permute-start(f32[]{:T(128)} %add_reduce_fusion), channel_id=1, source_target_pairs={{0,3},{1,0},{2,1},{3,2},{4,7},{5,4},{6,5},{7,6},{8,11},{9,8},{10,9... | collective-permute-start | bytes 20 | tf_op jit(solution)/shard_map/ppermute | solution.py:64
  14.8 0.8 copy.19
  18.2 1.6 %pad_maximum_fusion = bf16[64,4,2176]{2,1,0:T(4,128)(2,1)} fusion(bf16[64,4,2048]{2,1,0:T(4,128)(2,1)S(1)} %copy.19, bf16[2176]{0:T(1024)(128)(2,1)S(1)} %pad.11.clone), kind=kLoop, calls=%fused_computation.10 | loop fusion | flops 2228224 | bytes 2167040 | tf_op jit(solution)/shard_map/concatenate | solution.py:77
  19.7 9.5 %all-to-all-start = ((bf16[64,4,2176]{2,1,0:T(4,128)(2,1)}), bf16[64,4,2176]{2,1,0:T(4,128)(2,1)S(1)}, u32[]{:S(2)}, u32[]{:S(2)}) async-start(bf16[64,4,2176]{2,1,0:T(4,128)(2,1)} %pad_maximum_fusion), calls=%async_computation | async-start | bytes 2228224 | tf_op jit(solution)/shard_map/all_to_all | solution.py:78
  29.9 2.0 %fusion.26 = (f32[2048,64]{0,1:T(8,128)S(1)}, f32[2048,64]{0,1:T(8,128)S(1)}) fusion(), kind=kLoop, calls=%fused_computation.53 | loop fusion | flops 1835008 | bytes 1048576 | tf_op jit(solution)/shard_map/sin | solution.py:25
  31.9 1.1 %fusion.40 = (f32[2048,32]{0,1:T(8,128)S(1)}, f32[2048,32]{0,1:T(8,128)S(1)}) fusion(s32[32]{0:T(128)S(1)} %iota_multiply_fusion), kind=kLoop, calls=%fused_computation.67 | loop fusion | flops 917504 | bytes 524416 | tf_op jit(solution)/shard_map/cos | solution.py:24
  33.0 8.2 %add_convert_fusion = (bf16[2048,32,64]{0,2,1:T(8,128)(2,1)}, bf16[2048,32,64]{0,2,1:T(8,128)(2,1)}) fusion(f32[2048,64]{0,1:T(8,128)S(1)} %get-tuple-element.25, f32[2048,32]{0,1:T(8,128)S(1)} %get-tuple-element.24, f32[2048,64]{0,1:T(8,128)S(1)} %get-tuple-element.26, f32[2048,32]{0,1:T(8,128)S(1)} %get-tuple-element.23), kind=kLoop, calls=%fused_computation | loop fusion | flops 33554432 | bytes 18350080 | tf_op jit(solution)/shard_map/convert_element_type | solution.py:27
  41.3 6.9 %all-to-all-done = bf16[64,4,2176]{2,1,0:T(4,128)(2,1)S(1)} async-done(((bf16[64,4,2176]{2,1,0:T(4,128)(2,1)}), bf16[64,4,2176]{2,1,0:T(4,128)(2,1)S(1)}, u32[]{:S(2)}, u32[]{:S(2)}) %all-to-all-start) | async-done | bytes 1114144 | tf_op jit(solution)/shard_map/all_to_all | solution.py:78
  48.4 1.2 %slice_convert_fusion.1 = (f32[64,2,2048]{2,1,0:T(2,128)S(1)}, f32[64,2,2048]{2,1,0:T(2,128)S(1)}) fusion(bf16[64,4,2176]{2,1,0:T(4,128)(2,1)S(1)} %all-to-all-done), kind=kLoop, calls=%fused_computation.43 | loop fusion | flops 524288 | bytes 3145728 | tf_op jit(solution)/shard_map/convert_element_type | solution.py:96
  49.6 1.7 %reshape.226 = f32[128,2048]{1,0:T(8,128)} reshape(f32[64,2,2048]{2,1,0:T(2,128)S(1)} %get-tuple-element.19) | data formatting | bytes 2097152 | tf_op jit(solution)/shard_map/convert_element_type | solution.py:96
  51.3 1.7 %reshape.229 = f32[128,2048]{1,0:T(8,128)} reshape(f32[64,2,2048]{2,1,0:T(2,128)S(1)} %get-tuple-element.20) | data formatting | bytes 2097152 | tf_op jit(solution)/shard_map/convert_element_type | solution.py:97
  53.7 0.5 reshape.220
  54.2 1.0 convolution_multiply_fusion.1
  55.4 1.3 %add_convert_fusion.1 = (bf16[128,2048]{1,0:T(8,128)(2,1)S(1)}, bf16[128,2048]{1,0:T(8,128)(2,1)S(1)}) fusion(f32[128,2048]{1,0:T(8,128)S(1)} %convolution_multiply_fusion.1, f32[128,2048]{1,0:T(8,128)S(1)} %copy-done.1, f32[128,2048]{1,0:T(8,128)S(1)} %copy-done, f32[128]{0:T(128)S(1)} %mul.288, f32[]{:T(128)} %bitcast.10, ...), kind=kOutput, calls=%fused_computation.28 | convolution fusion | flops 137134080 | bytes 5243908 | tf_op jit(solution)/shard_map/dot_general | solution.py:92
  56.7 5.9 %fusion.16 = f32[256,2048]{1,0:T(8,128)S(1)} fusion(bf16[2048,2048]{0,1:T(8,128)(2,1)} %bitcast.46, bf16[128,2048]{1,0:T(8,128)(2,1)S(1)} %get-tuple-element.14, bf16[128,2048]{1,0:T(8,128)(2,1)S(1)} %get-tuple-element.13), kind=kOutput, calls=%fused_computation.38 | convolution fusion | flops 2149580800 | bytes 11534336 | tf_op jit(solution)/shard_map/dot_general | solution.py:104
  62.7 2.4 %fusion.15 = f32[256,2048]{1,0:T(8,128)S(1)} fusion(bf16[2048,2048]{0,1:T(8,128)(2,1)S(1)} %bitcast.44, bf16[128,2048]{1,0:T(8,128)(2,1)S(1)} %get-tuple-element.14, bf16[128,2048]{1,0:T(8,128)(2,1)S(1)} %get-tuple-element.13), kind=kOutput, calls=%fused_computation.37 | convolution fusion | flops 2149580800 | bytes 11534336 | tf_op jit(solution)/shard_map/dot_general | solution.py:105
  65.5 2.4 %fusion.14 = f32[256,2048]{1,0:T(8,128)S(1)} fusion(bf16[2048,2048]{0,1:T(8,128)(2,1)S(1)} %bitcast.49, bf16[128,2048]{1,0:T(8,128)(2,1)S(1)} %get-tuple-element.12, bf16[128,2048]{1,0:T(8,128)(2,1)S(1)} %get-tuple-element.11), kind=kOutput, calls=%fused_computation.36 | convolution fusion | flops 2149580800 | bytes 11534336 | tf_op jit(solution)/shard_map/dot_general | solution.py:113
  67.8 2.4 %fusion.13 = f32[256,2048]{1,0:T(8,128)S(1)} fusion(bf16[2048,2048]{0,1:T(8,128)(2,1)S(1)} %bitcast.45, bf16[128,2048]{1,0:T(8,128)(2,1)S(1)} %get-tuple-element.12, bf16[128,2048]{1,0:T(8,128)(2,1)S(1)} %get-tuple-element.11), kind=kOutput, calls=%fused_computation.35 | convolution fusion | flops 2149580800 | bytes 11534336 | tf_op jit(solution)/shard_map/dot_general | solution.py:114
  70.7 0.7 reshape.221
  71.8 1.3 %copy.21 = bf16[2048,256]{1,0:T(8,128)(2,1)} copy(bf16[2048,256]{0,1:T(8,128)(2,1)S(1)} %bitcast.54) | data formatting | bytes 2097152 | tf_op jit(solution)/shard_map/transpose | solution.py:119
  73.1 4.7 %all-to-all-start.1 = ((bf16[64,32,256]{2,1,0:T(8,128)(2,1)}), bf16[64,32,256]{2,1,0:T(8,128)(2,1)S(1)}, u32[]{:S(2)}, u32[]{:S(2)}) async-start(bf16[64,32,256]{2,1,0:T(8,128)(2,1)} %bitcast.16), calls=%async_computation.1 | async-start | bytes 2097152 | tf_op jit(solution)/shard_map/all_to_all | solution.py:120
  77.8 0.7 convert_bitcast_fusion
  79.2 17.0 %all-to-all-done.1 = bf16[64,32,256]{2,1,0:T(8,128)(2,1)S(1)} async-done(((bf16[64,32,256]{2,1,0:T(8,128)(2,1)}), bf16[64,32,256]{2,1,0:T(8,128)(2,1)S(1)}, u32[]{:S(2)}, u32[]{:S(2)}) %all-to-all-start.1) | async-done | bytes 1048608 | tf_op jit(solution)/shard_map/all_to_all | solution.py:120
  96.5 1.2 %copy.22 = bf16[64,32,2,128]{3,0,2,1:T(8,128)(2,1)S(1)} copy(bf16[64,32,2,128]{3,2,1,0:T(2,128)(2,1)S(1)} %reshape.223) | data formatting | bytes 2097152 | tf_op jit(solution)/shard_map/reshape | solution.py:121
  97.7 0.9 multiply_reduce_fusion
  98.8 1.2 %fusion.31 = f32[4096,512]{1,0:T(8,128)S(1)} fusion(bf16[4096,128]{1,0:T(8,128)(2,1)S(1)} %bitcast.50, bf16[64,256]{1,0:T(8,128)(2,1)S(1)} %get-tuple-element.22, bf16[64,256]{1,0:T(8,128)(2,1)S(1)} %get-tuple-element.21, bf16[64,256]{1,0:T(8,128)(2,1)S(1)} %fusion.59), kind=kOutput, calls=%fused_computation.58 | convolution fusion | flops 537395200 | bytes 9535488 | tf_op jit(solution)/shard_map/dot_general | solution.py:126
  100.0 3.7 %fusion.2 = f32[4096,256]{1,0:T(8,128)} fusion(f32[4096,512]{1,0:T(8,128)S(1)} %fusion.31, f32[4096]{0:T(1024)S(1)} %convert_bitcast_fusion, f32[4096]{0:T(1024)S(1)} %mul.337), kind=kLoop, calls=%fused_computation.5 | loop fusion | flops 5242880 | bytes 12615680 | tf_op jit(solution)/shard_map/mul | solution.py:136
  (43 shorter events, 3.6 us)
Async XLA Ops:
  3.4 12.2 %collective-permute-start = (f32[]{:T(128)}, f32[]{:T(128)}, u32[]{:S(2)}, u32[]{:S(2)}) collective-permute-start(f32[]{:T(128)} %add_reduce_fusion), channel_id=1, source_target_pairs={{0,1},{1,2},{2,3},{3,0},{4,5},{5,6},{6,7},{7,4},{8,9},{9,10},{10,1... | collective-permute-start | bytes 20 | tf_op jit(solution)/shard_map/ppermute | solution.py:64
  7.2 9.7 %collective-permute-start.1 = (f32[]{:T(128)}, f32[]{:T(128)}, u32[]{:S(2)}, u32[]{:S(2)}) collective-permute-start(f32[]{:T(128)} %add_reduce_fusion), channel_id=1, source_target_pairs={{0,2},{1,3},{2,0},{3,1},{4,6},{5,7},{6,4},{7,5},{8,10},{9,11},{10,... | collective-permute-start | bytes 20 | tf_op jit(solution)/shard_map/ppermute | solution.py:64
  12.3 5.2 %collective-permute-start.2 = (f32[]{:T(128)}, f32[]{:T(128)}, u32[]{:S(2)}, u32[]{:S(2)}) collective-permute-start(f32[]{:T(128)} %add_reduce_fusion), channel_id=1, source_target_pairs={{0,3},{1,0},{2,1},{3,2},{4,7},{5,4},{6,5},{7,6},{8,11},{9,8},{10,9... | collective-permute-start | bytes 20 | tf_op jit(solution)/shard_map/ppermute | solution.py:64
  19.7 28.4 %all-to-all-start = ((bf16[64,4,2176]{2,1,0:T(4,128)(2,1)}), bf16[64,4,2176]{2,1,0:T(4,128)(2,1)S(1)}, u32[]{:S(2)}, u32[]{:S(2)}) async-start(bf16[64,4,2176]{2,1,0:T(4,128)(2,1)} %pad_maximum_fusion), calls=%async_computation | async-start | bytes 2228224 | tf_op jit(solution)/shard_map/all_to_all | solution.py:78
  53.0 2.2 %copy-start = (f32[128,2048]{1,0:T(8,128)S(1)}, f32[128,2048]{1,0:T(8,128)}, u32[]{:S(2)}) copy-start(f32[128,2048]{1,0:T(8,128)} %reshape.226) | copy-start | bytes 3145732
  54.2 1.2 %copy-start.1 = (f32[128,2048]{1,0:T(8,128)S(1)}, f32[128,2048]{1,0:T(8,128)}, u32[]{:S(2)}) copy-start(f32[128,2048]{1,0:T(8,128)} %reshape.229) | copy-start | bytes 3145732
  55.4 7.2 %slice-start = ((s8[8388608]{0:T(1024)(128)(4,1)}), s8[4194304]{0:T(1024)(128)(4,1)S(1)}, s32[]{:S(2)}) async-start(s8[8388608]{0:T(1024)(128)(4,1)} %bitcast.42), calls=%async_computation.2 | async-start | bytes 8388608
  56.7 5.9 %slice-start.1 = ((s8[8388608]{0:T(1024)(128)(4,1)}), s8[4194304]{0:T(1024)(128)(4,1)S(1)}, s32[]{:S(2)}) async-start(s8[8388608]{0:T(1024)(128)(4,1)} %bitcast.42), calls=%async_computation.3 | async-start | bytes 8388608
  56.7 8.7 %slice-start.2 = ((s8[8388608]{0:T(1024)(128)(4,1)}), s8[4194304]{0:T(1024)(128)(4,1)S(1)}, s32[]{:S(2)}) async-start(s8[8388608]{0:T(1024)(128)(4,1)} %bitcast.47), calls=%async_computation.4 | async-start | bytes 8388608
  62.6 2.4 %copy-start.2 = (f32[2048]{0:T(1024)S(1)}, f32[2048]{0:T(1024)}, u32[]{:S(2)}) copy-start(f32[2048]{0:T(1024)} %param.10) | copy-start | bytes 24580
  62.7 2.8 %slice-start.3 = ((s8[8388608]{0:T(1024)(128)(4,1)}), s8[4194304]{0:T(1024)(128)(4,1)S(1)}, s32[]{:S(2)}) async-start(s8[8388608]{0:T(1024)(128)(4,1)} %bitcast.47), calls=%async_computation.5 | async-start | bytes 8388608
  71.8 6.8 %copy-start.3 = (s32[64]{0:T(128)S(1)}, s32[64]{0:T(128)}, u32[]{:S(2)}) copy-start(s32[64]{0:T(128)} %param.12) | copy-start | bytes 772
  71.8 6.8 %copy-start.4 = (s32[64]{0:T(128)S(1)}, s32[64]{0:T(128)}, u32[]{:S(2)}) copy-start(s32[64]{0:T(128)} %param.11) | copy-start | bytes 772
  73.1 23.1 %all-to-all-start.1 = ((bf16[64,32,256]{2,1,0:T(8,128)(2,1)}), bf16[64,32,256]{2,1,0:T(8,128)(2,1)S(1)}, u32[]{:S(2)}, u32[]{:S(2)}) async-start(bf16[64,32,256]{2,1,0:T(8,128)(2,1)} %bitcast.16), calls=%async_computation.1 | async-start | bytes 2097152 | tf_op jit(solution)/shard_map/all_to_all | solution.py:120

commit v13 on v11

--- a/solution.py
+++ b/solution.py
@@ -109,13 +109,17 @@
         [(spec_re * weights).astype(jnp.bfloat16), (spec_im * weights).astype(jnp.bfloat16)],
         axis=0,
     )
-    bc = jnp.dot(held, cos_t, preferred_element_type=f32)
-    bs = jnp.dot(held, sin_t, preferred_element_type=f32)
-    filt_re = ((bc[:rows] - bs[rows:]) * (1.0 / lines)).astype(jnp.bfloat16)
-    filt_im = ((bs[:rows] + bc[rows:]) * (1.0 / lines)).astype(jnp.bfloat16)
-
-    pair = jnp.concatenate([filt_re, filt_im], axis=0).reshape(2, n_date, cols, lines)
-    pair = pair.transpose(2, 0, 1, 3).reshape(2 * rows, lines).T
+    held = held.reshape(2, n_date, cols, lines).transpose(0, 2, 1, 3).reshape(2 * rows, lines)
+    contract = (((0,), (1,)), ((), ()))
+    bc = lax.dot_general(cos_t, held, contract, preferred_element_type=f32)
+    bs = lax.dot_general(sin_t, held, contract, preferred_element_type=f32)
+    filt_re = ((bc[:, :rows] - bs[:, rows:]) * (1.0 / lines)).astype(jnp.bfloat16)
+    filt_im = ((bs[:, :rows] + bc[:, rows:]) * (1.0 / lines)).astype(jnp.bfloat16)
+    blocks = []
+    for c2 in range(cols):
+        blocks.append(filt_re[:, c2 * n_date:(c2 + 1) * n_date])
+        blocks.append(filt_im[:, c2 * n_date:(c2 + 1) * n_date])
+    pair = jnp.concatenate(blocks, axis=1)
     got = lax.all_to_all(pair, "date", split_axis=0, concat_axis=0, tiled=True)
     z = got.reshape(n_date, lines_dev, cols, 2 * n_date).transpose(1, 2, 0, 3)
     z = z.reshape(lines_dev * cols * n_date, 2 * n_date)

time: 102 us -> 106 us (1.039)
  matrix products: 16.6 us -> 20.3 us
    dot_general x2, matrix products: 4.72 us -> 8.43 us  [the longest x1 6.05 us: shards(): bc = lax.dot_general(cos_t, held, contract, preferred_element_type=f32)]
    concatenate x0 -> x1, local copies, waits for them, and re-layouts: none -> 1.31 us  [shards(): pair = jnp.concatenate(blocks, axis=1)]
    transpose x1 -> x0, local copies, waits for them, and re-layouts: 1.31 us -> none  [shards(): pair = pair.transpose(2, 0, 1, 3).reshape(2 * rows, lines).T]
  transfers between devices with their start and end apart: 5 -> 5, of which waited for: 2 -> 2; matrix products, arithmetic and copies ran while one was open for 14% -> 13% of each run, Pallas kernels for 0% -> 0%
where the time goes in v13:
time: 106 us; the launch traced here: 105 us
  starting transfers between devices  25.5 us (24%)
  waiting for transfers between devices  23.9 us (23%)
  other arithmetic  21.2 us (20%)
  matrix products  20.3 us (19%)
  local copies, waits for them, and re-layouts  10.8 us (10%)
  between operations  3.58 us (3%)
    all_to_all x1, waiting for transfers between devices, shards(): got = lax.all_to_all(pair, 'date', split_axis=0, concat_axis=0, tiled=True)  17 us
    ppermute x3, starting transfers between devices, shards(): lax.ppermute(local, 'rng', [(r, (r + k) % n_rng) for r in range(n_rng)])  11.3 us
    all_to_all x1, starting transfers between devices, shards(): got = lax.all_to_all(both, 'date', split_axis=0, concat_axis=0, tiled=True)  9.45 us
    convert_element_type x1, other arithmetic, dft_table(): (hi_c * lo_s + hi_s * lo_c).reshape(length, length).astype(jnp.bfloat16)  8.27 us
    all_to_all x1, waiting for transfers between devices, shards(): got = lax.all_to_all(both, 'date', split_axis=0, concat_axis=0, tiled=True)  6.91 us
    dot_general x1, matrix products, shards(): bc = lax.dot_general(cos_t, held, contract, preferred_element_type=f32)  6.05 us
    dot_general x1, matrix products, shards(): fc = jnp.dot(stacked, cos_t, preferred_element_type=f32)  5.89 us
    all_to_all x1, starting transfers between devices, shards(): got = lax.all_to_all(pair, 'date', split_axis=0, concat_axis=0, tiled=True)  4.71 us
  transfers between devices with their start and end apart: 5, of which 2 were waited for; matrix products, arithmetic and copies ran while one was open for 13% of the time, Pallas kernels for 0%

profile of v13, /device:TPU:1, one launch (start us, length us, event | category | flops | bytes accessed | tf_op | source)
XLA Modules:
  0.0 105.2 jit_solution(7999228816957057217)
XLA Ops:
  0.0 1.2 %copy.27 = bf16[1,2048,128]{1,2,0:T(8,128)(2,1)S(1)} copy(bf16[1,2048,128]{2,1,0:T(8,128)(2,1)} %param.7) | data formatting | bytes 1048576 | tf_op args[0]
  1.3 1.2 %copy.28 = bf16[1,2048,128]{1,2,0:T(8,128)(2,1)S(1)} copy(bf16[1,2048,128]{2,1,0:T(8,128)(2,1)} %param.8) | data formatting | bytes 1048576 | tf_op args[1]
  2.5 0.9 add_reduce_fusion
  3.4 3.8 %collective-permute-start = (f32[]{:T(128)}, f32[]{:T(128)}, u32[]{:S(2)}, u32[]{:S(2)}) collective-permute-start(f32[]{:T(128)} %add_reduce_fusion), channel_id=1, source_target_pairs={{0,1},{1,2},{2,3},{3,0},{4,5},{5,6},{6,7},{7,4},{8,9},{9,10},{10,1... | collective-permute-start | bytes 20 | tf_op jit(solution)/shard_map/ppermute | solution.py:64
  7.2 5.1 %collective-permute-start.1 = (f32[]{:T(128)}, f32[]{:T(128)}, u32[]{:S(2)}, u32[]{:S(2)}) collective-permute-start(f32[]{:T(128)} %add_reduce_fusion), channel_id=1, source_target_pairs={{0,2},{1,3},{2,0},{3,1},{4,6},{5,7},{6,4},{7,5},{8,10},{9,11},{10,... | collective-permute-start | bytes 20 | tf_op jit(solution)/shard_map/ppermute | solution.py:64
  12.3 2.4 %collective-permute-start.2 = (f32[]{:T(128)}, f32[]{:T(128)}, u32[]{:S(2)}, u32[]{:S(2)}) collective-permute-start(f32[]{:T(128)} %add_reduce_fusion), channel_id=1, source_target_pairs={{0,3},{1,0},{2,1},{3,2},{4,7},{5,4},{6,5},{7,6},{8,11},{9,8},{10,9... | collective-permute-start | bytes 20 | tf_op jit(solution)/shard_map/ppermute | solution.py:64
  14.8 0.8 copy.29
  18.2 1.6 %pad_maximum_fusion = bf16[64,4,2176]{2,1,0:T(4,128)(2,1)} fusion(bf16[64,4,2048]{2,1,0:T(4,128)(2,1)S(1)} %copy.29, bf16[2176]{0:T(1024)(128)(2,1)S(1)} %pad.13.clone), kind=kLoop, calls=%fused_computation.10 | loop fusion | flops 2228224 | bytes 2167040 | tf_op jit(solution)/shard_map/concatenate | solution.py:77
  19.7 9.5 %all-to-all-start = ((bf16[64,4,2176]{2,1,0:T(4,128)(2,1)}), bf16[64,4,2176]{2,1,0:T(4,128)(2,1)S(1)}, u32[]{:S(2)}, u32[]{:S(2)}) async-start(bf16[64,4,2176]{2,1,0:T(4,128)(2,1)} %pad_maximum_fusion), calls=%async_computation | async-start | bytes 2228224 | tf_op jit(solution)/shard_map/all_to_all | solution.py:78
  29.9 2.0 %fusion.22 = (f32[2048,64]{0,1:T(8,128)S(1)}, f32[2048,64]{0,1:T(8,128)S(1)}) fusion(), kind=kLoop, calls=%fused_computation.51 | loop fusion | flops 1835008 | bytes 1048576 | tf_op jit(solution)/shard_map/sin | solution.py:25
  31.9 1.1 %fusion.36 = (f32[2048,32]{0,1:T(8,128)S(1)}, f32[2048,32]{0,1:T(8,128)S(1)}) fusion(s32[32]{0:T(128)S(1)} %iota_multiply_fusion), kind=kLoop, calls=%fused_computation.65 | loop fusion | flops 917504 | bytes 524416 | tf_op jit(solution)/shard_map/cos | solution.py:24
  33.0 8.3 %add_convert_fusion = (bf16[2048,32,64]{0,2,1:T(8,128)(2,1)}, bf16[2048,32,64]{0,2,1:T(8,128)(2,1)}) fusion(f32[2048,64]{0,1:T(8,128)S(1)} %get-tuple-element.29, f32[2048,32]{0,1:T(8,128)S(1)} %get-tuple-element.28, f32[2048,64]{0,1:T(8,128)S(1)} %get-tuple-element.30, f32[2048,32]{0,1:T(8,128)S(1)} %get-tuple-element.27), kind=kLoop, calls=%fused_computation | loop fusion | flops 33554432 | bytes 18350080 | tf_op jit(solution)/shard_map/convert_element_type | solution.py:27
  41.3 6.9 %all-to-all-done = bf16[64,4,2176]{2,1,0:T(4,128)(2,1)S(1)} async-done(((bf16[64,4,2176]{2,1,0:T(4,128)(2,1)}), bf16[64,4,2176]{2,1,0:T(4,128)(2,1)S(1)}, u32[]{:S(2)}, u32[]{:S(2)}) %all-to-all-start) | async-done | bytes 1114144 | tf_op jit(solution)/shard_map/all_to_all | solution.py:78
  48.4 0.6 slice.84
  49.0 0.7 reshape.211
  49.7 0.7 slice_bitcast_fusion.1
  51.1 0.5 constant_dynamic-slice_fusion
  51.6 1.0 convolution_multiply_fusion.1
  52.6 1.4 %add_convert_fusion.1 = (bf16[128,2048]{1,0:T(8,128)(2,1)S(1)}, bf16[128,2048]{1,0:T(8,128)(2,1)S(1)}) fusion(bf16[128,2048]{1,0:T(8,128)(2,1)S(1)} %reshape_squeeze.7, f32[128,2048]{1,0:T(8,128)S(1)} %convolution_multiply_fusion.1, bf16[128,2048]{1,0:T(8,128)(2,1)S(1)} %reshape_squeeze.6, f32[128]{0:T(128)S(1)} %mul.307, f32[]{:T(128)} %bitcast.12, ...), kind=kOutput, calls=%fused_computation.28 | convolution fusion | flops 70533120 | bytes 3146756 | tf_op jit(solution)/shard_map/dot_general | solution.py:93
  54.0 5.9 %fusion.12 = f32[256,2048]{1,0:T(8,128)S(1)} fusion(bf16[2048,2048]{0,1:T(8,128)(2,1)} %bitcast.58, bf16[128,2048]{1,0:T(8,128)(2,1)S(1)} %get-tuple-element.16, bf16[128,2048]{1,0:T(8,128)(2,1)S(1)} %get-tuple-element.15), kind=kOutput, calls=%fused_computation.36 | convolution fusion | flops 2149580800 | bytes 11534336 | tf_op jit(solution)/shard_map/dot_general | solution.py:103
  60.0 2.4 %fusion.11 = f32[256,2048]{1,0:T(8,128)S(1)} fusion(bf16[2048,2048]{0,1:T(8,128)(2,1)S(1)} %bitcast.54, bf16[128,2048]{1,0:T(8,128)(2,1)S(1)} %get-tuple-element.16, bf16[128,2048]{1,0:T(8,128)(2,1)S(1)} %get-tuple-element.15), kind=kOutput, calls=%fused_computation.35 | convolution fusion | flops 2149580800 | bytes 11534336 | tf_op jit(solution)/shard_map/dot_general | solution.py:104
  62.8 0.9 reshape.212
  64.1 6.0 %fusion.58 = f32[2048,256]{0,1:T(8,128)S(1)} fusion(bf16[2048,2048]{0,1:T(8,128)(2,1)} %bitcast.59, bf16[256,2048]{1,0:T(8,128)(2,1)S(1)} %bitcast.64), kind=kOutput, calls=%fused_computation.110 | convolution fusion | flops 2147483648 | bytes 11534336 | tf_op jit(solution)/shard_map/dot_general | solution.py:114
  70.2 2.4 %fusion.59 = f32[2048,256]{0,1:T(8,128)S(1)} fusion(bf16[2048,2048]{0,1:T(8,128)(2,1)S(1)} %bitcast.57, bf16[256,2048]{1,0:T(8,128)(2,1)S(1)} %bitcast.65), kind=kOutput, calls=%fused_computation.111 | convolution fusion | flops 2147483648 | bytes 11534336 | tf_op jit(solution)/shard_map/dot_general | solution.py:115
  73.2 1.3 %copy.33 = bf16[2048,256]{1,0:T(8,128)(2,1)} copy(bf16[2048,256]{0,1:T(8,128)(2,1)S(1)} %pad_maximum_fusion.4) | data formatting | bytes 2097152 | tf_op jit(solution)/shard_map/concatenate | solution.py:122
  74.6 4.7 %all-to-all-start.1 = ((bf16[64,32,256]{2,1,0:T(8,128)(2,1)}), bf16[64,32,256]{2,1,0:T(8,128)(2,1)S(1)}, u32[]{:S(2)}, u32[]{:S(2)}) async-start(bf16[64,32,256]{2,1,0:T(8,128)(2,1)} %bitcast.16), calls=%async_computation.1 | async-start | bytes 2097152 | tf_op jit(solution)/shard_map/all_to_all | solution.py:123
  79.3 0.7 convert_bitcast_fusion
  80.7 17.0 %all-to-all-done.1 = bf16[64,32,256]{2,1,0:T(8,128)(2,1)S(1)} async-done(((bf16[64,32,256]{2,1,0:T(8,128)(2,1)}), bf16[64,32,256]{2,1,0:T(8,128)(2,1)S(1)}, u32[]{:S(2)}, u32[]{:S(2)}) %all-to-all-start.1) | async-done | bytes 1048608 | tf_op jit(solution)/shard_map/all_to_all | solution.py:123
  98.0 1.2 %copy.34 = bf16[64,32,2,128]{3,0,2,1:T(8,128)(2,1)S(1)} copy(bf16[64,32,2,128]{3,2,1,0:T(2,128)(2,1)S(1)} %reshape.214) | data formatting | bytes 2097152 | tf_op jit(solution)/shard_map/reshape | solution.py:124
  99.2 0.9 multiply_reduce_fusion
  100.2 1.2 %fusion.27 = f32[4096,512]{1,0:T(8,128)S(1)} fusion(bf16[4096,128]{1,0:T(8,128)(2,1)S(1)} %bitcast.60, bf16[64,256]{1,0:T(8,128)(2,1)S(1)} %get-tuple-element.26, bf16[64,256]{1,0:T(8,128)(2,1)S(1)} %get-tuple-element.25, bf16[64,256]{1,0:T(8,128)(2,1)S(1)} %fusion.53), kind=kOutput, calls=%fused_computation.56 | convolution fusion | flops 537395200 | bytes 9535488 | tf_op jit(solution)/shard_map/dot_general | solution.py:129
  101.5 3.7 %fusion.2 = f32[4096,256]{1,0:T(8,128)} fusion(f32[4096,512]{1,0:T(8,128)S(1)} %fusion.27, f32[4096]{0:T(1024)S(1)} %convert_bitcast_fusion, f32[4096]{0:T(1024)S(1)} %mul.336), kind=kLoop, calls=%fused_computation.5 | loop fusion | flops 5242880 | bytes 12615680 | tf_op jit(solution)/shard_map/mul | solution.py:139
  (43 shorter events, 3.4 us)
Async XLA Ops:
  3.4 12.2 %collective-permute-start = (f32[]{:T(128)}, f32[]{:T(128)}, u32[]{:S(2)}, u32[]{:S(2)}) collective-permute-start(f32[]{:T(128)} %add_reduce_fusion), channel_id=1, source_target_pairs={{0,1},{1,2},{2,3},{3,0},{4,5},{5,6},{6,7},{7,4},{8,9},{9,10},{10,1... | collective-permute-start | bytes 20 | tf_op jit(solution)/shard_map/ppermute | solution.py:64
  7.2 9.7 %collective-permute-start.1 = (f32[]{:T(128)}, f32[]{:T(128)}, u32[]{:S(2)}, u32[]{:S(2)}) collective-permute-start(f32[]{:T(128)} %add_reduce_fusion), channel_id=1, source_target_pairs={{0,2},{1,3},{2,0},{3,1},{4,6},{5,7},{6,4},{7,5},{8,10},{9,11},{10,... | collective-permute-start | bytes 20 | tf_op jit(solution)/shard_map/ppermute | solution.py:64
  12.3 5.2 %collective-permute-start.2 = (f32[]{:T(128)}, f32[]{:T(128)}, u32[]{:S(2)}, u32[]{:S(2)}) collective-permute-start(f32[]{:T(128)} %add_reduce_fusion), channel_id=1, source_target_pairs={{0,3},{1,0},{2,1},{3,2},{4,7},{5,4},{6,5},{7,6},{8,11},{9,8},{10,9... | collective-permute-start | bytes 20 | tf_op jit(solution)/shard_map/ppermute | solution.py:64
  19.7 28.4 %all-to-all-start = ((bf16[64,4,2176]{2,1,0:T(4,128)(2,1)}), bf16[64,4,2176]{2,1,0:T(4,128)(2,1)S(1)}, u32[]{:S(2)}, u32[]{:S(2)}) async-start(bf16[64,4,2176]{2,1,0:T(4,128)(2,1)} %pad_maximum_fusion), calls=%async_computation | async-start | bytes 2228224 | tf_op jit(solution)/shard_map/all_to_all | solution.py:78
  52.6 7.3 %slice-start = ((s8[8388608]{0:T(1024)(128)(4,1)}), s8[4194304]{0:T(1024)(128)(4,1)S(1)}, s32[]{:S(2)}) async-start(s8[8388608]{0:T(1024)(128)(4,1)} %bitcast.52), calls=%async_computation.2 | async-start | bytes 8388608
  54.0 5.9 %slice-start.1 = ((s8[8388608]{0:T(1024)(128)(4,1)}), s8[4194304]{0:T(1024)(128)(4,1)S(1)}, s32[]{:S(2)}) async-start(s8[8388608]{0:T(1024)(128)(4,1)} %bitcast.52), calls=%async_computation.3 | async-start | bytes 8388608
  59.9 2.4 %copy-start = (f32[2048]{0:T(1024)S(1)}, f32[2048]{0:T(1024)}, u32[]{:S(2)}) copy-start(f32[2048]{0:T(1024)} %param.10) | copy-start | bytes 24580
  63.7 6.4 %slice-start.2 = ((s8[8388608]{0:T(1024)(128)(4,1)}), s8[4194304]{0:T(1024)(128)(4,1)S(1)}, s32[]{:S(2)}) async-start(s8[8388608]{0:T(1024)(128)(4,1)} %bitcast.55), calls=%async_computation.4 | async-start | bytes 8388608
  64.1 6.1 %slice-start.3 = ((s8[8388608]{0:T(1024)(128)(4,1)}), s8[4194304]{0:T(1024)(128)(4,1)S(1)}, s32[]{:S(2)}) async-start(s8[8388608]{0:T(1024)(128)(4,1)} %bitcast.55), calls=%async_computation.5 | async-start | bytes 8388608
  73.0 7.0 %copy-start.1 = (s32[64]{0:T(128)S(1)}, s32[64]{0:T(128)}, u32[]{:S(2)}) copy-start(s32[64]{0:T(128)} %param.12) | copy-start | bytes 772
  73.0 7.0 %copy-start.2 = (s32[64]{0:T(128)S(1)}, s32[64]{0:T(128)}, u32[]{:S(2)}) copy-start(s32[64]{0:T(128)} %param.11) | copy-start | bytes 772
  74.6 23.1 %all-to-all-start.1 = ((bf16[64,32,256]{2,1,0:T(8,128)(2,1)}), bf16[64,32,256]{2,1,0:T(8,128)(2,1)S(1)}, u32[]{:S(2)}, u32[]{:S(2)}) async-start(bf16[64,32,256]{2,1,0:T(8,128)(2,1)} %bitcast.16), calls=%async_computation.1 | async-start | bytes 2097152 | tf_op jit(solution)/shard_map/all_to_all | solution.py:123

commit v14 on v11

--- a/solution.py
+++ b/solution.py
@@ -100,8 +100,9 @@
     cos_t, sin_t = dft_table(lines)
     rows = n_date * cols
     stacked = jnp.concatenate([ifg_re, ifg_im], axis=0)
-    fc = jnp.dot(stacked, cos_t, preferred_element_type=f32)
     fs = jnp.dot(stacked, sin_t, preferred_element_type=f32)
+    stacked_after, fs = lax.optimization_barrier((stacked, fs))
+    fc = jnp.dot(stacked_after, cos_t, preferred_element_type=f32)
     spec_re = fc[:rows] + fs[rows:]
     spec_im = fc[rows:] - fs[:rows]
     weights = gain[None, :]

time: 102 us -> 102 us (level)
    dot_general x1, matrix products: 5.89 us -> 2.36 us  [shards(): fc = jnp.dot(stacked_after, cos_t, preferred_element_type=f32)]
    dot_general x1, matrix products: 2.36 us -> 5.89 us  [shards(): fs = jnp.dot(stacked, sin_t, preferred_element_type=f32)]
  transfers between devices with their start and end apart: 5 -> 5, of which waited for: 2 -> 2; matrix products, arithmetic and copies ran while one was open for 14% -> 13% of each run, Pallas kernels for 0% -> 0%
where the time goes in v14:
time: 102 us
  starting transfers between devices  25.5 us (25%)
  waiting for transfers between devices  23.9 us (23%)
  other arithmetic  21.2 us (21%)
  matrix products  16.4 us (16%)
  local copies, waits for them, and re-layouts  11.5 us (11%)
  between operations  3.55 us (3%)
    all_to_all x1, waiting for transfers between devices, shards(): got = lax.all_to_all(pair, 'date', split_axis=0, concat_axis=0, tiled=True)  17 us
    ppermute x3, starting transfers between devices, shards(): lax.ppermute(local, 'rng', [(r, (r + k) % n_rng) for r in range(n_rng)])  11.3 us
    all_to_all x1, starting transfers between devices, shards(): got = lax.all_to_all(both, 'date', split_axis=0, concat_axis=0, tiled=True)  9.45 us
    convert_element_type x1, other arithmetic, dft_table(): (hi_c * lo_s + hi_s * lo_c).reshape(length, length).astype(jnp.bfloat16)  8.27 us
    all_to_all x1, waiting for transfers between devices, shards(): got = lax.all_to_all(both, 'date', split_axis=0, concat_axis=0, tiled=True)  6.9 us
    dot_general x1, matrix products, shards(): fs = jnp.dot(stacked, sin_t, preferred_element_type=f32)  5.89 us
    all_to_all x1, starting transfers between devices, shards(): got = lax.all_to_all(pair, 'date', split_axis=0, concat_axis=0, tiled=True)  4.71 us
    unnamed x17, local copies, waits for them, and re-layouts  4.03 us
  transfers between devices with their start and end apart: 5, of which 2 were waited for; matrix products, arithmetic and copies ran while one was open for 13% of the time, Pallas kernels for 0%

profile of v14, /device:TPU:1, one launch (start us, length us, event | category | flops | bytes accessed | tf_op | source)
XLA Modules:
  0.0 102.0 jit_solution(1418300475133530319)
XLA Ops:
  0.0 1.2 %copy.27 = bf16[1,2048,128]{1,2,0:T(8,128)(2,1)S(1)} copy(bf16[1,2048,128]{2,1,0:T(8,128)(2,1)} %param.7) | data formatting | bytes 1048576 | tf_op args[0]
  1.3 1.2 %copy.28 = bf16[1,2048,128]{1,2,0:T(8,128)(2,1)S(1)} copy(bf16[1,2048,128]{2,1,0:T(8,128)(2,1)} %param.8) | data formatting | bytes 1048576 | tf_op args[1]
  2.5 0.9 add_reduce_fusion
  3.4 3.8 %collective-permute-start = (f32[]{:T(128)}, f32[]{:T(128)}, u32[]{:S(2)}, u32[]{:S(2)}) collective-permute-start(f32[]{:T(128)} %add_reduce_fusion), channel_id=1, source_target_pairs={{0,1},{1,2},{2,3},{3,0},{4,5},{5,6},{6,7},{7,4},{8,9},{9,10},{10,1... | collective-permute-start | bytes 20 | tf_op jit(solution)/shard_map/ppermute | solution.py:64
  7.2 5.1 %collective-permute-start.1 = (f32[]{:T(128)}, f32[]{:T(128)}, u32[]{:S(2)}, u32[]{:S(2)}) collective-permute-start(f32[]{:T(128)} %add_reduce_fusion), channel_id=1, source_target_pairs={{0,2},{1,3},{2,0},{3,1},{4,6},{5,7},{6,4},{7,5},{8,10},{9,11},{10,... | collective-permute-start | bytes 20 | tf_op jit(solution)/shard_map/ppermute | solution.py:64
  12.3 2.4 %collective-permute-start.2 = (f32[]{:T(128)}, f32[]{:T(128)}, u32[]{:S(2)}, u32[]{:S(2)}) collective-permute-start(f32[]{:T(128)} %add_reduce_fusion), channel_id=1, source_target_pairs={{0,3},{1,0},{2,1},{3,2},{4,7},{5,4},{6,5},{7,6},{8,11},{9,8},{10,9... | collective-permute-start | bytes 20 | tf_op jit(solution)/shard_map/ppermute | solution.py:64
  14.8 0.8 copy.29
  18.2 1.6 %pad_maximum_fusion = bf16[64,4,2176]{2,1,0:T(4,128)(2,1)} fusion(bf16[64,4,2048]{2,1,0:T(4,128)(2,1)S(1)} %copy.29, bf16[2176]{0:T(1024)(128)(2,1)S(1)} %pad.11.clone), kind=kLoop, calls=%fused_computation.10 | loop fusion | flops 2228224 | bytes 2167040 | tf_op jit(solution)/shard_map/concatenate | solution.py:77
  19.7 9.5 %all-to-all-start = ((bf16[64,4,2176]{2,1,0:T(4,128)(2,1)}), bf16[64,4,2176]{2,1,0:T(4,128)(2,1)S(1)}, u32[]{:S(2)}, u32[]{:S(2)}) async-start(bf16[64,4,2176]{2,1,0:T(4,128)(2,1)} %pad_maximum_fusion), calls=%async_computation | async-start | bytes 2228224 | tf_op jit(solution)/shard_map/all_to_all | solution.py:78
  29.9 2.0 %fusion.22 = (f32[2048,64]{0,1:T(8,128)S(1)}, f32[2048,64]{0,1:T(8,128)S(1)}) fusion(), kind=kLoop, calls=%fused_computation.51 | loop fusion | flops 1835008 | bytes 1048576 | tf_op jit(solution)/shard_map/sin | solution.py:25
  31.9 1.1 %fusion.36 = (f32[2048,32]{0,1:T(8,128)S(1)}, f32[2048,32]{0,1:T(8,128)S(1)}) fusion(s32[32]{0:T(128)S(1)} %iota_multiply_fusion), kind=kLoop, calls=%fused_computation.65 | loop fusion | flops 917504 | bytes 524416 | tf_op jit(solution)/shard_map/cos | solution.py:24
  33.0 8.3 %add_convert_fusion = (bf16[2048,32,64]{0,2,1:T(8,128)(2,1)}, bf16[2048,32,64]{0,2,1:T(8,128)(2,1)}) fusion(f32[2048,64]{0,1:T(8,128)S(1)} %get-tuple-element.29, f32[2048,32]{0,1:T(8,128)S(1)} %get-tuple-element.28, f32[2048,64]{0,1:T(8,128)S(1)} %get-tuple-element.30, f32[2048,32]{0,1:T(8,128)S(1)} %get-tuple-element.27), kind=kLoop, calls=%fused_computation | loop fusion | flops 33554432 | bytes 18350080 | tf_op jit(solution)/shard_map/convert_element_type | solution.py:27
  41.3 6.9 %all-to-all-done = bf16[64,4,2176]{2,1,0:T(4,128)(2,1)S(1)} async-done(((bf16[64,4,2176]{2,1,0:T(4,128)(2,1)}), bf16[64,4,2176]{2,1,0:T(4,128)(2,1)S(1)}, u32[]{:S(2)}, u32[]{:S(2)}) %all-to-all-start) | async-done | bytes 1114144 | tf_op jit(solution)/shard_map/all_to_all | solution.py:78
  48.4 0.6 slice.68
  49.0 0.7 reshape.211
  49.7 0.7 slice_bitcast_fusion.1
  51.6 1.0 convolution_multiply_fusion.1
  52.6 1.2 %add_convert_fusion.1 = (bf16[128,2048]{1,0:T(8,128)(2,1)S(1)}, bf16[128,2048]{1,0:T(8,128)(2,1)S(1)}) fusion(bf16[128,2048]{1,0:T(8,128)(2,1)S(1)} %reshape_squeeze.7, f32[128,2048]{1,0:T(8,128)S(1)} %convolution_multiply_fusion.1, bf16[128,2048]{1,0:T(8,128)(2,1)S(1)} %reshape_squeeze.6, f32[128]{0:T(128)S(1)} %mul.287, f32[]{:T(128)} %bitcast.10, ...), kind=kOutput, calls=%fused_computation.28 | convolution fusion | flops 70533120 | bytes 3146756 | tf_op jit(solution)/shard_map/dot_general | solution.py:93
  54.0 5.9 %fusion.54 = f32[256,2048]{1,0:T(8,128)S(1)} fusion(bf16[2048,2048]{0,1:T(8,128)(2,1)} %bitcast.53, bf16[128,2048]{1,0:T(8,128)(2,1)S(1)} %get-tuple-element.20, bf16[128,2048]{1,0:T(8,128)(2,1)S(1)} %get-tuple-element.19), kind=kOutput, calls=%fused_computation.107 | convolution fusion | flops 2149580800 | bytes 11534336 | tf_op jit(solution)/shard_map/dot_general | solution.py:103
  59.9 2.4 %fusion.57 = f32[256,2048]{1,0:T(8,128)S(1)} fusion(bf16[256,2048]{1,0:T(8,128)(2,1)S(1)} %pad_maximum_fusion.2, bf16[2048,2048]{0,1:T(8,128)(2,1)S(1)} %bitcast.59), kind=kOutput, calls=%fused_computation.109 | convolution fusion | flops 2147483648 | bytes 11534336 | tf_op jit(solution)/shard_map/dot_general | solution.py:105
  62.7 2.4 %fusion.12 = f32[256,2048]{1,0:T(8,128)S(1)} fusion(bf16[2048,2048]{0,1:T(8,128)(2,1)S(1)} %bitcast.60, bf16[128,2048]{1,0:T(8,128)(2,1)S(1)} %get-tuple-element.16, bf16[128,2048]{1,0:T(8,128)(2,1)S(1)} %get-tuple-element.15), kind=kOutput, calls=%fused_computation.36 | convolution fusion | flops 2149580800 | bytes 11534336 | tf_op jit(solution)/shard_map/dot_general | solution.py:113
  65.1 0.8 slice-done.1
  65.9 2.4 %fusion.11 = f32[256,2048]{1,0:T(8,128)S(1)} fusion(bf16[2048,2048]{0,1:T(8,128)(2,1)S(1)} %bitcast.56, bf16[128,2048]{1,0:T(8,128)(2,1)S(1)} %get-tuple-element.16, bf16[128,2048]{1,0:T(8,128)(2,1)S(1)} %get-tuple-element.15), kind=kOutput, calls=%fused_computation.35 | convolution fusion | flops 2149580800 | bytes 11534336 | tf_op jit(solution)/shard_map/dot_general | solution.py:114
  68.7 0.9 reshape.212
  70.0 1.3 %copy.33 = bf16[2048,256]{1,0:T(8,128)(2,1)} copy(bf16[2048,256]{0,1:T(8,128)(2,1)S(1)} %bitcast.65) | data formatting | bytes 2097152 | tf_op jit(solution)/shard_map/transpose | solution.py:119
  71.4 4.7 %all-to-all-start.1 = ((bf16[64,32,256]{2,1,0:T(8,128)(2,1)}), bf16[64,32,256]{2,1,0:T(8,128)(2,1)S(1)}, u32[]{:S(2)}, u32[]{:S(2)}) async-start(bf16[64,32,256]{2,1,0:T(8,128)(2,1)} %bitcast.16), calls=%async_computation.1 | async-start | bytes 2097152 | tf_op jit(solution)/shard_map/all_to_all | solution.py:120
  76.1 0.7 convert_bitcast_fusion
  77.5 17.0 %all-to-all-done.1 = bf16[64,32,256]{2,1,0:T(8,128)(2,1)S(1)} async-done(((bf16[64,32,256]{2,1,0:T(8,128)(2,1)}), bf16[64,32,256]{2,1,0:T(8,128)(2,1)S(1)}, u32[]{:S(2)}, u32[]{:S(2)}) %all-to-all-start.1) | async-done | bytes 1048608 | tf_op jit(solution)/shard_map/all_to_all | solution.py:120
  94.8 1.2 %copy.34 = bf16[64,32,2,128]{3,0,2,1:T(8,128)(2,1)S(1)} copy(bf16[64,32,2,128]{3,2,1,0:T(2,128)(2,1)S(1)} %reshape.214) | data formatting | bytes 2097152 | tf_op jit(solution)/shard_map/reshape | solution.py:121
  96.0 0.9 multiply_reduce_fusion
  97.0 1.2 %fusion.27 = f32[4096,512]{1,0:T(8,128)S(1)} fusion(bf16[4096,128]{1,0:T(8,128)(2,1)S(1)} %bitcast.61, bf16[64,256]{1,0:T(8,128)(2,1)S(1)} %get-tuple-element.26, bf16[64,256]{1,0:T(8,128)(2,1)S(1)} %get-tuple-element.25, bf16[64,256]{1,0:T(8,128)(2,1)S(1)} %fusion.53), kind=kOutput, calls=%fused_computation.56 | convolution fusion | flops 537395200 | bytes 9535488 | tf_op jit(solution)/shard_map/dot_general | solution.py:126
  98.3 3.7 %fusion.2 = f32[4096,256]{1,0:T(8,128)} fusion(f32[4096,512]{1,0:T(8,128)S(1)} %fusion.27, f32[4096]{0:T(1024)S(1)} %convert_bitcast_fusion, f32[4096]{0:T(1024)S(1)} %mul.336), kind=kLoop, calls=%fused_computation.5 | loop fusion | flops 5242880 | bytes 12615680 | tf_op jit(solution)/shard_map/mul | solution.py:136
  (41 shorter events, 3.9 us)
Async XLA Ops:
  3.4 12.2 %collective-permute-start = (f32[]{:T(128)}, f32[]{:T(128)}, u32[]{:S(2)}, u32[]{:S(2)}) collective-permute-start(f32[]{:T(128)} %add_reduce_fusion), channel_id=1, source_target_pairs={{0,1},{1,2},{2,3},{3,0},{4,5},{5,6},{6,7},{7,4},{8,9},{9,10},{10,1... | collective-permute-start | bytes 20 | tf_op jit(solution)/shard_map/ppermute | solution.py:64
  7.2 9.8 %collective-permute-start.1 = (f32[]{:T(128)}, f32[]{:T(128)}, u32[]{:S(2)}, u32[]{:S(2)}) collective-permute-start(f32[]{:T(128)} %add_reduce_fusion), channel_id=1, source_target_pairs={{0,2},{1,3},{2,0},{3,1},{4,6},{5,7},{6,4},{7,5},{8,10},{9,11},{10,... | collective-permute-start | bytes 20 | tf_op jit(solution)/shard_map/ppermute | solution.py:64
  12.3 5.2 %collective-permute-start.2 = (f32[]{:T(128)}, f32[]{:T(128)}, u32[]{:S(2)}, u32[]{:S(2)}) collective-permute-start(f32[]{:T(128)} %add_reduce_fusion), channel_id=1, source_target_pairs={{0,3},{1,0},{2,1},{3,2},{4,7},{5,4},{6,5},{7,6},{8,11},{9,8},{10,9... | collective-permute-start | bytes 20 | tf_op jit(solution)/shard_map/ppermute | solution.py:64
  19.7 28.4 %all-to-all-start = ((bf16[64,4,2176]{2,1,0:T(4,128)(2,1)}), bf16[64,4,2176]{2,1,0:T(4,128)(2,1)S(1)}, u32[]{:S(2)}, u32[]{:S(2)}) async-start(bf16[64,4,2176]{2,1,0:T(4,128)(2,1)} %pad_maximum_fusion), calls=%async_computation | async-start | bytes 2228224 | tf_op jit(solution)/shard_map/all_to_all | solution.py:78
  53.8 6.0 %slice-start.2 = ((s8[8388608]{0:T(1024)(128)(4,1)}), s8[4194304]{0:T(1024)(128)(4,1)S(1)}, s32[]{:S(2)}) async-start(s8[8388608]{0:T(1024)(128)(4,1)} %bitcast.57), calls=%async_computation.4 | async-start | bytes 8388608
  54.0 5.9 %slice-start.3 = ((s8[8388608]{0:T(1024)(128)(4,1)}), s8[4194304]{0:T(1024)(128)(4,1)S(1)}, s32[]{:S(2)}) async-start(s8[8388608]{0:T(1024)(128)(4,1)} %bitcast.57), calls=%async_computation.5 | async-start | bytes 8388608
  59.9 2.4 %copy-start = (f32[2048]{0:T(1024)S(1)}, f32[2048]{0:T(1024)}, u32[]{:S(2)}) copy-start(f32[2048]{0:T(1024)} %param.10) | copy-start | bytes 24580
  62.3 2.8 %slice-start = ((s8[8388608]{0:T(1024)(128)(4,1)}), s8[4194304]{0:T(1024)(128)(4,1)S(1)}, s32[]{:S(2)}) async-start(s8[8388608]{0:T(1024)(128)(4,1)} %bitcast.54), calls=%async_computation.2 | async-start | bytes 8388608
  62.7 3.2 %slice-start.1 = ((s8[8388608]{0:T(1024)(128)(4,1)}), s8[4194304]{0:T(1024)(128)(4,1)S(1)}, s32[]{:S(2)}) async-start(s8[8388608]{0:T(1024)(128)(4,1)} %bitcast.54), calls=%async_computation.3 | async-start | bytes 8388608
  68.7 8.1 %copy-start.1 = (s32[64]{0:T(128)S(1)}, s32[64]{0:T(128)}, u32[]{:S(2)}) copy-start(s32[64]{0:T(128)} %param.12) | copy-start | bytes 772
  68.7 8.1 %copy-start.2 = (s32[64]{0:T(128)S(1)}, s32[64]{0:T(128)}, u32[]{:S(2)}) copy-start(s32[64]{0:T(128)} %param.11) | copy-start | bytes 772
  71.4 23.1 %all-to-all-start.1 = ((bf16[64,32,256]{2,1,0:T(8,128)(2,1)}), bf16[64,32,256]{2,1,0:T(8,128)(2,1)S(1)}, u32[]{:S(2)}, u32[]{:S(2)}) async-start(bf16[64,32,256]{2,1,0:T(8,128)(2,1)} %bitcast.16), calls=%async_computation.1 | async-start | bytes 2097152 | tf_op jit(solution)/shard_map/all_to_all | solution.py:120
